TPU v7x, 32 devices: a whole 2x2x4 slice. The times are simulated.
32 devices in a mesh: shard: 2 (over core), tensor: 4 (over y, x), section: 4 (over z).
Axes of the slice: x: 2, y: 2, z: 4, core: 2. Of those that a mesh axis runs over, the one named last changes fastest.
Arguments:
- grad_parts: bfloat16 [2, 2304, 2304], P('shard', ('tensor', 'section')), may hold values from -1.5 to 1.5
- moment: float32 [2304, 2304], P('shard', ('tensor', 'section')), may hold values from -6 to 6
- second: float32 [2304, 2304], P('shard', ('tensor', 'section')), may hold values from 0.05 to 2
- stat_left: float32 [2304, 2304], P('shard', ('tensor', 'section')), may hold values from -0.1 to 12
- basis_left: float32 [2304, 2304], P('shard', ('tensor', 'section')), may hold values from -0.2 to 1.5
Outputs:
- update: float32 [2304, 2304], P('shard', ('tensor', 'section'))
- moment_next: float32 [2304, 2304], P('shard', ('tensor', 'section'))
- second_next: float32 [2304, 2304], P('shard', ('tensor', 'section'))
- stat_next: float32 [2304, 2304], P('shard', ('tensor', 'section'))
- basis_next: float32 [2304, 2304], P('shard', ('tensor', 'section'))
All inputs are finite; a program needn't handle non-finite values.
Results may differ from a plain program's by a relative error of at most 0.00074.
Values may be sent and summed in bfloat16 or wider, within the bound.
No kernel may reach another device: no remote copies, remote signals or barrier semaphores. Data moves between devices by JAX's collectives and lax.ppermute only.
A program may use at most 128 MiB of HBM per device.

v0:
```python
import jax
import jax.numpy as jnp
from jax import lax
from jax.sharding import PartitionSpec as P

D = 2304
NS_ITERS = 2


beta_one = 0.9
beta_two = 0.95
stat_decay = 0.95
adam_eps = 1e-08
first_fix = 1.0 - 0.9**10
second_fix = 1.0 - 0.95**10
shrink = 0.6
norm_eps = 1e-06


def exact_dot(left, right):
    return jnp.dot(left, right, precision=lax.Precision.HIGHEST, preferred_element_type=jnp.float32)


def contract_rows(left, right):
    return lax.dot_general(
        left,
        right,
        (((0,), (0,)), ((), ())),
        precision=lax.Precision.HIGHEST,
        preferred_element_type=jnp.float32,
    )


def contract_cols(left, right):
    return lax.dot_general(
        left,
        right,
        (((1,), (1,)), ((), ())),
        precision=lax.Precision.HIGHEST,
        preferred_element_type=jnp.float32,
    )


def newton_product(iterate):
    iterate_cols = lax.all_gather(iterate, "shard", axis=0, tiled=True)
    gram_part = lax.psum_scatter(
        contract_cols(iterate_cols, iterate), ("tensor", "section"), scatter_dimension=0, tiled=True
    )
    gram_block = lax.all_gather(gram_part, ("tensor", "section"), axis=0, tiled=True)
    return contract_rows(gram_block, iterate_cols)


def shards(grad_parts, moment, second, stat_left, basis_left):
    partial_value = grad_parts[0].astype(jnp.float32)
    grad_flip = lax.psum_scatter(
        partial_value.astype(jnp.bfloat16), "shard", scatter_dimension=1, tiled=True
    )
    grad = grad_flip.T
    grad_cols = lax.all_gather(grad, "shard", axis=0, tiled=True)
    piece = grad_cols
    gram_part = lax.psum_scatter(
        lax.dot_general(
            piece, grad, (((1,), (1,)), ((), ())), preferred_element_type=jnp.float32
        ).astype(jnp.bfloat16),
        ("tensor", "section"),
        scatter_dimension=0,
        tiled=True,
    ).astype(jnp.float32)
    stat_next = stat_decay * stat_left + (1.0 - stat_decay) / D * gram_part.T
    basis_rows = lax.all_gather(basis_left, ("tensor", "section"), axis=1, tiled=True)
    rotated = exact_dot(basis_rows, grad_cols.astype(jnp.float32))
    moment_next = beta_one * moment + (1.0 - beta_one) * rotated
    second_next = beta_two * second + (1.0 - beta_two) * rotated * rotated
    ratio = moment_next / first_fix / (jnp.sqrt(second_next / second_fix) + adam_eps)
    piece = basis_rows
    update = lax.psum_scatter(contract_rows(piece, ratio), "shard", scatter_dimension=0, tiled=True)
    power = exact_dot(basis_rows, lax.all_gather(stat_next, "shard", axis=0, tiled=True))
    total_sq = lax.psum(jnp.sum(power * power), ("shard", "tensor", "section"))
    scale = shrink * jnp.sqrt(D / (total_sq + norm_eps))
    iterate = power * scale
    remaining = NS_ITERS
    for turn in range(remaining):
        iterate = 1.5 * iterate - 0.5 * newton_product(iterate)
    return (update, moment_next, second_next, stat_next, iterate)


def solution(mesh):
    in_specs = (
        P("shard", ("tensor", "section"), None),
        P("shard", ("tensor", "section")),
        P("shard", ("tensor", "section")),
        P("shard", ("tensor", "section")),
        P("shard", ("tensor", "section")),
    )
    out_specs = (
        P("shard", ("tensor", "section")),
        P("shard", ("tensor", "section")),
        P("shard", ("tensor", "section")),
        P("shard", ("tensor", "section")),
        P("shard", ("tensor", "section")),
    )
    return jax.shard_map(shards, mesh=mesh, in_specs=in_specs, out_specs=out_specs, check_vma=False)
```

profile of v0, /device:TPU:0, one launch (start us, length us, event | category | flops | bytes accessed | tf_op | source)
XLA Modules:
  0.0 1082.0 jit_solution(9778263371361913803)
XLA Ops:
  7.2 2.4 copy.10
  9.7 12.0 %reduce-scatter.16.cloned.1.call-done = bf16[1152,144]{1,0:T(8,128)(2,1)} async-done(((bf16[2304,144]{1,0:T(8,128)(2,1)}), bf16[1152,144]{1,0:T(8,128)(2,1)}) %reduce-scatter.16.cloned.1.call-update) | async-done | bytes 331792
  21.7 1.3 copy.11
  23.0 2.3 all_gather.22
  25.2 5.2 convolution_convert_fusion
  30.5 141.9 %reduce-scatter.10.cloned.1.call-done = bf16[144,1152]{1,0:T(8,128)(2,1)} async-done(((bf16[2304,1152]{1,0:T(8,128)(2,1)}), bf16[144,1152]{1,0:T(8,128)(2,1)}) %reduce-scatter.10.cloned.1.call-update) | async-done | bytes 331792 | tf_op jit(solution)/shard_map/reduce_scatter | solution.py:61
  172.4 1.9 bitcast_add_fusion
  175.0 8.1 all-gather.9.cloned.1.call-done
  183.1 137.7 %all-gather.7.cloned.1.call-done = f32[1152,2304]{0,1:T(8,128)} async-done(((f32[1152,144]{0,1:T(8,128)}), f32[1152,2304]{0,1:T(8,128)}) %all-gather.7.cloned.1.call-update) | async-done | bytes 10616848 | tf_op jit(solution)/shard_map/all_gather | solution.py:70
  320.7 11.3 %multiply_reduce_fusion = (f32[]{:T(128)}, f32[144,1152]{1,0:T(8,128)S(1)}) fusion(f32[2304,144]{0,1:T(8,128)} %all-gather.9.cloned.1.call-done, f32[1152,2304]{0,1:T(8,128)} %all-gather.7.cloned.1.call-done), kind=kOutput, calls=%fused_computation.9 | convolution fusion | flops 4586803200 | bytes 12607492 | tf_op jit(solution)/shard_map/dot_general | solution.py:21
  332.0 38.6 %psum.7 = f32[]{:T(128)} all-reduce(f32[]{:T(128)} %get-tuple-element.7), channel_id=1, replica_groups=mesh['shard'=2,'tensor'=4,'section'=4] {'shard','tensor','section'}, use_global_device_ids=true, to_apply=%region_4.0 | all-reduce | flops 1 | bytes 8 | tf_op jit(solution)/shard_map/psum | solution.py:78
  371.4 0.9 multiply_bitcast_fusion
  372.5 10.3 all-gather.11.cloned.1.call-done
  382.8 12.9 %fusion.8 = f32[2304,1152]{1,0:T(8,128)} fusion(f32[2304,144]{0,1:T(8,128)} %all-gather.11.cloned.1.call-done, f32[144,1152]{1,0:T(8,128)S(1)} %get-tuple-element.8, f32[]{:T(128)S(6)} %mul_shard_map.3), kind=kOutput, calls=%fused_computation.16 | convolution fusion | flops 4586637312 | bytes 12607492 | tf_op jit(solution)/shard_map/dot_general | solution.py:35
  395.8 183.4 %reduce-scatter.12.cloned.1.call-done = f32[144,1152]{1,0:T(8,128)} async-done(((f32[2304,1152]{1,0:T(8,128)}), f32[144,1152]{1,0:T(8,128)}) %reduce-scatter.12.cloned.1.call-update) | async-done | bytes 663568 | tf_op jit(solution)/shard_map/reduce_scatter | solution.py:46
  579.3 135.5 %all-gather.13.cloned.1.call-done = f32[2304,1152]{1,0:T(8,128)} async-done(((f32[144,1152]{1,0:T(8,128)}), f32[2304,1152]{1,0:T(8,128)}) %all-gather.13.cloned.1.call-update) | async-done | bytes 10616848 | tf_op jit(solution)/shard_map/all_gather | solution.py:49
  714.8 10.2 fusion
  725.1 7.7 all-gather.15.cloned.1.call-done
  732.8 13.1 %fusion.18 = f32[2304,1152]{1,0:T(8,128)} fusion(f32[2304,144]{0,1:T(8,128)} %all-gather.15.cloned.1.call-done, f32[1152,144]{0,1:T(8,128)} %fusion), kind=kOutput, calls=%fused_computation.27 | convolution fusion | flops 4586471424 | bytes 12607488 | tf_op jit(solution)/shard_map/dot_general | solution.py:35
  746.0 183.5 %reduce-scatter.14.cloned.1.call-done = f32[144,1152]{1,0:T(8,128)} async-done(((f32[2304,1152]{1,0:T(8,128)}), f32[144,1152]{1,0:T(8,128)}) %reduce-scatter.14.cloned.1.call-update) | async-done | bytes 663568 | tf_op jit(solution)/shard_map/reduce_scatter | solution.py:46
  929.8 8.1 multiply_add_fusion
  938.0 17.8 %convolution_bitcast_fusion = f32[2304,144]{0,1:T(8,128)} fusion(f32[1152,2304]{0,1:T(8,128)} %all-gather.7.cloned.1.call-done, f32[1152,144]{0,1:T(8,128)S(1)} %get-tuple-element.6, f32[1152,144]{0,1:T(8,128)S(1)} %get-tuple-element.5), kind=kOutput, calls=%fused_computation.1 | convolution fusion | flops 4587134976 | bytes 13271040 | tf_op jit(solution)/shard_map/dot_general | solution.py:25
  955.8 109.6 %all-gather.17.cloned.1.call-done = f32[2304,1152]{1,0:T(8,128)} async-done(((f32[144,1152]{1,0:T(8,128)}), f32[2304,1152]{1,0:T(8,128)}) %all-gather.17.cloned.1.call-update) | async-done | bytes 10616848 | tf_op jit(solution)/shard_map/all_gather | solution.py:49
  1065.3 10.2 fusion.1
  (41 shorter events, 1.6 us)
Async XLA Ops:
  7.2 165.3 %copy-start.8 = (f32[1152,144]{0,1:T(8,128)S(1)}, f32[1152,144]{0,1:T(8,128)}, u32[]{:S(2)}) copy-start(f32[1152,144]{0,1:T(8,128)} %param.8) | copy-start | bytes 1990660
  7.2 14.5 %reduce-scatter.16.cloned.1.call-start = ((), (), s32[]{:S(2)}) async-start(), calls=%async_computation.15 | async-start | bytes 1769472
  9.6 162.8 %reduce-scatter.10.cloned.1.call-start = ((), (), s32[]{:S(2)}) async-start(), calls=%async_computation.7 | async-start | bytes 5640192 | tf_op jit(solution)/shard_map/reduce_scatter | solution.py:61
  30.5 152.6 %all-gather.9.cloned.1.call-start = ((), (), s32[]{:S(2)}) async-start(), calls=%async_computation.8 | async-start | bytes 1990656 | tf_op jit(solution)/shard_map/all_gather | solution.py:77
  174.4 146.3 %all-gather.7.cloned.1.call-start = ((), (), s32[]{:S(2)}) async-start(), calls=%async_computation.5 | async-start | bytes 11280384 | tf_op jit(solution)/shard_map/all_gather | solution.py:70
  175.0 207.8 %all-gather.11.cloned.1.call-start = ((), (), s32[]{:S(2)}) async-start(), calls=%async_computation.9 | async-start | bytes 1990656 | tf_op jit(solution)/shard_map/all_gather | solution.py:45
  372.3 342.5 %copy-start.1 = (f32[1152,144]{0,1:T(8,128)S(1)}, f32[1152,144]{0,1:T(8,128)}, u32[]{:S(2)}) copy-start(f32[1152,144]{0,1:T(8,128)} %multiply_bitcast_fusion) | copy-start | bytes 1990660
  372.3 206.9 %reduce-scatter.12.cloned.1.call-start = ((), (), s32[]{:S(2)}) async-start(), calls=%async_computation.10 | async-start | bytes 11280384 | tf_op jit(solution)/shard_map/reduce_scatter | solution.py:46
  382.8 332.0 %copy-start.2 = (f32[2304,144]{0,1:T(8,128)S(1)}, f32[2304,144]{0,1:T(8,128)}, u32[]{:S(2)}) copy-start(f32[2304,144]{0,1:T(8,128)} %all-gather.11.cloned.1.call-done) | copy-start | bytes 3981316
  395.8 319.0 %all-gather.13.cloned.1.call-start = ((), (), s32[]{:S(2)}) async-start(), calls=%async_computation.11 | async-start | bytes 11280384 | tf_op jit(solution)/shard_map/all_gather | solution.py:49
  579.3 153.6 %all-gather.15.cloned.1.call-start = ((), (), s32[]{:S(2)}) async-start(), calls=%async_computation.12 | async-start | bytes 1990656 | tf_op jit(solution)/shard_map/all_gather | solution.py:45
  725.0 204.8 %copy-start.6 = (f32[1152,144]{0,1:T(8,128)S(1)}, f32[1152,144]{0,1:T(8,128)}, u32[]{:S(2)}) copy-start(f32[1152,144]{0,1:T(8,128)} %param.6) | copy-start | bytes 1990660
  725.0 204.8 %copy-start.7 = (f32[1152,144]{0,1:T(8,128)S(1)}, f32[1152,144]{0,1:T(8,128)}, u32[]{:S(2)}) copy-start(f32[1152,144]{0,1:T(8,128)} %param.7) | copy-start | bytes 1990660
  725.1 204.5 %reduce-scatter.14.cloned.1.call-start = ((), (), s32[]{:S(2)}) async-start(), calls=%async_computation.13 | async-start | bytes 11280384 | tf_op jit(solution)/shard_map/reduce_scatter | solution.py:46
  745.9 319.4 %all-gather.17.cloned.1.call-start = ((), (), s32[]{:S(2)}) async-start(), calls=%async_computation.14 | async-start | bytes 11280384 | tf_op jit(solution)/shard_map/all_gather | solution.py:49
  929.5 146.0 %reduce-scatter.8.cloned.1.call-start = ((), (), s32[]{:S(2)}) async-start(), calls=%async_computation.6 | async-start | bytes 1990656 | tf_op jit(solution)/shard_map/reduce_scatter | solution.py:76
  937.9 137.6 %copy-start.4 = (f32[1152,144]{0,1:T(8,128)}, f32[1152,144]{0,1:T(8,128)S(1)}, u32[]{:S(2)}) copy-start(f32[1152,144]{0,1:T(8,128)S(1)} %get-tuple-element.5) | copy-start | bytes 1990660
  937.9 137.6 %copy-start.5 = (f32[1152,144]{0,1:T(8,128)}, f32[1152,144]{0,1:T(8,128)S(1)}, u32[]{:S(2)}) copy-start(f32[1152,144]{0,1:T(8,128)S(1)} %get-tuple-element.6) | copy-start | bytes 1990660
  937.9 127.4 %copy-start = (f32[1152,144]{0,1:T(8,128)S(1)}, f32[1152,144]{0,1:T(8,128)}, u32[]{:S(2)}) copy-start(f32[1152,144]{0,1:T(8,128)} %fusion) | copy-start | bytes 1990660
  937.9 127.4 %copy-start.3 = (f32[2304,144]{0,1:T(8,128)S(1)}, f32[2304,144]{0,1:T(8,128)}, u32[]{:S(2)}) copy-start(f32[2304,144]{0,1:T(8,128)} %all-gather.15.cloned.1.call-done) | copy-start | bytes 3981316
Sparse Core Ops, SparseCore 0:
  10.3 11.3 reduce-scatter.15
  30.6 141.7 reduce-scatter.9
  174.6 8.3 all-gather.8
  186.1 134.6 all-gather.6
  372.4 10.3 all-gather.10
  395.9 183.2 reduce-scatter.11
  582.0 132.7 all-gather.12
  725.2 7.6 all-gather.14
  746.0 183.4 reduce-scatter.13
  932.5 132.7 all-gather.16
  1068.2 6.9 reduce-scatter.7
where the time goes:
time: 1080 us
  waiting for transfers between devices  930 us (86%)
  matrix products  88.8 us (8%)
  blocking collectives  40.9 us (4%)
  between operations  14.7 us (1%)
    reduce_scatter x2, waiting for transfers between devices, newton_product(): lax.psum_scatter(contract_cols(iterate_cols, iterate), ('tensor', 'sectio...  367 us
    all_gather x2, waiting for transfers between devices, newton_product(): lax.all_gather(gram_part, ('tensor', 'section'), axis=0, tiled=True)  245 us
    reduce_scatter x1, waiting for transfers between devices, shards(): lax.psum_scatter(lax.dot_general(piece, grad, (((1,), (1,)), ((), ())), p...  142 us
    all_gather x1, waiting for transfers between devices, shards(): lax.all_gather(basis_left, ('tensor', 'section'), axis=1, tiled=True)  138 us
    psum x1, blocking collectives, shards(): total_sq = lax.psum(jnp.sum(power * power), ('shard', 'tensor', 'section'))  38.6 us
    dot_general x3, matrix products, contract_rows(): lax.dot_general(left, right, (((0,), (0,)), ((), ())), precision=lax.Prec...  38.1 us
    dot_general x2, matrix products, contract_cols(): lax.dot_general(left, right, (((1,), (1,)), ((), ())), precision=lax.Prec...  26 us
  transfers between devices with their start and end apart: 11, of which 10 were waited for; matrix products, arithmetic and copies ran while one was open for 3% of the time, Pallas kernels for 0%

commit v1 on v0

v1 whole, which is shorter than its diff:
```python
import jax
import jax.numpy as jnp
from jax import lax
from jax.sharding import PartitionSpec as P

D = 2304
NS_ITERS = 2


beta_one = 0.9
beta_two = 0.95
stat_decay = 0.95
adam_eps = 1e-08
first_fix = 1.0 - 0.9**10
second_fix = 1.0 - 0.95**10
shrink = 0.6
norm_eps = 1e-06

TS = ("tensor", "section")


def exact_dot(left, right):
    return jnp.dot(left, right, precision=lax.Precision.HIGHEST, preferred_element_type=jnp.float32)


def contract_rows(left, right):
    return lax.dot_general(
        left,
        right,
        (((0,), (0,)), ((), ())),
        precision=lax.Precision.HIGHEST,
        preferred_element_type=jnp.float32,
    )


def make_shards(n_shard, n_section, n_ts):
    rows = D // n_shard
    cols = D // n_ts
    assert rows % cols == 0 or cols % rows == 0

    def block_rows(grad_rows, k):
        start = k * cols
        if cols <= rows:
            piece = lax.dynamic_slice_in_dim(grad_rows, start % rows, cols, axis=0)
            pieces = lax.all_gather(piece, "shard", axis=0, tiled=False)
            return lax.dynamic_index_in_dim(pieces, start // rows, axis=0, keepdims=False)
        full = lax.all_gather(grad_rows, "shard", axis=0, tiled=True)
        return lax.dynamic_slice_in_dim(full, start, cols, axis=0)

    def newton_step(iterate):
        iterate_rows = lax.all_gather(iterate, TS, axis=1, tiled=True)
        z_cols = lax.psum(contract_rows(iterate_rows, iterate), "shard")
        return 1.5 * iterate - 0.5 * exact_dot(iterate_rows, z_cols)

    def shards(grad_parts, moment, second, stat_left, basis_left):
        k = lax.axis_index("tensor") * n_section + lax.axis_index("section")
        partial_value = grad_parts[0].astype(jnp.float32)
        grad_flip = lax.psum_scatter(
            partial_value.astype(jnp.bfloat16), "shard", scatter_dimension=1, tiled=True
        )
        grad = grad_flip.T
        grad_cols = lax.all_gather(grad, "shard", axis=0, tiled=True)
        grad_rows = lax.all_gather(grad, TS, axis=1, tiled=True)
        grad_krows = block_rows(grad_rows, k)
        gram = lax.dot_general(
            grad_rows, grad_krows, (((1,), (1,)), ((), ())), preferred_element_type=jnp.float32
        )
        stat_next = stat_decay * stat_left + (1.0 - stat_decay) / D * gram
        basis_rows = lax.all_gather(basis_left, TS, axis=1, tiled=True)
        rotated = exact_dot(basis_rows, grad_cols.astype(jnp.float32))
        moment_next = beta_one * moment + (1.0 - beta_one) * rotated
        second_next = beta_two * second + (1.0 - beta_two) * rotated * rotated
        ratio = moment_next / first_fix / (jnp.sqrt(second_next / second_fix) + adam_eps)
        update = lax.psum_scatter(contract_rows(basis_rows, ratio), "shard", scatter_dimension=0, tiled=True)
        power = exact_dot(basis_rows, lax.all_gather(stat_next, "shard", axis=0, tiled=True))
        total_sq = lax.psum(jnp.sum(power * power), ("shard", "tensor", "section"))
        scale = shrink * jnp.sqrt(D / (total_sq + norm_eps))
        iterate = power * scale
        for turn in range(NS_ITERS):
            iterate = newton_step(iterate)
        return (update, moment_next, second_next, stat_next, iterate)

    return shards


def solution(mesh):
    n_shard = mesh.shape["shard"]
    n_section = mesh.shape["section"]
    n_ts = mesh.shape["tensor"] * n_section
    in_specs = (
        P("shard", TS, None),
        P("shard", TS),
        P("shard", TS),
        P("shard", TS),
        P("shard", TS),
    )
    out_specs = (
        P("shard", TS),
        P("shard", TS),
        P("shard", TS),
        P("shard", TS),
        P("shard", TS),
    )
    return jax.shard_map(
        make_shards(n_shard, n_section, n_ts), mesh=mesh, in_specs=in_specs, out_specs=out_specs, check_vma=False
    )
```

time: 1080 us -> 700 us (0.65)
  waiting for transfers between devices: 930 us -> 544 us
    reduce_scatter x4 -> x1, waiting for transfers between devices: 509 us -> 0.01 us  [shards(): lax.psum_scatter(contract_rows(basis_rows, ratio), 'shard', scatter_dimen...]
    all_gather x5, waiting for transfers between devices: 401 us -> 503 us  [the longest x2 269 us: newton_step(): iterate_rows = lax.all_gather(iterate, TS, axis=1, tiled=True)]
    dot_general x3 -> x1, matrix products: 31.3 us -> 4.66 us  [shards(): lax.dot_general(grad_rows, grad_krows, (((1,), (1,)), ((), ())), preferre...]
    dot_general x2 -> x4, matrix products: 19.4 us -> 41.6 us  [exact_dot(): jnp.dot(left, right, precision=lax.Precision.HIGHEST, preferred_element_t...]
    psum x0 -> x2, waiting for transfers between devices: none -> 18.3 us  [newton_step(): z_cols = lax.psum(contract_rows(iterate_rows, iterate), 'shard')]
  transfers between devices with their start and end apart: 11 -> 10, of which waited for: 10 -> 8; matrix products, arithmetic and copies ran while one was open for 3% -> 5% of each run, Pallas kernels for 0% -> 0%
where the time goes in v1:
time: 700 us; the launch traced here: 699 us
  waiting for transfers between devices  544 us (78%)
  matrix products  89.3 us (13%)
  blocking collectives  41.2 us (6%)
  between operations  15.1 us (2%)
  local copies, waits for them, and re-layouts  7.69 us (1%)
    all_gather x2, waiting for transfers between devices, newton_step(): iterate_rows = lax.all_gather(iterate, TS, axis=1, tiled=True)  269 us
    all_gather x1, waiting for transfers between devices, shards(): basis_rows = lax.all_gather(basis_left, TS, axis=1, tiled=True)  138 us
    all_gather x1, waiting for transfers between devices, shards(): grad_rows = lax.all_gather(grad, TS, axis=1, tiled=True)  88.6 us
    dot_general x3, matrix products, contract_rows(): lax.dot_general(left, right, (((0,), (0,)), ((), ())), precision=lax.Prec...  43.1 us
    dot_general x4, matrix products, exact_dot(): jnp.dot(left, right, precision=lax.Precision.HIGHEST, preferred_element_t...  41.6 us
    psum x1, blocking collectives, shards(): total_sq = lax.psum(jnp.sum(power * power), ('shard', 'tensor', 'section'))  38.6 us
    psum x2, waiting for transfers between devices, newton_step(): z_cols = lax.psum(contract_rows(iterate_rows, iterate), 'shard')  18.3 us
  transfers between devices with their start and end apart: 10, of which 8 were waited for; matrix products, arithmetic and copies ran while one was open for 5% of the time, Pallas kernels for 0%

profile of v1, /device:TPU:0, one launch (start us, length us, event | category | flops | bytes accessed | tf_op | source)
XLA Modules:
  0.0 699.2 jit_solution(2090115665471393711)
XLA Ops:
  7.2 2.4 copy.13
  9.7 12.0 %reduce-scatter.7.cloned.1.call-done = bf16[1152,144]{1,0:T(8,128)(2,1)} async-done(((bf16[2304,144]{1,0:T(8,128)(2,1)}), bf16[1152,144]{1,0:T(8,128)(2,1)}) %reduce-scatter.7.cloned.1.call-update) | async-done | bytes 331792
  21.7 2.0 copy.14
  23.8 88.6 %all-gather.10.cloned.1.call-done = bf16[1152,2304]{0,1:T(8,128)(2,1)} async-done(((bf16[1152,144]{0,1:T(8,128)(2,1)}), bf16[1152,2304]{0,1:T(8,128)(2,1)}) %all-gather.10.cloned.1.call-update) | async-done | bytes 5308432 | tf_op jit(solution)/shard_map/all_gather | solution.py:63
  112.3 2.0 constant_dynamic-slice_fusion
  114.3 1.3 copy.15
  115.7 8.0 %all-gather.18.cloned.1.call-done = bf16[288,2304]{1,0:T(8,128)(2,1)} async-done(((bf16[144,2304]{1,0:T(8,128)(2,1)}), bf16[288,2304]{1,0:T(8,128)(2,1)}) %all-gather.18.cloned.1.call-update) | async-done | bytes 1327120 | tf_op jit(solution)/shard_map/all_gather | solution.py:45
  123.7 4.7 fusion.3
  128.4 0.5 all-gather.8.cloned.1.call-update
  129.0 10.1 %all-gather.12.cloned.1.call-done = f32[2304,144]{0,1:T(8,128)} async-done(((f32[1152,144]{0,1:T(8,128)}), f32[2304,144]{0,1:T(8,128)}) %all-gather.12.cloned.1.call-update) | async-done | bytes 1327120 | tf_op jit(solution)/shard_map/all_gather | solution.py:75
  139.1 137.6 %all-gather.8.cloned.1.call-done = f32[1152,2304]{0,1:T(8,128)} async-done(((f32[1152,144]{0,1:T(8,128)}), f32[1152,2304]{0,1:T(8,128)}) %all-gather.8.cloned.1.call-update) | async-done | bytes 10616848 | tf_op jit(solution)/shard_map/all_gather | solution.py:69
  276.8 11.3 %multiply_reduce_fusion = (f32[]{:T(128)}, f32[144,1152]{1,0:T(8,128)S(1)}) fusion(f32[2304,144]{0,1:T(8,128)} %all-gather.12.cloned.1.call-done, f32[1152,2304]{0,1:T(8,128)} %all-gather.8.cloned.1.call-done), kind=kOutput, calls=%fused_computation.11 | convolution fusion | flops 4586803200 | bytes 12607492 | tf_op jit(solution)/shard_map/dot_general | solution.py:23
  288.1 38.6 %psum.21 = f32[]{:T(128)} all-reduce(f32[]{:T(128)} %get-tuple-element.7), channel_id=1, replica_groups=mesh['shard'=2,'tensor'=4,'section'=4] {'shard','tensor','section'}, use_global_device_ids=true, to_apply=%region_3.4 | all-reduce | flops 1 | bytes 8 | tf_op jit(solution)/shard_map/psum | solution.py:76
  327.4 0.9 multiply_bitcast_fusion
  328.6 134.3 %all-gather.14.cloned.1.call-done = f32[1152,2304]{0,1:T(8,128)} async-done(((f32[1152,144]{0,1:T(8,128)}), f32[1152,2304]{0,1:T(8,128)}) %all-gather.14.cloned.1.call-update) | async-done | bytes 10616848 | tf_op jit(solution)/shard_map/all_gather | solution.py:51
  462.9 15.9 %fusion.12 = f32[2304,144]{0,1:T(8,128)} fusion(f32[1152,2304]{0,1:T(8,128)} %all-gather.14.cloned.1.call-done, f32[144,1152]{1,0:T(8,128)S(1)} %get-tuple-element.8, f32[]{:T(128)S(6)} %mul_shard_map.3), kind=kOutput, calls=%fused_computation.19 | convolution fusion | flops 4586637312 | bytes 12607492 | tf_op jit(solution)/shard_map/dot_general | solution.py:27
  478.9 18.3 %all-reduce.3.cloned.1.call-done = f32[2304,144]{0,1:T(8,128)} async-done(((f32[2304,144]{0,1:T(8,128)}), f32[2304,144]{0,1:T(8,128)}) %all-reduce.3.cloned.1.call-update) | async-done | bytes 1327120 | tf_op jit(solution)/shard_map/psum | solution.py:52
  497.2 10.6 %fusion = f32[1152,144]{0,1:T(8,128)} fusion(f32[1152,2304]{0,1:T(8,128)} %all-gather.14.cloned.1.call-done, f32[2304,144]{0,1:T(8,128)} %all-reduce.3.cloned.1.call-done, f32[1152,144]{0,1:T(8,128)S(1)} %copy-done.1), kind=kOutput, calls=%fused_computation.4 | convolution fusion | flops 4586969088 | bytes 13271040 | tf_op jit(solution)/shard_map/dot_general | solution.py:23
  507.9 134.7 %all-gather.16.cloned.1.call-done = f32[1152,2304]{0,1:T(8,128)} async-done(((f32[1152,144]{0,1:T(8,128)}), f32[1152,2304]{0,1:T(8,128)}) %all-gather.16.cloned.1.call-update) | async-done | bytes 10616848 | tf_op jit(solution)/shard_map/all_gather | solution.py:51
  642.6 14.7 %fusion.22 = f32[2304,144]{0,1:T(8,128)} fusion(f32[1152,2304]{0,1:T(8,128)} %all-gather.16.cloned.1.call-done, f32[1152,144]{0,1:T(8,128)} %fusion), kind=kOutput, calls=%fused_computation.31 | convolution fusion | flops 4586471424 | bytes 12607488 | tf_op jit(solution)/shard_map/dot_general | solution.py:27
  657.5 2.6 all_gather.25
  660.1 8.9 %multiply_add_fusion = (f32[1152,144]{0,1:T(8,128)S(1)}, f32[1152,144]{0,1:T(8,128)S(1)}) fusion(f32[1152,144]{0,1:T(8,128)S(1)} %copy-done.5, f32[1152,144]{0,1:T(8,128)S(1)} %copy-done.6, f32[1152,2304]{0,1:T(8,128)} %all-gather.8.cloned.1.call-done, bf16[2304,144]{0,1:T(8,128)(2,1)S(1)} %all_gather.25), kind=kOutput, calls=%fused_computation.18 | convolution fusion | flops 4587632640 | bytes 13934592 | tf_op jit(solution)/shard_map/dot_general | solution.py:23
  669.1 12.5 %convolution_bitcast_fusion = f32[2304,144]{0,1:T(8,128)} fusion(f32[1152,2304]{0,1:T(8,128)S(1)} %bitcast.30, f32[1152,144]{0,1:T(8,128)S(1)} %get-tuple-element.6, f32[1152,144]{0,1:T(8,128)S(1)} %get-tuple-element.5), kind=kOutput, calls=%fused_computation | convolution fusion | flops 4587134976 | bytes 13271040 | tf_op jit(solution)/shard_map/dot_general | solution.py:27
  681.6 10.8 %fusion.1 = f32[1152,144]{0,1:T(8,128)} fusion(f32[1152,2304]{0,1:T(8,128)} %all-gather.16.cloned.1.call-done, f32[2304,144]{0,1:T(8,128)} %all-reduce.5.cloned.1.call-done, f32[1152,144]{0,1:T(8,128)S(1)} %copy-done), kind=kOutput, calls=%fused_computation.5 | convolution fusion | flops 4586969088 | bytes 13271040 | tf_op jit(solution)/shard_map/dot_general | solution.py:23
  (44 shorter events, 0.8 us)
Async XLA Ops:
  7.2 116.5 %copy-start.7 = (f32[1152,144]{0,1:T(8,128)S(1)}, f32[1152,144]{0,1:T(8,128)}, u32[]{:S(2)}) copy-start(f32[1152,144]{0,1:T(8,128)} %param.8) | copy-start | bytes 1990660
  7.2 14.5 %reduce-scatter.7.cloned.1.call-start = ((), (), s32[]{:S(2)}) async-start(), calls=%async_computation.11 | async-start | bytes 1769472
  9.6 102.7 %all-gather.10.cloned.1.call-start = ((), (), s32[]{:S(2)}) async-start(), calls=%async_computation.4 | async-start | bytes 5640192 | tf_op jit(solution)/shard_map/all_gather | solution.py:63
  23.7 100.0 %all-gather.18.cloned.1.call-start = ((), (), s32[]{:S(2)}) async-start(), calls=%async_computation.10 | async-start | bytes 1990656 | tf_op jit(solution)/shard_map/all_gather | solution.py:45
  115.6 23.6 %all-gather.12.cloned.1.call-start = ((), (), s32[]{:S(2)}) async-start(), calls=%async_computation.5 | async-start | bytes 1990656 | tf_op jit(solution)/shard_map/all_gather | solution.py:75
  128.4 148.4 %all-gather.8.cloned.1.call-start = ((), (), s32[]{:S(2)}) async-start(), calls=%async_computation.2 | async-start | bytes 11280384 | tf_op jit(solution)/shard_map/all_gather | solution.py:69
  129.0 333.9 %all-gather.14.cloned.1.call-start = ((), (), s32[]{:S(2)}) async-start(), calls=%async_computation.6 | async-start | bytes 11280384 | tf_op jit(solution)/shard_map/all_gather | solution.py:51
  328.3 168.9 %copy-start.1 = (f32[1152,144]{0,1:T(8,128)S(1)}, f32[1152,144]{0,1:T(8,128)}, u32[]{:S(2)}) copy-start(f32[1152,144]{0,1:T(8,128)} %multiply_bitcast_fusion) | copy-start | bytes 1990660
  328.4 168.9 %all-reduce.3.cloned.1.call-start = ((), (), s32[]{:S(2)}) async-start(), calls=%async_computation.7 | async-start | bytes 2654208 | tf_op jit(solution)/shard_map/psum | solution.py:52
  478.8 163.8 %all-gather.16.cloned.1.call-start = ((), (), s32[]{:S(2)}) async-start(), calls=%async_computation.8 | async-start | bytes 11280384 | tf_op jit(solution)/shard_map/all_gather | solution.py:51
  507.8 149.6 %copy-start.4 = (bf16[144,1152]{1,0:T(8,128)(2,1)S(1)}, bf16[144,1152]{1,0:T(8,128)(2,1)}, u32[]{:S(2)}) copy-start(bf16[144,1152]{1,0:T(8,128)(2,1)} %copy.14) | copy-start | bytes 995332
  507.9 152.2 %copy-start.5 = (f32[1152,144]{0,1:T(8,128)S(1)}, f32[1152,144]{0,1:T(8,128)}, u32[]{:S(2)}) copy-start(f32[1152,144]{0,1:T(8,128)} %param.6) | copy-start | bytes 1990660
  507.9 152.2 %copy-start.6 = (f32[1152,144]{0,1:T(8,128)S(1)}, f32[1152,144]{0,1:T(8,128)}, u32[]{:S(2)}) copy-start(f32[1152,144]{0,1:T(8,128)} %param.7) | copy-start | bytes 1990660
  507.9 173.7 %all-reduce.5.cloned.1.call-start = ((), (), s32[]{:S(2)}) async-start(), calls=%async_computation.9 | async-start | bytes 2654208 | tf_op jit(solution)/shard_map/psum | solution.py:52
  657.4 35.0 %reduce-scatter.5.cloned.1.call-start = ((), (), s32[]{:S(2)}) async-start(), calls=%async_computation.3 | async-start | bytes 1990656 | tf_op jit(solution)/shard_map/reduce_scatter | solution.py:74
  657.4 11.6 %slice-start = ((s8[10616832]{0:T(1024)(128)(4,1)}), s8[4194304]{0:T(1024)(128)(4,1)S(1)}, s32[]{:S(2)}) async-start(s8[10616832]{0:T(1024)(128)(4,1)} %bitcast.29), calls=%async_computation.12 | async-start | bytes 8388608
  660.1 8.9 %slice-start.1 = ((s8[10616832]{0:T(1024)(128)(4,1)}), s8[4194304]{0:T(1024)(128)(4,1)S(1)}, s32[]{:S(2)}) async-start(s8[10616832]{0:T(1024)(128)(4,1)} %bitcast.29), calls=%async_computation.13 | async-start | bytes 8388608
  660.1 8.9 %slice-start.2 = ((s8[10616832]{0:T(1024)(128)(4,1)}), s8[2228224]{0:T(1024)(128)(4,1)S(1)}, s32[]{:S(2)}) async-start(s8[10616832]{0:T(1024)(128)(4,1)} %bitcast.29), calls=%async_computation.14 | async-start | bytes 4456448
  669.0 12.5 %copy-start.2 = (f32[1152,144]{0,1:T(8,128)}, f32[1152,144]{0,1:T(8,128)S(1)}, u32[]{:S(2)}) copy-start(f32[1152,144]{0,1:T(8,128)S(1)} %get-tuple-element.5) | copy-start | bytes 1990660
  669.0 12.5 %copy-start.3 = (f32[1152,144]{0,1:T(8,128)}, f32[1152,144]{0,1:T(8,128)S(1)}, u32[]{:S(2)}) copy-start(f32[1152,144]{0,1:T(8,128)S(1)} %get-tuple-element.6) | copy-start | bytes 1990660
  669.1 12.5 %copy-start = (f32[1152,144]{0,1:T(8,128)S(1)}, f32[1152,144]{0,1:T(8,128)}, u32[]{:S(2)}) copy-start(f32[1152,144]{0,1:T(8,128)} %fusion) | copy-start | bytes 1990660
Sparse Core Ops, SparseCore 0:
  10.3 11.3 reduce-scatter.6
  25.4 86.8 all-gather.9
  115.7 7.9 all-gather.17
  128.5 10.6 all-gather.11
  142.1 134.6 all-gather.7
  328.5 134.3 all-gather.13
  479.0 18.2 all-reduce.2
  508.0 134.6 all-gather.15
  657.5 18.1 all-reduce.4
  681.7 6.7 reduce-scatter.4

commit v2 on v1

--- a/solution.py
+++ b/solution.py
@@ -20,7 +20,7 @@
 
 
 def exact_dot(left, right):
-    return jnp.dot(left, right, precision=lax.Precision.HIGHEST, preferred_element_type=jnp.float32)
+    return jnp.dot(left, right, precision=lax.Precision.HIGH, preferred_element_type=jnp.float32)
 
 
 def contract_rows(left, right):
@@ -28,7 +28,7 @@
         left,
         right,
         (((0,), (0,)), ((), ())),
-        precision=lax.Precision.HIGHEST,
+        precision=lax.Precision.HIGH,
         preferred_element_type=jnp.float32,
     )
 
@@ -73,10 +73,15 @@
         ratio = moment_next / first_fix / (jnp.sqrt(second_next / second_fix) + adam_eps)
         update = lax.psum_scatter(contract_rows(basis_rows, ratio), "shard", scatter_dimension=0, tiled=True)
         power = exact_dot(basis_rows, lax.all_gather(stat_next, "shard", axis=0, tiled=True))
-        total_sq = lax.psum(jnp.sum(power * power), ("shard", "tensor", "section"))
+        power_rows = lax.all_gather(power, TS, axis=1, tiled=True)
+        power_rows, update = lax.optimization_barrier((power_rows, update))
+        z_part = contract_rows(power_rows, power)
+        sq_part = jnp.full((8, cols), jnp.sum(power_rows * power_rows), jnp.float32)
+        summed = lax.psum(jnp.concatenate([z_part, sq_part], axis=0), "shard")
+        total_sq = summed[D, 0]
         scale = shrink * jnp.sqrt(D / (total_sq + norm_eps))
-        iterate = power * scale
-        for turn in range(NS_ITERS):
+        iterate = (1.5 * scale) * power - (0.5 * scale * scale * scale) * exact_dot(power_rows, summed[:D])
+        for turn in range(NS_ITERS - 1):
             iterate = newton_step(iterate)
         return (update, moment_next, second_next, stat_next, iterate)
 

time: 700 us -> 643 us (0.919)
  blocking collectives: 41.2 us -> 2.28 us
  matrix products: 89.3 us -> 56.4 us
    all_gather x0 -> x1, waiting for transfers between devices: none -> 138 us  [shards(): power_rows = lax.all_gather(power, TS, axis=1, tiled=True)]
    all_gather x2 -> x1, waiting for transfers between devices: 269 us -> 135 us  [newton_step(): iterate_rows = lax.all_gather(iterate, TS, axis=1, tiled=True)]
    psum x1 -> x0, blocking collectives: 38.6 us -> none  [shards(): total_sq = lax.psum(jnp.sum(power * power), ('shard', 'tensor', 'section'))]
    dot_general x3, matrix products: 43.1 us -> 20.5 us  [contract_rows(): lax.dot_general(left, right, (((0,), (0,)), ((), ())), precision=lax.Prec...]
    psum x0 -> x1, waiting for transfers between devices: none -> 18.2 us  [shards(): summed = lax.psum(jnp.concatenate([z_part, sq_part], axis=0), 'shard')]
    dot_general x4, matrix products: 41.6 us -> 31.2 us  [exact_dot(): jnp.dot(left, right, precision=lax.Precision.HIGH, preferred_element_type...]
    all_gather x1, waiting for transfers between devices: 10.1 us -> 0.02 us  [shards(): lax.all_gather(stat_next, 'shard', axis=0, tiled=True)]
    reduce_sum x0 -> x1, other arithmetic: none -> 7.56 us  [shards(): sq_part = jnp.full((8, cols), jnp.sum(power_rows * power_rows), jnp.float32)]
  transfers between devices with their start and end apart: 10 -> 10, of which waited for: 8 -> 8; matrix products, arithmetic and copies ran while one was open for 5% -> 4% of each run, Pallas kernels for 0% -> 0%
where the time goes in v2:
time: 643 us; the launch traced here: 642 us
  waiting for transfers between devices  548 us (85%)
  matrix products  56.4 us (9%)
  between operations  15 us (2%)
  local copies, waits for them, and re-layouts  12.2 us (2%)
  other arithmetic  7.56 us (1%)
    all_gather x1, waiting for transfers between devices, shards(): power_rows = lax.all_gather(power, TS, axis=1, tiled=True)  138 us
    all_gather x1, waiting for transfers between devices, newton_step(): iterate_rows = lax.all_gather(iterate, TS, axis=1, tiled=True)  135 us
    all_gather x1, waiting for transfers between devices, shards(): basis_rows = lax.all_gather(basis_left, TS, axis=1, tiled=True)  131 us
    all_gather x1, waiting for transfers between devices, shards(): grad_rows = lax.all_gather(grad, TS, axis=1, tiled=True)  88.6 us
    dot_general x4, matrix products, exact_dot(): jnp.dot(left, right, precision=lax.Precision.HIGH, preferred_element_type...  31.2 us
    dot_general x3, matrix products, contract_rows(): lax.dot_general(left, right, (((0,), (0,)), ((), ())), precision=lax.Prec...  20.5 us
    psum x1, waiting for transfers between devices, newton_step(): z_cols = lax.psum(contract_rows(iterate_rows, iterate), 'shard')  18.4 us
    psum x1, waiting for transfers between devices, shards(): summed = lax.psum(jnp.concatenate([z_part, sq_part], axis=0), 'shard')  18.2 us
  transfers between devices with their start and end apart: 10, of which 8 were waited for; matrix products, arithmetic and copies ran while one was open for 4% of the time, Pallas kernels for 0%

profile of v2, /device:TPU:0, one launch (start us, length us, event | category | flops | bytes accessed | tf_op | source)
XLA Modules:
  0.0 642.4 jit_solution(11158889341009871335)
XLA Ops:
  7.2 2.3 copy.13
  9.6 12.1 %reduce-scatter.7.cloned.1.call-done = bf16[1152,144]{1,0:T(8,128)(2,1)} async-done(((bf16[2304,144]{1,0:T(8,128)(2,1)}), bf16[1152,144]{1,0:T(8,128)(2,1)}) %reduce-scatter.7.cloned.1.call-update) | async-done | bytes 331792
  21.6 2.0 copy.14
  23.7 88.6 %all-gather.8.cloned.1.call-done = bf16[1152,2304]{0,1:T(8,128)(2,1)} async-done(((bf16[1152,144]{0,1:T(8,128)(2,1)}), bf16[1152,2304]{0,1:T(8,128)(2,1)}) %all-gather.8.cloned.1.call-update) | async-done | bytes 5308432 | tf_op jit(solution)/shard_map/all_gather | solution.py:63
  112.3 2.0 constant_dynamic-slice_fusion
  114.3 1.3 copy.15
  116.3 7.4 %all-gather.18.cloned.1.call-done = bf16[288,2304]{1,0:T(8,128)(2,1)} async-done(((bf16[144,2304]{1,0:T(8,128)(2,1)}), bf16[288,2304]{1,0:T(8,128)(2,1)}) %all-gather.18.cloned.1.call-update) | async-done | bytes 1327120 | tf_op jit(solution)/shard_map/all_gather | solution.py:45
  123.7 4.8 fusion.3
  128.6 2.3 all_gather.30
  130.9 130.5 %all-gather.12.cloned.1.call-done = f32[1152,2304]{0,1:T(8,128)} async-done(((f32[1152,144]{0,1:T(8,128)}), f32[1152,2304]{0,1:T(8,128)}) %all-gather.12.cloned.1.call-update) | async-done | bytes 10616848 | tf_op jit(solution)/shard_map/all_gather | solution.py:69
  261.4 6.1 multiply_add_fusion
  267.5 1.4 copy-done
  268.9 6.4 convolution_bitcast_fusion
  275.6 8.7 %fusion.20 = f32[144,1152]{1,0:T(8,128)} fusion(f32[2304,144]{0,1:T(8,128)} %all-gather.10.cloned.1.call-done, f32[1152,2304]{0,1:T(8,128)} %all-gather.12.cloned.1.call-done), kind=kOutput, calls=%fused_computation.28 | convolution fusion | flops 2293235712 | bytes 12607488 | tf_op jit(solution)/shard_map/dot_general | solution.py:23
  284.3 137.5 %all-gather.14.cloned.1.call-done = f32[1152,2304]{0,1:T(8,128)} async-done(((f32[1152,144]{0,1:T(8,128)}), f32[1152,2304]{0,1:T(8,128)}) %all-gather.14.cloned.1.call-update) | async-done | bytes 10616848 | tf_op jit(solution)/shard_map/all_gather | solution.py:76
  421.9 7.6 %multiply_reduce_fusion = f32[]{:T(128)} fusion(f32[1152,2304]{0,1:T(8,128)} %all-gather.14.cloned.1.call-done), kind=kLoop, calls=%fused_computation | loop fusion | flops 5308415 | bytes 10616836 | tf_op jit(solution)/shard_map/reduce_sum | solution.py:79
  429.4 4.5 fusion.21
  433.9 1.9 concatenate.3
  436.2 18.2 %all-reduce.4.cloned.1.call-done = f32[2312,144]{0,1:T(8,128)} async-done(((f32[2312,144]{0,1:T(8,128)}), f32[2312,144]{0,1:T(8,128)}) %all-reduce.4.cloned.1.call-update) | async-done | bytes 1331728 | tf_op jit(solution)/shard_map/psum | solution.py:80
  456.3 8.2 %fusion = f32[1152,144]{0,1:T(8,128)} fusion(f32[1152,2304]{0,1:T(8,128)} %all-gather.14.cloned.1.call-done, f32[2312,144]{0,1:T(8,128)} %all-reduce.4.cloned.1.call-done, f32[]{:T(128)S(6)} %mul.101, f32[]{:T(128)S(6)} %mul.96, f32[144,1152]{1,0:T(8,128)S(1)} %copy-done.3), kind=kOutput, calls=%fused_computation.5 | convolution fusion | flops 2293733376 | bytes 13271048 | tf_op jit(solution)/shard_map/dot_general | solution.py:23
  464.6 134.8 %all-gather.16.cloned.1.call-done = f32[1152,2304]{0,1:T(8,128)} async-done(((f32[1152,144]{0,1:T(8,128)}), f32[1152,2304]{0,1:T(8,128)}) %all-gather.16.cloned.1.call-update) | async-done | bytes 10616848 | tf_op jit(solution)/shard_map/all_gather | solution.py:51
  599.4 9.6 %fusion.22 = f32[2304,144]{0,1:T(8,128)} fusion(f32[1152,2304]{0,1:T(8,128)} %all-gather.16.cloned.1.call-done, f32[1152,144]{0,1:T(8,128)} %fusion), kind=kOutput, calls=%fused_computation.30 | convolution fusion | flops 2293235712 | bytes 12607488 | tf_op jit(solution)/shard_map/dot_general | solution.py:27
  609.0 18.4 %all-reduce.6.cloned.1.call-done = f32[2304,144]{0,1:T(8,128)} async-done(((f32[2304,144]{0,1:T(8,128)}), f32[2304,144]{0,1:T(8,128)}) %all-reduce.6.cloned.1.call-update) | async-done | bytes 1327120 | tf_op jit(solution)/shard_map/psum | solution.py:52
  627.4 8.2 %fusion.1 = f32[1152,144]{0,1:T(8,128)} fusion(f32[1152,2304]{0,1:T(8,128)} %all-gather.16.cloned.1.call-done, f32[2304,144]{0,1:T(8,128)} %all-reduce.6.cloned.1.call-done, f32[1152,144]{0,1:T(8,128)S(1)} %copy-done.2), kind=kOutput, calls=%fused_computation.6 | convolution fusion | flops 2293733376 | bytes 13271040 | tf_op jit(solution)/shard_map/dot_general | solution.py:23
  (40 shorter events, 2.8 us)
Async XLA Ops:
  7.2 14.5 %reduce-scatter.7.cloned.1.call-start = ((), (), s32[]{:S(2)}) async-start(), calls=%async_computation.11 | async-start | bytes 1769472
  9.5 102.8 %all-gather.8.cloned.1.call-start = ((), (), s32[]{:S(2)}) async-start(), calls=%async_computation.2 | async-start | bytes 5640192 | tf_op jit(solution)/shard_map/all_gather | solution.py:63
  23.7 100.0 %all-gather.18.cloned.1.call-start = ((), (), s32[]{:S(2)}) async-start(), calls=%async_computation.10 | async-start | bytes 1990656 | tf_op jit(solution)/shard_map/all_gather | solution.py:45
  114.3 14.2 %copy-start.6 = (bf16[144,1152]{1,0:T(8,128)(2,1)S(1)}, bf16[144,1152]{1,0:T(8,128)(2,1)}, u32[]{:S(2)}) copy-start(bf16[144,1152]{1,0:T(8,128)(2,1)} %copy.14) | copy-start | bytes 995332
  115.6 145.8 %copy-start.7 = (f32[1152,144]{0,1:T(8,128)S(1)}, f32[1152,144]{0,1:T(8,128)}, u32[]{:S(2)}) copy-start(f32[1152,144]{0,1:T(8,128)} %param.6) | copy-start | bytes 1990660
  115.6 145.8 %copy-start.8 = (f32[1152,144]{0,1:T(8,128)S(1)}, f32[1152,144]{0,1:T(8,128)}, u32[]{:S(2)}) copy-start(f32[1152,144]{0,1:T(8,128)} %param.7) | copy-start | bytes 1990660
  115.6 145.8 %all-gather.12.cloned.1.call-start = ((), (), s32[]{:S(2)}) async-start(), calls=%async_computation.4 | async-start | bytes 11280384 | tf_op jit(solution)/shard_map/all_gather | solution.py:69
  116.2 159.4 %all-gather.10.cloned.1.call-start = ((), (), s32[]{:S(2)}) async-start(), calls=%async_computation.3 | async-start | bytes 1990656 | tf_op jit(solution)/shard_map/all_gather | solution.py:75
  128.5 155.8 %reduce-scatter.5.cloned.1.call-start = ((), (), s32[]{:S(2)}) async-start(), calls=%async_computation.6 | async-start | bytes 1990656 | tf_op jit(solution)/shard_map/reduce_scatter | solution.py:74
  261.4 7.6 %copy-start = (f32[1152,2304]{0,1:T(8,128)S(1)}, f32[1152,2304]{0,1:T(8,128)}, u32[]{:S(2)}) copy-start(f32[1152,2304]{0,1:T(8,128)} %all-gather.12.cloned.1.call-done) | copy-start | bytes 31850500
  267.5 7.8 %copy-start.4 = (f32[1152,144]{0,1:T(8,128)}, f32[1152,144]{0,1:T(8,128)S(1)}, u32[]{:S(2)}) copy-start(f32[1152,144]{0,1:T(8,128)S(1)} %get-tuple-element.9) | copy-start | bytes 1990660
  267.5 7.8 %copy-start.5 = (f32[1152,144]{0,1:T(8,128)}, f32[1152,144]{0,1:T(8,128)S(1)}, u32[]{:S(2)}) copy-start(f32[1152,144]{0,1:T(8,128)S(1)} %get-tuple-element.10) | copy-start | bytes 1990660
  275.3 146.6 %all-gather.14.cloned.1.call-start = ((), (), s32[]{:S(2)}) async-start(), calls=%async_computation.5 | async-start | bytes 11280384 | tf_op jit(solution)/shard_map/all_gather | solution.py:76
  284.2 145.2 %copy-start.3 = (f32[144,1152]{1,0:T(8,128)S(1)}, f32[144,1152]{1,0:T(8,128)}, u32[]{:S(2)}) copy-start(f32[144,1152]{1,0:T(8,128)} %fusion.20) | copy-start | bytes 1990660
  284.2 170.2 %all-reduce.4.cloned.1.call-start = ((), (), s32[]{:S(2)}) async-start(), calls=%async_computation.7 | async-start | bytes 2801664 | tf_op jit(solution)/shard_map/psum | solution.py:80
  421.9 7.6 %copy-start.1 = (f32[1152,2304]{0,1:T(8,128)S(1)}, f32[1152,2304]{0,1:T(8,128)}, u32[]{:S(2)}) copy-start(f32[1152,2304]{0,1:T(8,128)} %all-gather.14.cloned.1.call-done) | copy-start | bytes 31850500
  435.9 163.5 %all-gather.16.cloned.1.call-start = ((), (), s32[]{:S(2)}) async-start(), calls=%async_computation.8 | async-start | bytes 11280384 | tf_op jit(solution)/shard_map/all_gather | solution.py:51
  464.6 162.8 %copy-start.2 = (f32[1152,144]{0,1:T(8,128)S(1)}, f32[1152,144]{0,1:T(8,128)}, u32[]{:S(2)}) copy-start(f32[1152,144]{0,1:T(8,128)} %fusion) | copy-start | bytes 1990660
  464.6 162.8 %all-reduce.6.cloned.1.call-start = ((), (), s32[]{:S(2)}) async-start(), calls=%async_computation.9 | async-start | bytes 2654208 | tf_op jit(solution)/shard_map/psum | solution.py:52
Sparse Core Ops, SparseCore 0:
  10.2 11.3 reduce-scatter.6
  25.4 86.8 all-gather.7
  115.7 7.9 all-gather.17
  126.7 134.6 all-gather.11
  263.4 7.6 all-gather.9
  275.4 8.3 reduce-scatter.4
  287.2 134.6 all-gather.13
  436.0 18.3 all-reduce.3
  464.7 134.6 all-gather.15
  609.1 18.1 all-reduce.5

commit v3 on v2

--- a/solution.py
+++ b/solution.py
@@ -17,6 +17,7 @@
 norm_eps = 1e-06
 
 TS = ("tensor", "section")
+PAD = 8
 
 
 def exact_dot(left, right):
@@ -37,47 +38,87 @@
     rows = D // n_shard
     cols = D // n_ts
     assert rows % cols == 0 or cols % rows == 0
+    pair = n_shard == 2
 
-    def block_rows(grad_rows, k):
+    def partner(x):
+        return lax.ppermute(x, "shard", [(0, 1), (1, 0)])
+
+    def shard_concat(x, c):
+        if not pair:
+            return lax.all_gather(x, "shard", axis=0, tiled=True)
+        other = partner(x)
+        first = jnp.where(c == 0, x, other)
+        last = jnp.where(c == 0, other, x)
+        return jnp.concatenate([first, last], axis=0)
+
+    def shard_sum(x):
+        if not pair:
+            return lax.psum(x, "shard")
+        return x + partner(x)
+
+    def shard_sum_scatter(x, c, axis):
+        if not pair:
+            return lax.psum_scatter(x, "shard", scatter_dimension=axis, tiled=True)
+        size = x.shape[axis] // 2
+        mine = lax.dynamic_slice_in_dim(x, c * size, size, axis=axis)
+        theirs = lax.dynamic_slice_in_dim(x, (1 - c) * size, size, axis=axis)
+        return mine + partner(theirs)
+
+    def block_rows(grad_rows, k, c):
         start = k * cols
         if cols <= rows:
             piece = lax.dynamic_slice_in_dim(grad_rows, start % rows, cols, axis=0)
+            owner = start // rows
+            if pair:
+                return jnp.where(owner == c, piece, partner(piece))
             pieces = lax.all_gather(piece, "shard", axis=0, tiled=False)
-            return lax.dynamic_index_in_dim(pieces, start // rows, axis=0, keepdims=False)
+            return lax.dynamic_index_in_dim(pieces, owner, axis=0, keepdims=False)
         full = lax.all_gather(grad_rows, "shard", axis=0, tiled=True)
         return lax.dynamic_slice_in_dim(full, start, cols, axis=0)
 
+    def gather_rows(block, extra):
+        padded = jnp.concatenate([block, jnp.full((PAD, cols), extra, jnp.float32)], axis=0)
+        gathered = lax.all_gather(padded, TS, axis=1, tiled=True)
+        return gathered[:rows], gathered[rows, ::cols]
+
     def newton_step(iterate):
         iterate_rows = lax.all_gather(iterate, TS, axis=1, tiled=True)
-        z_cols = lax.psum(contract_rows(iterate_rows, iterate), "shard")
+        z_cols = shard_sum(contract_rows(iterate_rows, iterate))
         return 1.5 * iterate - 0.5 * exact_dot(iterate_rows, z_cols)
 
     def shards(grad_parts, moment, second, stat_left, basis_left):
+        c = lax.axis_index("shard")
         k = lax.axis_index("tensor") * n_section + lax.axis_index("section")
-        partial_value = grad_parts[0].astype(jnp.float32)
-        grad_flip = lax.psum_scatter(
-            partial_value.astype(jnp.bfloat16), "shard", scatter_dimension=1, tiled=True
-        )
+        part = grad_parts[0]
+        if pair:
+            mine = lax.dynamic_slice_in_dim(part, c * rows, rows, axis=1)
+            theirs = lax.dynamic_slice_in_dim(part, (1 - c) * rows, rows, axis=1)
+            grad_flip = (mine.astype(jnp.float32) + partner(theirs).astype(jnp.float32)).astype(jnp.bfloat16)
+        else:
+            grad_flip = lax.psum_scatter(
+                part.astype(jnp.float32).astype(jnp.bfloat16), "shard", scatter_dimension=1, tiled=True
+            )
         grad = grad_flip.T
-        grad_cols = lax.all_gather(grad, "shard", axis=0, tiled=True)
+        grad_cols = shard_concat(grad, c)
         grad_rows = lax.all_gather(grad, TS, axis=1, tiled=True)
-        grad_krows = block_rows(grad_rows, k)
+        grad_krows = block_rows(grad_rows, k, c)
         gram = lax.dot_general(
             grad_rows, grad_krows, (((1,), (1,)), ((), ())), preferred_element_type=jnp.float32
         )
         stat_next = stat_decay * stat_left + (1.0 - stat_decay) / D * gram
         basis_rows = lax.all_gather(basis_left, TS, axis=1, tiled=True)
-        rotated = exact_dot(basis_rows, grad_cols.astype(jnp.float32))
+        power = exact_dot(basis_rows, shard_concat(stat_next, c))
+        power, basis_later = lax.optimization_barrier((power, basis_rows))
+        rotated = exact_dot(basis_later, grad_cols.astype(jnp.float32))
         moment_next = beta_one * moment + (1.0 - beta_one) * rotated
         second_next = beta_two * second + (1.0 - beta_two) * rotated * rotated
         ratio = moment_next / first_fix / (jnp.sqrt(second_next / second_fix) + adam_eps)
-        update = lax.psum_scatter(contract_rows(basis_rows, ratio), "shard", scatter_dimension=0, tiled=True)
-        power = exact_dot(basis_rows, lax.all_gather(stat_next, "shard", axis=0, tiled=True))
-        power_rows = lax.all_gather(power, TS, axis=1, tiled=True)
+        update = shard_sum_scatter(contract_rows(basis_later, ratio), c, 0)
+        power_rows, block_sq = gather_rows(power, jnp.sum(power * power))
         power_rows, update = lax.optimization_barrier((power_rows, update))
         z_part = contract_rows(power_rows, power)
-        sq_part = jnp.full((8, cols), jnp.sum(power_rows * power_rows), jnp.float32)
-        summed = lax.psum(jnp.concatenate([z_part, sq_part], axis=0), "shard")
+        sq_part = jnp.full((PAD, cols), jnp.sum(block_sq), jnp.float32)
+        summed = shard_sum(jnp.concatenate([z_part, sq_part], axis=0))
         total_sq = summed[D, 0]
         scale = shrink * jnp.sqrt(D / (total_sq + norm_eps))
         iterate = (1.5 * scale) * power - (0.5 * scale * scale * scale) * exact_dot(power_rows, summed[:D])

time: 643 us -> 572 us (0.89)
  waiting for transfers between devices: 548 us -> 483 us
  matrix products: 56.4 us -> 48 us
  local copies, waits for them, and re-layouts: 12.2 us -> 19.1 us
    psum x2 -> x0, waiting for transfers between devices: 36.6 us -> none  [the longest x1 18.4 us: newton_step(): z_cols = lax.psum(contract_rows(iterate_rows, iterate), 'shard')]
    all_gather x3 -> x1, waiting for transfers between devices: 145 us -> 124 us  [gather_rows(): gathered = lax.all_gather(padded, TS, axis=1, tiled=True)]
    ppermute x0 -> x7, waiting for transfers between devices: none -> 15.2 us  [partner(): return lax.ppermute(x, 'shard', [(0, 1), (1, 0)])]
    unnamed x11 -> x4, waiting for transfers between devices: 12.7 us -> 0.74 us
    all_gather x1, waiting for transfers between devices: 131 us -> 123 us  [shards(): basis_rows = lax.all_gather(basis_left, TS, axis=1, tiled=True)]
  transfers between devices with their start and end apart: 10 -> 11, of which waited for: 8 -> 11; matrix products, arithmetic and copies ran while one was open for 4% -> 3% of each run, Pallas kernels for 0% -> 0%
where the time goes in v3:
time: 572 us
  waiting for transfers between devices  483 us (84%)
  matrix products  48 us (8%)
  local copies, waits for them, and re-layouts  19.1 us (3%)
  between operations  14.8 us (3%)
    all_gather x1, waiting for transfers between devices, newton_step(): iterate_rows = lax.all_gather(iterate, TS, axis=1, tiled=True)  132 us
    all_gather x1, waiting for transfers between devices, gather_rows(): gathered = lax.all_gather(padded, TS, axis=1, tiled=True)  124 us
    all_gather x1, waiting for transfers between devices, shards(): basis_rows = lax.all_gather(basis_left, TS, axis=1, tiled=True)  123 us
    all_gather x1, waiting for transfers between devices, shards(): grad_rows = lax.all_gather(grad, TS, axis=1, tiled=True)  87.7 us
    dot_general x4, matrix products, exact_dot(): jnp.dot(left, right, precision=lax.Precision.HIGH, preferred_element_type...  25.9 us
    dot_general x3, matrix products, contract_rows(): lax.dot_general(left, right, (((0,), (0,)), ((), ())), precision=lax.Prec...  18.3 us
    ppermute x7, waiting for transfers between devices, partner(): return lax.ppermute(x, 'shard', [(0, 1), (1, 0)])  15.2 us
  transfers between devices with their start and end apart: 11, of which 11 were waited for; matrix products, arithmetic and copies ran while one was open for 3% of the time, Pallas kernels for 0%

profile of v3, /device:TPU:0, one launch (start us, length us, event | category | flops | bytes accessed | tf_op | source)
XLA Modules:
  0.0 571.6 jit_solution(4249538830481590003)
XLA Ops:
  10.0 1.8 fusion.21
  12.6 87.7 %all-gather.5.cloned.1.call-done = bf16[1152,2304]{0,1:T(8,128)(2,1)} async-done(((bf16[1152,144]{0,1:T(8,128)(2,1)}), bf16[1152,2304]{0,1:T(8,128)(2,1)}) %all-gather.5.cloned.1.call-update) | async-done | bytes 5308432 | tf_op jit(solution)/shard_map/all_gather | solution.py:103
  100.3 2.0 constant_dynamic-slice_fusion.1
  103.0 2.1 collective-permute-done.1
  105.7 3.8 fusion
  109.7 2.0 collective-permute-done.2
  111.7 123.3 %all-gather.7.cloned.1.call-done = f32[1152,2304]{0,1:T(8,128)} async-done(((f32[1152,144]{0,1:T(8,128)}), f32[1152,2304]{0,1:T(8,128)}) %all-gather.7.cloned.1.call-update) | async-done | bytes 10616848 | tf_op jit(solution)/shard_map/all_gather | solution.py:109
  235.1 7.4 %convolution_bitcast_fusion = f32[1152,144]{0,1:T(8,128)S(1)} fusion(f32[1152,2304]{0,1:T(8,128)} %all-gather.7.cloned.1.call-done, f32[1152,144]{0,1:T(8,128)S(1)} %get-tuple-element.14, f32[1152,144]{0,1:T(8,128)S(1)} %get-tuple-element.13), kind=kOutput, calls=%fused_computation.5 | convolution fusion | flops 2293567488 | bytes 12607488 | tf_op jit(solution)/shard_map/dot_general | solution.py:24
  243.3 1.7 concatenate.13
  245.3 1.6 collective-permute-done.3
  247.0 6.2 %multiply_add_fusion = (f32[1152,144]{0,1:T(8,128)S(1)}, f32[1152,144]{0,1:T(8,128)S(1)}) fusion(f32[1152,144]{0,1:T(8,128)S(1)} %copy-done.6, f32[1152,144]{0,1:T(8,128)S(1)} %copy-done.7, f32[1152,2304]{0,1:T(8,128)} %all-gather.7.cloned.1.call-done, bf16[1152,144]{0,1:T(8,128)(2,1)S(1)} %get-tuple-element.18, bf16[1152,144]{0,1:T(8,128)(2,1)S(1)} %get-tuple-element.17), kind=kOutput, calls=%fused_computation.29 | convolution fusion | flops 2295724032 | bytes 13934592 | tf_op jit(solution)/shard_map/dot_general | solution.py:24
  255.3 5.0 fusion.15
  260.6 2.0 collective-permute-done.4
  263.5 124.3 %all-gather.9.cloned.1.call-done = f32[1160,2304]{0,1:T(8,128)} async-done(((f32[1160,144]{0,1:T(8,128)}), f32[1160,2304]{0,1:T(8,128)}) %all-gather.9.cloned.1.call-update) | async-done | bytes 10690576 | tf_op jit(solution)/shard_map/all_gather | solution.py:81
  387.9 4.7 slice.16
  392.6 3.9 copy-done
  396.5 4.6 fusion.32
  401.2 1.3 slice.13
  403.9 3.2 collective-permute-done.5
  409.1 8.0 %fusion.1 = f32[1152,144]{0,1:T(8,128)} fusion(f32[1152,2304]{0,1:T(8,128)} %copy-done, f32[2312,144]{0,1:T(8,128)S(1)} %pad_add_fusion, f32[1152,144]{0,1:T(8,128)S(1)} %convolution_bitcast_fusion, f32[]{:T(128)S(6)} %mul.107, f32[]{:T(128)S(6)} %mul.102), kind=kOutput, calls=%fused_computation.4 | convolution fusion | flops 2293733376 | bytes 13271048 | tf_op jit(solution)/shard_map/dot_general | solution.py:24
  417.1 131.8 %all-gather.11.cloned.1.call-done = f32[1152,2304]{0,1:T(8,128)} async-done(((f32[1152,144]{0,1:T(8,128)}), f32[1152,2304]{0,1:T(8,128)}) %all-gather.11.cloned.1.call-update) | async-done | bytes 10616848 | tf_op jit(solution)/shard_map/all_gather | solution.py:85
  548.9 8.6 %fusion.33 = f32[2304,144]{0,1:T(8,128)S(1)} fusion(f32[1152,2304]{0,1:T(8,128)} %all-gather.11.cloned.1.call-done, f32[1152,144]{0,1:T(8,128)} %fusion.1), kind=kOutput, calls=%fused_computation.49 | convolution fusion | flops 2293235712 | bytes 12607488 | tf_op jit(solution)/shard_map/dot_general | solution.py:28
  557.6 3.0 collective-permute-done.6
  560.7 4.3 multiply_subtract_fusion
  (52 shorter events, 12.4 us)
Async XLA Ops:
  7.2 93.1 %all-gather.5.cloned.1.call-start = ((), (), s32[]{:S(2)}) async-start(), calls=%async_computation | async-start | bytes 5640192 | tf_op jit(solution)/shard_map/all_gather | solution.py:103
  8.2 1.8 collective-permute-start
  11.8 223.2 %all-gather.7.cloned.1.call-start = ((), (), s32[]{:S(2)}) async-start(), calls=%async_computation.1 | async-start | bytes 11280384 | tf_op jit(solution)/shard_map/all_gather | solution.py:109
  12.6 375.3 %all-gather.9.cloned.1.call-start = ((), (), s32[]{:S(2)}) async-start(), calls=%async_computation.2 | async-start | bytes 12533760 | tf_op jit(solution)/shard_map/all_gather | solution.py:81
  102.9 2.2 collective-permute-start.1
  109.4 133.0 %copy-start.8 = (f32[1152,144]{0,1:T(8,128)}, f32[1152,144]{0,1:T(8,128)S(1)}, u32[]{:S(2)}) copy-start(f32[1152,144]{0,1:T(8,128)S(1)} %fusion) | copy-start | bytes 1990660
  109.5 2.2 collective-permute-start.2
  242.5 2.7 copy-start.5
  243.3 3.8 copy-start.6
  243.3 3.8 copy-start.7
  245.0 304.0 %all-gather.11.cloned.1.call-start = ((), (), s32[]{:S(2)}) async-start(), calls=%async_computation.3 | async-start | bytes 11280384 | tf_op jit(solution)/shard_map/all_gather | solution.py:85
  245.2 1.7 collective-permute-start.3
  247.0 6.3 %slice-start = ((s8[10616832]{0:T(1024)(128)(4,1)}), s8[4194304]{0:T(1024)(128)(4,1)S(1)}, s32[]{:S(2)}) async-start(s8[10616832]{0:T(1024)(128)(4,1)} %bitcast.20), calls=%async_computation.4 | async-start | bytes 8388608
  247.0 7.2 %slice-start.1 = ((s8[10616832]{0:T(1024)(128)(4,1)}), s8[4194304]{0:T(1024)(128)(4,1)S(1)}, s32[]{:S(2)}) async-start(s8[10616832]{0:T(1024)(128)(4,1)} %bitcast.20), calls=%async_computation.5 | async-start | bytes 8388608
  247.0 8.3 %slice-start.2 = ((s8[10616832]{0:T(1024)(128)(4,1)}), s8[2228224]{0:T(1024)(128)(4,1)S(1)}, s32[]{:S(2)}) async-start(s8[10616832]{0:T(1024)(128)(4,1)} %bitcast.20), calls=%async_computation.6 | async-start | bytes 4456448
  253.3 7.1 %copy-start.3 = (f32[1152,144]{0,1:T(8,128)}, f32[1152,144]{0,1:T(8,128)S(1)}, u32[]{:S(2)}) copy-start(f32[1152,144]{0,1:T(8,128)S(1)} %get-tuple-element.15) | copy-start | bytes 1990660
  253.3 7.1 %copy-start.4 = (f32[1152,144]{0,1:T(8,128)}, f32[1152,144]{0,1:T(8,128)S(1)}, u32[]{:S(2)}) copy-start(f32[1152,144]{0,1:T(8,128)S(1)} %get-tuple-element.16) | copy-start | bytes 1990660
  260.4 2.2 collective-permute-start.4
  392.6 3.9 copy-start
  403.8 3.2 collective-permute-start.5
  417.1 143.6 %copy-start.2 = (f32[1152,144]{0,1:T(8,128)S(1)}, f32[1152,144]{0,1:T(8,128)}, u32[]{:S(2)}) copy-start(f32[1152,144]{0,1:T(8,128)} %fusion.1) | copy-start | bytes 1990660
  548.9 11.8 %copy-start.1 = (f32[1152,2304]{0,1:T(8,128)S(1)}, f32[1152,2304]{0,1:T(8,128)}, u32[]{:S(2)}) copy-start(f32[1152,2304]{0,1:T(8,128)} %all-gather.11.cloned.1.call-done) | copy-start | bytes 31850500
  557.6 3.1 collective-permute-start.6
Sparse Core Ops, SparseCore 0:
  11.9 88.3 all-gather.4
  103.1 131.9 all-gather.6
  245.1 142.7 all-gather.8
  417.2 131.6 all-gather.10

commit v4 on v3

--- a/solution.py
+++ b/solution.py
@@ -76,10 +76,16 @@
         full = lax.all_gather(grad_rows, "shard", axis=0, tiled=True)
         return lax.dynamic_slice_in_dim(full, start, cols, axis=0)
 
-    def gather_rows(block, extra):
-        padded = jnp.concatenate([block, jnp.full((PAD, cols), extra, jnp.float32)], axis=0)
-        gathered = lax.all_gather(padded, TS, axis=1, tiled=True)
-        return gathered[:rows], gathered[rows, ::cols]
+    def all_sum(value):
+        x = jnp.full((PAD, 128), value, jnp.float32)
+        if n_ts & (n_ts - 1) == 0:
+            step = 1
+            while step < n_ts:
+                x = x + lax.ppermute(x, TS, [(i, i ^ step) for i in range(n_ts)])
+                step *= 2
+        else:
+            x = lax.psum(x, TS)
+        return shard_sum(x)[0, 0]
 
     def newton_step(iterate):
         iterate_rows = lax.all_gather(iterate, TS, axis=1, tiled=True)
@@ -100,13 +106,17 @@
             )
         grad = grad_flip.T
         grad_cols = shard_concat(grad, c)
-        grad_rows = lax.all_gather(grad, TS, axis=1, tiled=True)
+        basis_top = lax.reduce_precision(basis_left, exponent_bits=8, mantissa_bits=7)
+        basis_hi = basis_top.astype(jnp.bfloat16)
+        basis_lo = (basis_left - basis_top).astype(jnp.bfloat16)
+        stacked = lax.all_gather(jnp.stack([grad, basis_hi, basis_lo]), TS, axis=2, tiled=True)
+        grad_rows = stacked[0]
+        basis_rows = stacked[1].astype(jnp.float32) + stacked[2].astype(jnp.float32)
         grad_krows = block_rows(grad_rows, k, c)
         gram = lax.dot_general(
             grad_rows, grad_krows, (((1,), (1,)), ((), ())), preferred_element_type=jnp.float32
         )
         stat_next = stat_decay * stat_left + (1.0 - stat_decay) / D * gram
-        basis_rows = lax.all_gather(basis_left, TS, axis=1, tiled=True)
         power = exact_dot(basis_rows, shard_concat(stat_next, c))
         power, basis_later = lax.optimization_barrier((power, basis_rows))
         rotated = exact_dot(basis_later, grad_cols.astype(jnp.float32))
@@ -114,14 +124,12 @@
         second_next = beta_two * second + (1.0 - beta_two) * rotated * rotated
         ratio = moment_next / first_fix / (jnp.sqrt(second_next / second_fix) + adam_eps)
         update = shard_sum_scatter(contract_rows(basis_later, ratio), c, 0)
-        power_rows, block_sq = gather_rows(power, jnp.sum(power * power))
+        power_rows = lax.all_gather(power, TS, axis=1, tiled=True)
+        total_sq = all_sum(jnp.sum(power * power))
         power_rows, update = lax.optimization_barrier((power_rows, update))
-        z_part = contract_rows(power_rows, power)
-        sq_part = jnp.full((PAD, cols), jnp.sum(block_sq), jnp.float32)
-        summed = shard_sum(jnp.concatenate([z_part, sq_part], axis=0))
-        total_sq = summed[D, 0]
+        z_cols = shard_sum(contract_rows(power_rows, power))
         scale = shrink * jnp.sqrt(D / (total_sq + norm_eps))
-        iterate = (1.5 * scale) * power - (0.5 * scale * scale * scale) * exact_dot(power_rows, summed[:D])
+        iterate = (1.5 * scale) * power - (0.5 * scale * scale * scale) * exact_dot(power_rows, z_cols)
         for turn in range(NS_ITERS - 1):
             iterate = newton_step(iterate)
         return (update, moment_next, second_next, stat_next, iterate)

time: 572 us -> 550 us (0.962)
  waiting for transfers between devices: 483 us -> 452 us
  local copies, waits for them, and re-layouts: 19.1 us -> 7.9 us
  other arithmetic: 5.08 us -> 15.6 us
    all_gather x3 -> x2, waiting for transfers between devices: 335 us -> 300 us  [the longest x1 186 us: shards(): lax.all_gather(jnp.stack([grad, basis_hi, basis_lo]), TS, axis=2, tiled=T...]
    ppermute x0 -> x4, waiting for transfers between devices: none -> 10.9 us  [all_sum(): x = x + lax.ppermute(x, TS, [(i, i ^ step) for i in range(n_ts)])]
    add x0 -> x5, other arithmetic: none -> 10.5 us  [the longest x1 9.15 us: shards(): basis_rows = stacked[1].astype(jnp.float32) + stacked[2].astype(jnp.float32)]
    ppermute x7 -> x8, waiting for transfers between devices: 15.2 us -> 9.43 us  [partner(): return lax.ppermute(x, 'shard', [(0, 1), (1, 0)])]
  transfers between devices with their start and end apart: 11 -> 15, of which waited for: 11 -> 13; matrix products, arithmetic and copies ran while one was open for 3% -> 5% of each run, Pallas kernels for 0% -> 0%
where the time goes in v4:
time: 550 us
  waiting for transfers between devices  452 us (82%)
  matrix products  53.2 us (10%)
  other arithmetic  15.6 us (3%)
  between operations  14.8 us (3%)
  local copies, waits for them, and re-layouts  7.9 us (1%)
  starting transfers between devices  6.71 us (1%)
    all_gather x1, waiting for transfers between devices, shards(): lax.all_gather(jnp.stack([grad, basis_hi, basis_lo]), TS, axis=2, tiled=T...  186 us
    all_gather x1, waiting for transfers between devices, newton_step(): iterate_rows = lax.all_gather(iterate, TS, axis=1, tiled=True)  132 us
    all_gather x1, waiting for transfers between devices, shards(): power_rows = lax.all_gather(power, TS, axis=1, tiled=True)  113 us
    dot_general x4, matrix products, exact_dot(): jnp.dot(left, right, precision=lax.Precision.HIGH, preferred_element_type...  27.5 us
    dot_general x3, matrix products, contract_rows(): lax.dot_general(left, right, (((0,), (0,)), ((), ())), precision=lax.Prec...  22.1 us
  transfers between devices with their start and end apart: 15, of which 13 were waited for; matrix products, arithmetic and copies ran while one was open for 5% of the time, Pallas kernels for 0%

profile of v4, /device:TPU:0, one launch (start us, length us, event | category | flops | bytes accessed | tf_op | source)
XLA Modules:
  0.0 550.1 jit_solution(15560462241591011983)
XLA Ops:
  12.3 186.3 %all-gather.4.cloned.1.call-done = bf16[3,1152,2304]{1,2,0:T(8,128)(2,1)} async-done(((bf16[3,1152,144]{1,2,0:T(8,128)(2,1)}), bf16[3,1152,2304]{1,2,0:T(8,128)(2,1)}) %all-gather.4.cloned.1.call-update) | async-done | bytes 15925264 | tf_op jit(solution)/shard_map/all_gather | solution.py:112
  198.6 2.5 slice-done.3
  202.3 2.1 collective-permute-done.1
  204.4 3.6 fusion.5
  208.3 9.2 %add_bitcast_fusion = f32[1152,2304]{0,1:T(8,128)} fusion(bf16[3,1152,2304]{1,2,0:T(8,128)(2,1)} %all-gather.4.cloned.1.call-done), kind=kLoop, calls=%fused_computation | loop fusion | flops 7962624 | bytes 21233664 | tf_op jit(solution)/shard_map/add | solution.py:114
  217.6 8.9 %fusion.9 = f32[1152,144]{0,1:T(8,128)} fusion(f32[1152,144]{0,1:T(8,128)S(1)} %get-tuple-element.14, f32[1152,144]{0,1:T(8,128)S(1)} %get-tuple-element.13, bf16[3,1152,2304]{1,2,0:T(8,128)(2,1)} %all-gather.4.cloned.1.call-done), kind=kOutput, calls=%fused_computation.8 | convolution fusion | flops 2301530112 | bytes 12607488 | tf_op jit(solution)/shard_map/dot_general | solution.py:24
  227.2 1.3 collective-permute-done.3
  228.6 6.2 %multiply_add_fusion = (f32[1152,144]{0,1:T(8,128)S(1)}, f32[1152,144]{0,1:T(8,128)S(1)}) fusion(f32[1152,144]{0,1:T(8,128)S(1)} %copy-done.5, f32[1152,144]{0,1:T(8,128)S(1)} %copy-done.6, f32[1152,2304]{0,1:T(8,128)} %add_bitcast_fusion, bf16[1152,144]{0,1:T(8,128)(2,1)S(1)} %get-tuple-element.20, bf16[1152,144]{0,1:T(8,128)(2,1)S(1)} %get-tuple-element.19), kind=kOutput, calls=%fused_computation.35 | convolution fusion | flops 2295724032 | bytes 13934592 | tf_op jit(solution)/shard_map/dot_general | solution.py:24
  236.8 5.0 fusion.22
  242.3 1.8 collective-permute-done.4
  245.0 113.3 %all-gather.6.cloned.1.call-done = f32[1152,2304]{0,1:T(8,128)} async-done(((f32[1152,144]{0,1:T(8,128)}), f32[1152,2304]{0,1:T(8,128)}) %all-gather.6.cloned.1.call-update) | async-done | bytes 10616848 | tf_op jit(solution)/shard_map/all_gather | solution.py:127
  358.4 8.4 %fusion.46 = f32[2304,144]{0,1:T(8,128)S(1)} fusion(f32[1152,2304]{0,1:T(8,128)} %all-gather.6.cloned.1.call-done, f32[1152,144]{0,1:T(8,128)S(1)} %copy-done.2), kind=kOutput, calls=%fused_computation.60 | convolution fusion | flops 2293235712 | bytes 12607488 | tf_op jit(solution)/shard_map/dot_general | solution.py:28
  368.4 3.6 collective-permute-done.5
  372.6 1.6 collective-permute-start.6
  374.2 3.0 collective-permute-done.6
  377.8 1.5 collective-permute-start.7
  379.4 2.2 collective-permute-done.7
  381.5 1.5 collective-permute-start.8
  383.0 2.1 collective-permute-done.8
  387.6 8.0 %fusion.8 = f32[1152,144]{0,1:T(8,128)} fusion(f32[1152,2304]{0,1:T(8,128)} %all-gather.6.cloned.1.call-done, f32[2304,144]{0,1:T(8,128)S(1)} %fusion.46, f32[2304,144]{0,1:T(8,128)S(1)} %collective-permute-done.10, f32[1152,144]{0,1:T(8,128)S(1)} %copy-done.2, f32[]{:T(128)S(6)} %mul.107, f32[]{:T(128)S(6)} %mul.102), kind=kOutput, calls=%fused_computation.7 | convolution fusion | flops 2294065152 | bytes 14598152 | tf_op jit(solution)/shard_map/dot_general | solution.py:24
  395.6 131.8 %all-gather.8.cloned.1.call-done = f32[1152,2304]{0,1:T(8,128)} async-done(((f32[1152,144]{0,1:T(8,128)}), f32[1152,2304]{0,1:T(8,128)}) %all-gather.8.cloned.1.call-update) | async-done | bytes 10616848 | tf_op jit(solution)/shard_map/all_gather | solution.py:91
  527.4 8.6 %fusion.47 = f32[2304,144]{0,1:T(8,128)S(1)} fusion(f32[1152,2304]{0,1:T(8,128)} %all-gather.8.cloned.1.call-done, f32[1152,144]{0,1:T(8,128)} %fusion.8), kind=kOutput, calls=%fused_computation.61 | convolution fusion | flops 2293235712 | bytes 12607488 | tf_op jit(solution)/shard_map/dot_general | solution.py:28
  536.2 3.0 collective-permute-done.11
  539.2 4.3 multiply_subtract_fusion
  (63 shorter events, 15.3 us)
Async XLA Ops:
  7.2 191.5 %all-gather.4.cloned.1.call-start = ((), (), s32[]{:S(2)}) async-start(), calls=%async_computation | async-start | bytes 16920576 | tf_op jit(solution)/shard_map/all_gather | solution.py:112
  8.2 1.8 collective-permute-start
  12.2 346.2 %all-gather.6.cloned.1.call-start = ((), (), s32[]{:S(2)}) async-start(), calls=%async_computation.1 | async-start | bytes 11280384 | tf_op jit(solution)/shard_map/all_gather | solution.py:127
  12.3 192.1 %copy-start.8 = (f32[1152,144]{0,1:T(8,128)S(1)}, f32[1152,144]{0,1:T(8,128)}, u32[]{:S(2)}) copy-start(f32[1152,144]{0,1:T(8,128)} %param.8) | copy-start | bytes 1990660
  202.2 2.2 collective-permute-start.1
  208.1 9.4 %copy-start.7 = (f32[1152,144]{0,1:T(8,128)}, f32[1152,144]{0,1:T(8,128)S(1)}, u32[]{:S(2)}) copy-start(f32[1152,144]{0,1:T(8,128)S(1)} %fusion.5) | copy-start | bytes 1990660
  208.1 9.4 %collective-permute-start.2 = (f32[1152,144]{0,1:T(8,128)S(1)}, f32[1152,144]{0,1:T(8,128)S(1)}, u32[]{:S(2)}, u32[]{:S(2)}) collective-permute-start(f32[1152,144]{0,1:T(8,128)S(1)} %fusion.5), channel_id=1, source_target_pairs={{0,16},{16,0},{1,17},{17,1},{2,18},{18,2},{3,19},{19,3},{4,20},{20... | collective-permute-start | bytes 1990664 | tf_op jit(solution)/shard_map/ppermute | solution.py:44
  217.5 11.0 %copy-start.5 = (f32[1152,144]{0,1:T(8,128)S(1)}, f32[1152,144]{0,1:T(8,128)}, u32[]{:S(2)}) copy-start(f32[1152,144]{0,1:T(8,128)} %param.6) | copy-start | bytes 1990660
  217.5 11.0 %copy-start.6 = (f32[1152,144]{0,1:T(8,128)S(1)}, f32[1152,144]{0,1:T(8,128)}, u32[]{:S(2)}) copy-start(f32[1152,144]{0,1:T(8,128)} %param.7) | copy-start | bytes 1990660
  226.5 300.9 %all-gather.8.cloned.1.call-start = ((), (), s32[]{:S(2)}) async-start(), calls=%async_computation.2 | async-start | bytes 11280384 | tf_op jit(solution)/shard_map/all_gather | solution.py:91
  226.8 1.7 collective-permute-start.3
  228.6 7.1 %slice-start.1 = ((s8[10616832]{0:T(1024)(128)(4,1)}), s8[4194304]{0:T(1024)(128)(4,1)S(1)}, s32[]{:S(2)}) async-start(s8[10616832]{0:T(1024)(128)(4,1)} %bitcast.42), calls=%async_computation.4 | async-start | bytes 8388608
  228.6 8.2 %slice-start.2 = ((s8[10616832]{0:T(1024)(128)(4,1)}), s8[2228224]{0:T(1024)(128)(4,1)S(1)}, s32[]{:S(2)}) async-start(s8[10616832]{0:T(1024)(128)(4,1)} %bitcast.42), calls=%async_computation.5 | async-start | bytes 4456448
  236.8 121.5 %copy-start.2 = (f32[1152,144]{0,1:T(8,128)S(1)}, f32[1152,144]{0,1:T(8,128)}, u32[]{:S(2)}) copy-start(f32[1152,144]{0,1:T(8,128)} %fusion.9) | copy-start | bytes 1990660
  241.9 2.2 collective-permute-start.4
  366.8 20.8 %collective-permute-start.10 = (f32[2304,144]{0,1:T(8,128)S(1)}, f32[2304,144]{0,1:T(8,128)S(1)}, u32[]{:S(2)}, u32[]{:S(2)}) collective-permute-start(f32[2304,144]{0,1:T(8,128)S(1)} %fusion.46), channel_id=1, source_target_pairs={{0,16},{16,0},{1,17},{17,1},{2,18},{18,2},{3,19},{19,3},{4,20},{20... | collective-permute-start | bytes 3981320 | tf_op jit(solution)/shard_map/ppermute | solution.py:44
  368.3 3.7 collective-permute-start.5
  372.6 4.6 collective-permute-start.6
  377.8 3.7 collective-permute-start.7
  381.5 3.6 collective-permute-start.8
  385.1 1.2 collective-permute-start.9
  395.6 143.6 %copy-start.1 = (f32[1152,144]{0,1:T(8,128)S(1)}, f32[1152,144]{0,1:T(8,128)}, u32[]{:S(2)}) copy-start(f32[1152,144]{0,1:T(8,128)} %fusion.8) | copy-start | bytes 1990660
  527.4 11.8 %copy-start = (f32[1152,2304]{0,1:T(8,128)S(1)}, f32[1152,2304]{0,1:T(8,128)}, u32[]{:S(2)}) copy-start(f32[1152,2304]{0,1:T(8,128)} %all-gather.8.cloned.1.call-done) | copy-start | bytes 31850500
  536.1 3.1 collective-permute-start.11
  (4 other events, 22.9 us)
Sparse Core Ops, SparseCore 0:
  12.3 186.2 all-gather.3
  226.6 131.6 all-gather.5
  395.7 131.6 all-gather.7

commit v5 on v4

--- a/solution.py
+++ b/solution.py
@@ -32,6 +32,20 @@
         precision=lax.Precision.HIGH,
         preferred_element_type=jnp.float32,
     )
+
+
+def split_bf16(x):
+    top = lax.reduce_precision(x, exponent_bits=8, mantissa_bits=7)
+    return top.astype(jnp.bfloat16), (x - top).astype(jnp.bfloat16)
+
+
+def bf16_dot(left, right, dims):
+    return lax.dot_general(left, right, (dims, ((), ())), preferred_element_type=jnp.float32)
+
+
+def split_dot(left_hi, left_lo, right, dims):
+    right_hi, right_lo = split_bf16(right)
+    return bf16_dot(left_hi, right_hi, dims) + bf16_dot(left_hi, right_lo, dims) + bf16_dot(left_lo, right_hi, dims)
 
 
 def make_shards(n_shard, n_section, n_ts):
@@ -106,27 +120,25 @@
             )
         grad = grad_flip.T
         grad_cols = shard_concat(grad, c)
-        basis_top = lax.reduce_precision(basis_left, exponent_bits=8, mantissa_bits=7)
-        basis_hi = basis_top.astype(jnp.bfloat16)
-        basis_lo = (basis_left - basis_top).astype(jnp.bfloat16)
+        basis_hi, basis_lo = split_bf16(basis_left)
         stacked = lax.all_gather(jnp.stack([grad, basis_hi, basis_lo]), TS, axis=2, tiled=True)
-        grad_rows = stacked[0]
-        basis_rows = stacked[1].astype(jnp.float32) + stacked[2].astype(jnp.float32)
+        grad_rows, hi_rows, lo_rows = stacked[0], stacked[1], stacked[2]
         grad_krows = block_rows(grad_rows, k, c)
         gram = lax.dot_general(
             grad_rows, grad_krows, (((1,), (1,)), ((), ())), preferred_element_type=jnp.float32
         )
         stat_next = stat_decay * stat_left + (1.0 - stat_decay) / D * gram
-        power = exact_dot(basis_rows, shard_concat(stat_next, c))
-        power, basis_later = lax.optimization_barrier((power, basis_rows))
-        rotated = exact_dot(basis_later, grad_cols.astype(jnp.float32))
+        by_rows = ((1,), (0,))
+        power = split_dot(hi_rows, lo_rows, shard_concat(stat_next, c), by_rows)
+        power, hi_later, lo_later = lax.optimization_barrier((power, hi_rows, lo_rows))
+        rotated = bf16_dot(hi_later, grad_cols, by_rows) + bf16_dot(lo_later, grad_cols, by_rows)
         moment_next = beta_one * moment + (1.0 - beta_one) * rotated
         second_next = beta_two * second + (1.0 - beta_two) * rotated * rotated
         ratio = moment_next / first_fix / (jnp.sqrt(second_next / second_fix) + adam_eps)
-        update = shard_sum_scatter(contract_rows(basis_later, ratio), c, 0)
+        update = shard_sum_scatter(split_dot(hi_later, lo_later, ratio, ((0,), (0,))), c, 0)
         power_rows = lax.all_gather(power, TS, axis=1, tiled=True)
         total_sq = all_sum(jnp.sum(power * power))
-        power_rows, update = lax.optimization_barrier((power_rows, update))
+        power_rows, update, total_sq = lax.optimization_barrier((power_rows, update, total_sq))
         z_cols = shard_sum(contract_rows(power_rows, power))
         scale = shrink * jnp.sqrt(D / (total_sq + norm_eps))
         iterate = (1.5 * scale) * power - (0.5 * scale * scale * scale) * exact_dot(power_rows, z_cols)

time: 550 us -> 537 us (0.976)
  waiting for transfers between devices: 452 us -> 436 us
  other arithmetic: 15.6 us -> 6.55 us
  local copies, waits for them, and re-layouts: 7.9 us -> 14.1 us
  matrix products: 53.2 us -> 59 us
    dot_general x0 -> x8, matrix products: none -> 25.7 us  [bf16_dot(): lax.dot_general(left, right, (dims, ((), ())), preferred_element_type=jnp...]
    all_gather x1, waiting for transfers between devices: 113 us -> 94.3 us  [shards(): power_rows = lax.all_gather(power, TS, axis=1, tiled=True)]
    dot_general x4 -> x2, matrix products: 27.5 us -> 12.6 us  [exact_dot(): jnp.dot(left, right, precision=lax.Precision.HIGH, preferred_element_type...]
    squeeze x0 -> x1, local copies, waits for them, and re-layouts: none -> 10.6 us  [shards(): grad_rows, hi_rows, lo_rows = (stacked[0], stacked[1], stacked[2])]
    add x1 -> x0, other arithmetic: 9.15 us -> none  [shards(): basis_rows = stacked[1].astype(jnp.float32) + stacked[2].astype(jnp.float32)]
    dot_general x3 -> x2, matrix products: 22.1 us -> 17.1 us  [contract_rows(): lax.dot_general(left, right, (((0,), (0,)), ((), ())), precision=lax.Prec...]
  transfers between devices with their start and end apart: 15 -> 15, of which waited for: 13 -> 14; matrix products, arithmetic and copies ran while one was open for 5% -> 4% of each run, Pallas kernels for 0% -> 0%
where the time goes in v5:
time: 537 us; the launch traced here: 536 us
  waiting for transfers between devices  436 us (81%)
  matrix products  59 us (11%)
  between operations  14.9 us (3%)
  local copies, waits for them, and re-layouts  14.1 us (3%)
  other arithmetic  6.55 us (1%)
  starting transfers between devices  6.23 us (1%)
    all_gather x1, waiting for transfers between devices, shards(): lax.all_gather(jnp.stack([grad, basis_hi, basis_lo]), TS, axis=2, tiled=T...  186 us
    all_gather x1, waiting for transfers between devices, newton_step(): iterate_rows = lax.all_gather(iterate, TS, axis=1, tiled=True)  132 us
    all_gather x1, waiting for transfers between devices, shards(): power_rows = lax.all_gather(power, TS, axis=1, tiled=True)  94.3 us
    dot_general x8, matrix products, bf16_dot(): lax.dot_general(left, right, (dims, ((), ())), preferred_element_type=jnp...  25.7 us
    dot_general x2, matrix products, contract_rows(): lax.dot_general(left, right, (((0,), (0,)), ((), ())), precision=lax.Prec...  17.1 us
    dot_general x2, matrix products, exact_dot(): jnp.dot(left, right, precision=lax.Precision.HIGH, preferred_element_type...  12.6 us
    ppermute x8, waiting for transfers between devices, partner(): return lax.ppermute(x, 'shard', [(0, 1), (1, 0)])  12.1 us
    ppermute x4, waiting for transfers between devices, all_sum(): x = x + lax.ppermute(x, TS, [(i, i ^ step) for i in range(n_ts)])  11.1 us
  transfers between devices with their start and end apart: 15, of which 14 were waited for; matrix products, arithmetic and copies ran while one was open for 4% of the time, Pallas kernels for 0%

profile of v5, /device:TPU:0, one launch (start us, length us, event | category | flops | bytes accessed | tf_op | source)
XLA Modules:
  0.0 536.4 jit_solution(17518565113262837367)
XLA Ops:
  12.3 186.3 %all-gather.4.cloned.1.call-done = bf16[3,1152,2304]{1,2,0:T(8,128)(2,1)} async-done(((bf16[3,1152,144]{1,2,0:T(8,128)(2,1)}), bf16[3,1152,2304]{1,2,0:T(8,128)(2,1)}) %all-gather.4.cloned.1.call-update) | async-done | bytes 15925264 | tf_op jit(solution)/shard_map/all_gather | solution.py:124
  198.6 10.6 %slice_bitcast_fusion = (bf16[1152,2304]{0,1:T(8,128)(2,1)}, bf16[1,1152,2304]{1,2,0:T(8,128)(2,1)S(1)}, bf16[1152,2304]{0,1:T(8,128)(2,1)}) fusion(bf16[3,1152,2304]{1,2,0:T(8,128)(2,1)} %all-gather.4.cloned.1.call-done), kind=kLoop, calls=%fused_computation | loop fusion | bytes 31850496 | tf_op jit(solution)/shard_map/squeeze | solution.py:125
  210.5 2.1 collective-permute-done.1
  212.5 3.6 fusion.5
  216.4 2.0 collective-permute-done.2
  218.5 3.6 fusion.28
  222.1 3.6 convolution_add_fusion.4
  225.7 4.4 convolution_add_fusion.3
  232.1 3.7 fusion.19
  235.9 4.4 multiply_add_fusion
  242.4 2.0 convolution_add_fusion.1
  244.4 2.0 convolution_add_fusion
  248.2 3.7 collective-permute-done.5
  254.1 3.0 collective-permute-done.6
  259.2 2.2 collective-permute-done.7
  262.9 2.2 collective-permute-done.8
  267.8 94.3 %all-gather.6.cloned.1.call-done = f32[1152,2304]{0,1:T(8,128)} async-done(((f32[1152,144]{0,1:T(8,128)}), f32[1152,2304]{0,1:T(8,128)}) %all-gather.6.cloned.1.call-update) | async-done | bytes 10616848 | tf_op jit(solution)/shard_map/all_gather | solution.py:139
  362.1 8.4 %fusion.36 = f32[2304,144]{0,1:T(8,128)S(1)} fusion(f32[1152,2304]{0,1:T(8,128)} %all-gather.6.cloned.1.call-done, f32[1152,144]{0,1:T(8,128)S(1)} %copy-done.2), kind=kOutput, calls=%fused_computation.61 | convolution fusion | flops 2293235712 | bytes 12607488 | tf_op jit(solution)/shard_map/dot_general | solution.py:28
  371.4 2.3 collective-permute-done.10
  373.6 8.3 %fusion.8 = f32[1152,144]{0,1:T(8,128)} fusion(f32[1152,2304]{0,1:T(8,128)} %all-gather.6.cloned.1.call-done, f32[2304,144]{0,1:T(8,128)S(1)} %fusion.36, f32[2304,144]{0,1:T(8,128)S(1)} %collective-permute-done.10, f32[1152,144]{0,1:T(8,128)S(1)} %copy-done.2, f32[]{:T(128)S(6)} %mul.107, f32[]{:T(128)S(6)} %mul.102), kind=kOutput, calls=%fused_computation.13 | convolution fusion | flops 2294065152 | bytes 14598152 | tf_op jit(solution)/shard_map/dot_general | solution.py:24
  382.0 131.8 %all-gather.8.cloned.1.call-done = f32[1152,2304]{0,1:T(8,128)} async-done(((f32[1152,144]{0,1:T(8,128)}), f32[1152,2304]{0,1:T(8,128)}) %all-gather.8.cloned.1.call-update) | async-done | bytes 10616848 | tf_op jit(solution)/shard_map/all_gather | solution.py:105
  513.8 8.6 %fusion.37 = f32[2304,144]{0,1:T(8,128)S(1)} fusion(f32[1152,2304]{0,1:T(8,128)} %all-gather.8.cloned.1.call-done, f32[1152,144]{0,1:T(8,128)} %fusion.8), kind=kOutput, calls=%fused_computation.62 | convolution fusion | flops 2293235712 | bytes 12607488 | tf_op jit(solution)/shard_map/dot_general | solution.py:28
  522.5 3.0 collective-permute-done.11
  525.5 4.3 multiply_subtract_fusion
  (67 shorter events, 21.0 us)
Async XLA Ops:
  7.2 191.5 %all-gather.4.cloned.1.call-start = ((), (), s32[]{:S(2)}) async-start(), calls=%async_computation | async-start | bytes 16920576 | tf_op jit(solution)/shard_map/all_gather | solution.py:124
  8.2 1.8 collective-permute-start
  12.2 349.9 %all-gather.6.cloned.1.call-start = ((), (), s32[]{:S(2)}) async-start(), calls=%async_computation.1 | async-start | bytes 11280384 | tf_op jit(solution)/shard_map/all_gather | solution.py:139
  12.3 200.3 %copy-start.7 = (f32[1152,144]{0,1:T(8,128)S(1)}, f32[1152,144]{0,1:T(8,128)}, u32[]{:S(2)}) copy-start(f32[1152,144]{0,1:T(8,128)} %param.8) | copy-start | bytes 1990660
  210.4 2.2 collective-permute-start.1
  216.2 5.9 %copy-start.5 = (f32[1152,144]{0,1:T(8,128)}, f32[1152,144]{0,1:T(8,128)S(1)}, u32[]{:S(2)}) copy-start(f32[1152,144]{0,1:T(8,128)S(1)} %fusion.5) | copy-start | bytes 1990660
  216.2 2.2 collective-permute-start.2
  230.1 5.8 %copy-start.6 = (f32[1152,144]{0,1:T(8,128)S(1)}, f32[1152,144]{0,1:T(8,128)}, u32[]{:S(2)}) copy-start(f32[1152,144]{0,1:T(8,128)} %param.6) | copy-start | bytes 1990660
  230.1 283.6 %all-gather.8.cloned.1.call-start = ((), (), s32[]{:S(2)}) async-start(), calls=%async_computation.2 | async-start | bytes 11280384 | tf_op jit(solution)/shard_map/all_gather | solution.py:105
  230.4 1.7 collective-permute-start.3
  232.1 8.2 %slice-start.2 = ((s8[5308416]{0:T(1024)(128)(4,1)}), s8[4194304]{0:T(1024)(128)(4,1)S(1)}, s32[]{:S(2)}) async-start(s8[5308416]{0:T(1024)(128)(4,1)} %bitcast.51), calls=%async_computation.5 | async-start | bytes 8388608
  235.9 4.5 slice-start.3
  240.3 4.1 copy-start.3
  240.3 4.1 copy-start.4
  246.5 20.3 %collective-permute-start.4 = (f32[1152,144]{0,1:T(8,128)S(1)}, f32[1152,144]{0,1:T(8,128)S(1)}, u32[]{:S(2)}, u32[]{:S(2)}) collective-permute-start(f32[1152,144]{0,1:T(8,128)S(1)} %constant_dynamic-slice_fusion), channel_id=1, source_target_pairs={{0,16},{16,0},{1,17},{17,1},{2,18},{18,2},{3,19},{19,3},{4,20},{20... | collective-permute-start | bytes 1990664 | tf_op jit(solution)/shard_map/ppermute | solution.py:58
  248.1 3.7 collective-permute-start.5
  252.5 4.6 collective-permute-start.6
  257.7 3.7 collective-permute-start.7
  261.4 3.7 collective-permute-start.8
  265.1 1.2 collective-permute-start.9
  370.5 3.1 collective-permute-start.10
  381.9 143.6 %copy-start.1 = (f32[1152,144]{0,1:T(8,128)S(1)}, f32[1152,144]{0,1:T(8,128)}, u32[]{:S(2)}) copy-start(f32[1152,144]{0,1:T(8,128)} %fusion.8) | copy-start | bytes 1990660
  513.7 11.8 %copy-start = (f32[1152,2304]{0,1:T(8,128)S(1)}, f32[1152,2304]{0,1:T(8,128)}, u32[]{:S(2)}) copy-start(f32[1152,2304]{0,1:T(8,128)} %all-gather.8.cloned.1.call-done) | copy-start | bytes 31850500
  522.4 3.1 collective-permute-start.11
  (3 other events, 8.3 us)
Sparse Core Ops, SparseCore 0:
  12.3 186.2 all-gather.3
  230.3 131.8 all-gather.5
  382.1 131.6 all-gather.7

commit v6 on v5

--- a/solution.py
+++ b/solution.py
@@ -130,7 +130,8 @@
         stat_next = stat_decay * stat_left + (1.0 - stat_decay) / D * gram
         by_rows = ((1,), (0,))
         power = split_dot(hi_rows, lo_rows, shard_concat(stat_next, c), by_rows)
-        power, hi_later, lo_later = lax.optimization_barrier((power, hi_rows, lo_rows))
+        power, stacked_later = lax.optimization_barrier((power, stacked))
+        hi_later, lo_later = stacked_later[1], stacked_later[2]
         rotated = bf16_dot(hi_later, grad_cols, by_rows) + bf16_dot(lo_later, grad_cols, by_rows)
         moment_next = beta_one * moment + (1.0 - beta_one) * rotated
         second_next = beta_two * second + (1.0 - beta_two) * rotated * rotated

time: 537 us -> 529 us (0.985)
  local copies, waits for them, and re-layouts: 14.1 us -> 5.91 us
    squeeze x1 -> x0, local copies, waits for them, and re-layouts: 10.6 us -> none  [shards(): grad_rows, hi_rows, lo_rows = (stacked[0], stacked[1], stacked[2])]
where the time goes in v6:
time: 529 us; the launch traced here: 528 us
  waiting for transfers between devices  433 us (82%)
  matrix products  62.3 us (12%)
  between operations  14.8 us (3%)
  other arithmetic  6.57 us (1%)
  starting transfers between devices  5.92 us (1%)
  local copies, waits for them, and re-layouts  5.91 us (1%)
    all_gather x1, waiting for transfers between devices, shards(): lax.all_gather(jnp.stack([grad, basis_hi, basis_lo]), TS, axis=2, tiled=T...  186 us
    all_gather x1, waiting for transfers between devices, newton_step(): iterate_rows = lax.all_gather(iterate, TS, axis=1, tiled=True)  132 us
    all_gather x1, waiting for transfers between devices, shards(): power_rows = lax.all_gather(power, TS, axis=1, tiled=True)  91 us
    dot_general x8, matrix products, bf16_dot(): lax.dot_general(left, right, (dims, ((), ())), preferred_element_type=jnp...  29 us
    dot_general x2, matrix products, contract_rows(): lax.dot_general(left, right, (((0,), (0,)), ((), ())), precision=lax.Prec...  17.1 us
    dot_general x2, matrix products, exact_dot(): jnp.dot(left, right, precision=lax.Precision.HIGH, preferred_element_type...  12.6 us
    ppermute x8, waiting for transfers between devices, partner(): return lax.ppermute(x, 'shard', [(0, 1), (1, 0)])  12.2 us
    ppermute x4, waiting for transfers between devices, all_sum(): x = x + lax.ppermute(x, TS, [(i, i ^ step) for i in range(n_ts)])  11.3 us
  transfers between devices with their start and end apart: 15, of which 14 were waited for; matrix products, arithmetic and copies ran while one was open for 4% of the time, Pallas kernels for 0%

profile of v6, /device:TPU:0, one launch (start us, length us, event | category | flops | bytes accessed | tf_op | source)
XLA Modules:
  0.0 528.3 jit_solution(17279098674189860225)
XLA Ops:
  12.3 186.3 %all-gather.4.cloned.1.call-done = bf16[3,1152,2304]{1,2,0:T(8,128)(2,1)} async-done(((bf16[3,1152,144]{1,2,0:T(8,128)(2,1)}), bf16[3,1152,2304]{1,2,0:T(8,128)(2,1)}) %all-gather.4.cloned.1.call-update) | async-done | bytes 15925264 | tf_op jit(solution)/shard_map/all_gather | solution.py:124
  198.6 2.5 slice-done.4
  202.3 2.1 collective-permute-done.1
  204.4 3.6 fusion.34
  210.4 3.6 fusion.13
  214.0 3.6 fusion
  217.6 4.5 fusion.30
  224.1 3.7 fusion.3
  227.8 4.7 multiply_add_fusion
  232.6 5.0 fusion.5
  237.7 2.0 fusion.20
  239.7 2.0 fusion.23
  243.4 3.6 collective-permute-done.5
  249.0 3.2 collective-permute-done.6
  254.4 2.3 collective-permute-done.7
  258.1 2.2 collective-permute-done.8
  262.9 91.0 %all-gather.6.cloned.1.call-done = f32[1152,2304]{0,1:T(8,128)} async-done(((f32[1152,144]{0,1:T(8,128)}), f32[1152,2304]{0,1:T(8,128)}) %all-gather.6.cloned.1.call-update) | async-done | bytes 10616848 | tf_op jit(solution)/shard_map/all_gather | solution.py:140
  354.0 8.4 %fusion.62 = f32[2304,144]{0,1:T(8,128)S(1)} fusion(f32[1152,2304]{0,1:T(8,128)} %all-gather.6.cloned.1.call-done, f32[1152,144]{0,1:T(8,128)S(1)} %copy-done.2), kind=kOutput, calls=%fused_computation.76 | convolution fusion | flops 2293235712 | bytes 12607488 | tf_op jit(solution)/shard_map/dot_general | solution.py:28
  363.1 2.4 collective-permute-done.10
  365.5 8.3 %fusion.37 = f32[1152,144]{0,1:T(8,128)} fusion(f32[1152,2304]{0,1:T(8,128)} %all-gather.6.cloned.1.call-done, f32[2304,144]{0,1:T(8,128)S(1)} %fusion.62, f32[2304,144]{0,1:T(8,128)S(1)} %collective-permute-done.10, f32[1152,144]{0,1:T(8,128)S(1)} %copy-done.2, f32[]{:T(128)S(6)} %mul.107, f32[]{:T(128)S(6)} %mul.102), kind=kOutput, calls=%fused_computation.31 | convolution fusion | flops 2294065152 | bytes 14598152 | tf_op jit(solution)/shard_map/dot_general | solution.py:24
  373.8 131.8 %all-gather.8.cloned.1.call-done = f32[1152,2304]{0,1:T(8,128)} async-done(((f32[1152,144]{0,1:T(8,128)}), f32[1152,2304]{0,1:T(8,128)}) %all-gather.8.cloned.1.call-update) | async-done | bytes 10616848 | tf_op jit(solution)/shard_map/all_gather | solution.py:105
  505.6 8.6 %fusion.63 = f32[2304,144]{0,1:T(8,128)S(1)} fusion(f32[1152,2304]{0,1:T(8,128)} %all-gather.8.cloned.1.call-done, f32[1152,144]{0,1:T(8,128)} %fusion.37), kind=kOutput, calls=%fused_computation.77 | convolution fusion | flops 2293235712 | bytes 12607488 | tf_op jit(solution)/shard_map/dot_general | solution.py:28
  514.3 3.0 collective-permute-done.11
  517.4 4.3 multiply_subtract_fusion
  (69 shorter events, 20.7 us)
Async XLA Ops:
  7.2 191.5 %all-gather.4.cloned.1.call-start = ((), (), s32[]{:S(2)}) async-start(), calls=%async_computation | async-start | bytes 16920576 | tf_op jit(solution)/shard_map/all_gather | solution.py:124
  8.2 1.8 collective-permute-start
  12.2 341.8 %all-gather.6.cloned.1.call-start = ((), (), s32[]{:S(2)}) async-start(), calls=%async_computation.1 | async-start | bytes 11280384 | tf_op jit(solution)/shard_map/all_gather | solution.py:140
  12.3 192.1 %copy-start.4 = (f32[1152,144]{0,1:T(8,128)S(1)}, f32[1152,144]{0,1:T(8,128)}, u32[]{:S(2)}) copy-start(f32[1152,144]{0,1:T(8,128)} %param.8) | copy-start | bytes 1990660
  202.2 2.2 collective-permute-start.1
  208.1 5.9 %copy-start.3 = (f32[1152,144]{0,1:T(8,128)}, f32[1152,144]{0,1:T(8,128)S(1)}, u32[]{:S(2)}) copy-start(f32[1152,144]{0,1:T(8,128)S(1)} %fusion.34) | copy-start | bytes 1990660
  208.1 2.2 collective-permute-start.2
  222.1 283.5 %all-gather.8.cloned.1.call-start = ((), (), s32[]{:S(2)}) async-start(), calls=%async_computation.2 | async-start | bytes 11280384 | tf_op jit(solution)/shard_map/all_gather | solution.py:105
  222.3 1.7 collective-permute-start.3
  224.1 13.5 %slice-start = ((s8[15925248]{0:T(1024)(128)(4,1)}), s8[4194304]{0:T(1024)(128)(4,1)S(1)}, s32[]{:S(2)}) async-start(s8[15925248]{0:T(1024)(128)(4,1)} %bitcast.68), calls=%async_computation.3 | async-start | bytes 8388608
  224.1 13.5 %slice-start.1 = ((s8[15925248]{0:T(1024)(128)(4,1)}), s8[4194304]{0:T(1024)(128)(4,1)S(1)}, s32[]{:S(2)}) async-start(s8[15925248]{0:T(1024)(128)(4,1)} %bitcast.68), calls=%async_computation.4 | async-start | bytes 8388608
  227.8 9.8 %slice-start.2 = ((s8[15925248]{0:T(1024)(128)(4,1)}), s8[4194304]{0:T(1024)(128)(4,1)S(1)}, s32[]{:S(2)}) async-start(s8[15925248]{0:T(1024)(128)(4,1)} %bitcast.68), calls=%async_computation.5 | async-start | bytes 8388608
  232.6 7.1 %copy-start.7 = (f32[1152,144]{0,1:T(8,128)}, f32[1152,144]{0,1:T(8,128)S(1)}, u32[]{:S(2)}) copy-start(f32[1152,144]{0,1:T(8,128)S(1)} %get-tuple-element.19) | copy-start | bytes 1990660
  232.6 7.1 %copy-start.8 = (f32[1152,144]{0,1:T(8,128)}, f32[1152,144]{0,1:T(8,128)S(1)}, u32[]{:S(2)}) copy-start(f32[1152,144]{0,1:T(8,128)S(1)} %get-tuple-element.20) | copy-start | bytes 1990660
  241.8 20.3 %collective-permute-start.4 = (f32[1152,144]{0,1:T(8,128)S(1)}, f32[1152,144]{0,1:T(8,128)S(1)}, u32[]{:S(2)}, u32[]{:S(2)}) collective-permute-start(f32[1152,144]{0,1:T(8,128)S(1)} %constant_dynamic-slice_fusion), channel_id=1, source_target_pairs={{0,16},{16,0},{1,17},{17,1},{2,18},{18,2},{3,19},{19,3},{4,20},{20... | collective-permute-start | bytes 1990664 | tf_op jit(solution)/shard_map/ppermute | solution.py:58
  243.4 3.7 collective-permute-start.5
  247.7 4.6 collective-permute-start.6
  252.9 3.7 collective-permute-start.7
  256.7 3.7 collective-permute-start.8
  260.3 1.2 collective-permute-start.9
  362.4 3.1 collective-permute-start.10
  373.8 143.6 %copy-start.1 = (f32[1152,144]{0,1:T(8,128)S(1)}, f32[1152,144]{0,1:T(8,128)}, u32[]{:S(2)}) copy-start(f32[1152,144]{0,1:T(8,128)} %fusion.37) | copy-start | bytes 1990660
  505.6 11.8 %copy-start = (f32[1152,2304]{0,1:T(8,128)S(1)}, f32[1152,2304]{0,1:T(8,128)}, u32[]{:S(2)}) copy-start(f32[1152,2304]{0,1:T(8,128)} %all-gather.8.cloned.1.call-done) | copy-start | bytes 31850500
  514.3 3.1 collective-permute-start.11
  (5 other events, 21.4 us)
Sparse Core Ops, SparseCore 0:
  12.3 186.2 all-gather.3
  222.2 131.7 all-gather.5
  373.9 131.6 all-gather.7

commit v7 on v6

--- a/solution.py
+++ b/solution.py
@@ -101,10 +101,17 @@
             x = lax.psum(x, TS)
         return shard_sum(x)[0, 0]
 
+    def gather_split_rows(block):
+        hi, lo = split_bf16(block)
+        return lax.all_gather(jnp.stack([hi, lo]), TS, axis=2, tiled=True)
+
+    def newton_products(split_rows, block):
+        rows_hi, rows_lo = split_rows[0], split_rows[1]
+        z_cols = shard_sum(split_dot(rows_hi, rows_lo, block, ((0,), (0,))))
+        return split_dot(rows_hi, rows_lo, z_cols, ((1,), (0,)))
+
     def newton_step(iterate):
-        iterate_rows = lax.all_gather(iterate, TS, axis=1, tiled=True)
-        z_cols = shard_sum(contract_rows(iterate_rows, iterate))
-        return 1.5 * iterate - 0.5 * exact_dot(iterate_rows, z_cols)
+        return 1.5 * iterate - 0.5 * newton_products(gather_split_rows(iterate), iterate)
 
     def shards(grad_parts, moment, second, stat_left, basis_left):
         c = lax.axis_index("shard")
@@ -129,7 +136,11 @@
         )
         stat_next = stat_decay * stat_left + (1.0 - stat_decay) / D * gram
         by_rows = ((1,), (0,))
-        power = split_dot(hi_rows, lo_rows, shard_concat(stat_next, c), by_rows)
+        stat_hi, stat_lo = split_bf16(stat_next)
+        stat_hi, stat_lo = shard_concat(stat_hi, c), shard_concat(stat_lo, c)
+        power = (
+            bf16_dot(hi_rows, stat_hi, by_rows) + bf16_dot(hi_rows, stat_lo, by_rows) + bf16_dot(lo_rows, stat_hi, by_rows)
+        )
         power, stacked_later = lax.optimization_barrier((power, stacked))
         hi_later, lo_later = stacked_later[1], stacked_later[2]
         rotated = bf16_dot(hi_later, grad_cols, by_rows) + bf16_dot(lo_later, grad_cols, by_rows)
@@ -137,12 +148,11 @@
         second_next = beta_two * second + (1.0 - beta_two) * rotated * rotated
         ratio = moment_next / first_fix / (jnp.sqrt(second_next / second_fix) + adam_eps)
         update = shard_sum_scatter(split_dot(hi_later, lo_later, ratio, ((0,), (0,))), c, 0)
-        power_rows = lax.all_gather(power, TS, axis=1, tiled=True)
+        power_rows = gather_split_rows(power)
         total_sq = all_sum(jnp.sum(power * power))
         power_rows, update, total_sq = lax.optimization_barrier((power_rows, update, total_sq))
-        z_cols = shard_sum(contract_rows(power_rows, power))
         scale = shrink * jnp.sqrt(D / (total_sq + norm_eps))
-        iterate = (1.5 * scale) * power - (0.5 * scale * scale * scale) * exact_dot(power_rows, z_cols)
+        iterate = (1.5 * scale) * power - (0.5 * scale * scale * scale) * newton_products(power_rows, power)
         for turn in range(NS_ITERS - 1):
             iterate = newton_step(iterate)
         return (update, moment_next, second_next, stat_next, iterate)

time: 529 us -> 533 us (level)
    dot_general x4 -> x0, matrix products: 29.7 us -> none  [the longest x2 17.1 us: contract_rows(): lax.dot_general(left, right, (((0,), (0,)), ((), ())), precision=lax.Prec...]
    dot_general x8 -> x20, matrix products: 29 us -> 56.1 us  [bf16_dot(): lax.dot_general(left, right, (dims, ((), ())), preferred_element_type=jnp...]
    ppermute x8 -> x9, waiting for transfers between devices: 12.2 us -> 11.7 us  [partner(): return lax.ppermute(x, 'shard', [(0, 1), (1, 0)])]
  transfers between devices with their start and end apart: 15 -> 16, of which waited for: 14 -> 15; matrix products, arithmetic and copies ran while one was open for 4% -> 4% of each run, Pallas kernels for 0% -> 0%
where the time goes in v7:
time: 533 us; the launch traced here: 532 us
  waiting for transfers between devices  433 us (81%)
  matrix products  60.6 us (11%)
  between operations  14.9 us (3%)
  other arithmetic  8.69 us (2%)
  local copies, waits for them, and re-layouts  8.64 us (2%)
  starting transfers between devices  6.16 us (1%)
    all_gather x2, waiting for transfers between devices, gather_split_rows(): return lax.all_gather(jnp.stack([hi, lo]), TS, axis=2, tiled=True)  224 us
    all_gather x1, waiting for transfers between devices, shards(): lax.all_gather(jnp.stack([grad, basis_hi, basis_lo]), TS, axis=2, tiled=T...  186 us
    dot_general x20, matrix products, bf16_dot(): lax.dot_general(left, right, (dims, ((), ())), preferred_element_type=jnp...  56.1 us
    ppermute x9, waiting for transfers between devices, partner(): return lax.ppermute(x, 'shard', [(0, 1), (1, 0)])  11.7 us
    ppermute x4, waiting for transfers between devices, all_sum(): x = x + lax.ppermute(x, TS, [(i, i ^ step) for i in range(n_ts)])  11.4 us
  transfers between devices with their start and end apart: 16, of which 15 were waited for; matrix products, arithmetic and copies ran while one was open for 4% of the time, Pallas kernels for 0%

profile of v7, /device:TPU:0, one launch (start us, length us, event | category | flops | bytes accessed | tf_op | source)
XLA Modules:
  0.0 532.1 jit_solution(14167743766404552858)
XLA Ops:
  12.3 186.3 %all-gather.4.cloned.1.call-done = bf16[3,1152,2304]{1,2,0:T(8,128)(2,1)} async-done(((bf16[3,1152,144]{1,2,0:T(8,128)(2,1)}), bf16[3,1152,2304]{1,2,0:T(8,128)(2,1)}) %all-gather.4.cloned.1.call-update) | async-done | bytes 15925264 | tf_op jit(solution)/shard_map/all_gather | solution.py:131
  198.6 2.5 slice-done.4
  202.3 2.1 collective-permute-done.1
  204.4 4.5 fusion.86
  211.1 3.6 fusion.26
  214.7 3.6 fusion
  218.2 3.6 fusion.64
  225.6 3.7 fusion.15
  229.3 4.9 multiply_add_fusion
  234.2 5.0 fusion.17
  241.3 2.0 fusion.43
  244.3 3.7 collective-permute-done.6
  249.9 3.3 collective-permute-done.7
  255.3 2.3 collective-permute-done.8
  259.0 2.2 collective-permute-done.9
  263.9 91.7 %all-gather.6.cloned.1.call-done = bf16[2,1152,2304]{1,2,0:T(8,128)(2,1)} async-done(((bf16[2,1152,144]{1,2,0:T(8,128)(2,1)}), bf16[2,1152,2304]{1,2,0:T(8,128)(2,1)}) %all-gather.6.cloned.1.call-update) | async-done | bytes 10616848 | tf_op jit(solution)/shard_map/all_gather | solution.py:106
  355.5 4.2 fusion.9
  365.1 2.3 collective-permute-done.11
  367.6 3.7 fusion.1
  371.3 3.9 fusion.7
  377.5 131.9 %all-gather.8.cloned.1.call-done = bf16[2,1152,2304]{1,2,0:T(8,128)(2,1)} async-done(((bf16[2,1152,144]{1,2,0:T(8,128)(2,1)}), bf16[2,1152,2304]{1,2,0:T(8,128)(2,1)}) %all-gather.8.cloned.1.call-update) | async-done | bytes 10616848 | tf_op jit(solution)/shard_map/all_gather | solution.py:106
  509.4 4.2 fusion.51
  518.3 3.0 collective-permute-done.12
  523.5 2.0 fusion.62
  (86 shorter events, 37.0 us)
Async XLA Ops:
  7.2 191.5 %all-gather.4.cloned.1.call-start = ((), (), s32[]{:S(2)}) async-start(), calls=%async_computation | async-start | bytes 16920576 | tf_op jit(solution)/shard_map/all_gather | solution.py:131
  8.2 1.8 collective-permute-start
  12.2 343.3 %all-gather.6.cloned.1.call-start = ((), (), s32[]{:S(2)}) async-start(), calls=%async_computation.1 | async-start | bytes 11280384 | tf_op jit(solution)/shard_map/all_gather | solution.py:106
  12.3 192.1 %copy-start.2 = (f32[1152,144]{0,1:T(8,128)S(1)}, f32[1152,144]{0,1:T(8,128)}, u32[]{:S(2)}) copy-start(f32[1152,144]{0,1:T(8,128)} %param.8) | copy-start | bytes 1990660
  202.2 2.2 collective-permute-start.1
  208.9 1.6 collective-permute-start.3
  209.1 2.0 collective-permute-start.2
  223.5 285.8 %all-gather.8.cloned.1.call-start = ((), (), s32[]{:S(2)}) async-start(), calls=%async_computation.2 | async-start | bytes 11280384 | tf_op jit(solution)/shard_map/all_gather | solution.py:106
  223.8 1.7 collective-permute-start.4
  225.5 13.7 %slice-start = ((s8[15925248]{0:T(1024)(128)(4,1)}), s8[4194304]{0:T(1024)(128)(4,1)S(1)}, s32[]{:S(2)}) async-start(s8[15925248]{0:T(1024)(128)(4,1)} %bitcast.124), calls=%async_computation.3 | async-start | bytes 8388608
  225.6 13.7 %slice-start.1 = ((s8[15925248]{0:T(1024)(128)(4,1)}), s8[4194304]{0:T(1024)(128)(4,1)S(1)}, s32[]{:S(2)}) async-start(s8[15925248]{0:T(1024)(128)(4,1)} %bitcast.124), calls=%async_computation.4 | async-start | bytes 8388608
  229.3 10.0 %slice-start.2 = ((s8[15925248]{0:T(1024)(128)(4,1)}), s8[4194304]{0:T(1024)(128)(4,1)S(1)}, s32[]{:S(2)}) async-start(s8[15925248]{0:T(1024)(128)(4,1)} %bitcast.124), calls=%async_computation.5 | async-start | bytes 8388608
  234.2 7.1 %copy-start.4 = (f32[1152,144]{0,1:T(8,128)}, f32[1152,144]{0,1:T(8,128)S(1)}, u32[]{:S(2)}) copy-start(f32[1152,144]{0,1:T(8,128)S(1)} %get-tuple-element.22) | copy-start | bytes 1990660
  234.2 7.1 %copy-start.5 = (f32[1152,144]{0,1:T(8,128)}, f32[1152,144]{0,1:T(8,128)S(1)}, u32[]{:S(2)}) copy-start(f32[1152,144]{0,1:T(8,128)S(1)} %get-tuple-element.23) | copy-start | bytes 1990660
  243.4 19.6 %collective-permute-start.5 = (f32[1152,144]{0,1:T(8,128)S(1)}, f32[1152,144]{0,1:T(8,128)S(1)}, u32[]{:S(2)}, u32[]{:S(2)}) collective-permute-start(f32[1152,144]{0,1:T(8,128)S(1)} %constant_dynamic-slice_fusion), channel_id=1, source_target_pairs={{0,16},{16,0},{1,17},{17,1},{2,18},{18,2},{3,19},{19,3},{4,20},{20... | collective-permute-start | bytes 1990664 | tf_op jit(solution)/shard_map/ppermute | solution.py:58
  244.2 3.7 collective-permute-start.6
  248.6 4.6 collective-permute-start.7
  253.9 3.7 collective-permute-start.8
  257.5 3.7 collective-permute-start.9
  261.2 1.2 collective-permute-start.10
  364.3 3.1 collective-permute-start.11
  367.5 7.8 %slice-start.5 = ((s8[10616832]{0:T(1024)(128)(4,1)}), s8[4194304]{0:T(1024)(128)(4,1)S(1)}, s32[]{:S(2)}) async-start(s8[10616832]{0:T(1024)(128)(4,1)} %bitcast.127), calls=%async_computation.8 | async-start | bytes 8388608
  367.6 7.7 %slice-start.6 = ((s8[10616832]{0:T(1024)(128)(4,1)}), s8[4194304]{0:T(1024)(128)(4,1)S(1)}, s32[]{:S(2)}) async-start(s8[10616832]{0:T(1024)(128)(4,1)} %bitcast.127), calls=%async_computation.9 | async-start | bytes 8388608
  518.2 3.1 collective-permute-start.12
  (6 other events, 28.5 us)
Sparse Core Ops, SparseCore 0:
  12.3 186.2 all-gather.3
  223.7 131.8 all-gather.5
  377.6 131.6 all-gather.7

commit v8 on v6

--- a/solution.py
+++ b/solution.py
@@ -129,7 +129,9 @@
         )
         stat_next = stat_decay * stat_left + (1.0 - stat_decay) / D * gram
         by_rows = ((1,), (0,))
-        power = split_dot(hi_rows, lo_rows, shard_concat(stat_next, c), by_rows)
+        stat_hi, stat_lo = split_bf16(shard_concat(stat_next, c))
+        both = bf16_dot(hi_rows, jnp.concatenate([stat_hi, stat_lo], axis=1), by_rows)
+        power = both[:, :cols] + both[:, cols:] + bf16_dot(lo_rows, stat_hi, by_rows)
         power, stacked_later = lax.optimization_barrier((power, stacked))
         hi_later, lo_later = stacked_later[1], stacked_later[2]
         rotated = bf16_dot(hi_later, grad_cols, by_rows) + bf16_dot(lo_later, grad_cols, by_rows)

time: 529 us -> 526 us (level)
    dot_general x8 -> x7, matrix products: 29 us -> 26.5 us  [bf16_dot(): lax.dot_general(left, right, (dims, ((), ())), preferred_element_type=jnp...]
where the time goes in v8:
time: 526 us
  waiting for transfers between devices  432 us (82%)
  matrix products  59.8 us (11%)
  between operations  14.8 us (3%)
  other arithmetic  6.7 us (1%)
  starting transfers between devices  6.11 us (1%)
  local copies, waits for them, and re-layouts  5.93 us (1%)
    all_gather x1, waiting for transfers between devices, shards(): lax.all_gather(jnp.stack([grad, basis_hi, basis_lo]), TS, axis=2, tiled=T...  186 us
    all_gather x1, waiting for transfers between devices, newton_step(): iterate_rows = lax.all_gather(iterate, TS, axis=1, tiled=True)  132 us
    all_gather x1, waiting for transfers between devices, shards(): power_rows = lax.all_gather(power, TS, axis=1, tiled=True)  90.8 us
    dot_general x7, matrix products, bf16_dot(): lax.dot_general(left, right, (dims, ((), ())), preferred_element_type=jnp...  26.5 us
    dot_general x2, matrix products, contract_rows(): lax.dot_general(left, right, (((0,), (0,)), ((), ())), precision=lax.Prec...  17.1 us
    dot_general x2, matrix products, exact_dot(): jnp.dot(left, right, precision=lax.Precision.HIGH, preferred_element_type...  12.6 us
    ppermute x8, waiting for transfers between devices, partner(): return lax.ppermute(x, 'shard', [(0, 1), (1, 0)])  12.2 us
    ppermute x4, waiting for transfers between devices, all_sum(): x = x + lax.ppermute(x, TS, [(i, i ^ step) for i in range(n_ts)])  11.2 us
  transfers between devices with their start and end apart: 15, of which 14 were waited for; matrix products, arithmetic and copies ran while one was open for 4% of the time, Pallas kernels for 0%

profile of v8, /device:TPU:0, one launch (start us, length us, event | category | flops | bytes accessed | tf_op | source)
XLA Modules:
  0.0 525.7 jit_solution(16127109791892036529)
XLA Ops:
  12.3 186.3 %all-gather.4.cloned.1.call-done = bf16[3,1152,2304]{1,2,0:T(8,128)(2,1)} async-done(((bf16[3,1152,144]{1,2,0:T(8,128)(2,1)}), bf16[3,1152,2304]{1,2,0:T(8,128)(2,1)}) %all-gather.4.cloned.1.call-update) | async-done | bytes 15925264 | tf_op jit(solution)/shard_map/all_gather | solution.py:124
  198.6 2.5 slice-done.4
  202.3 2.1 collective-permute-done.1
  204.4 3.6 fusion.32
  208.3 2.0 collective-permute-done.2
  210.6 4.4 fusion.1
  215.0 4.4 fusion.31
  221.5 3.7 fusion.4
  225.2 5.0 multiply_add_fusion
  230.3 5.0 fusion.6
  235.3 2.0 fusion.19
  237.4 2.0 fusion.22
  241.1 3.6 collective-permute-done.5
  246.8 3.2 collective-permute-done.6
  252.1 2.2 collective-permute-done.7
  255.8 2.2 collective-permute-done.8
  260.7 90.8 %all-gather.6.cloned.1.call-done = f32[1152,2304]{0,1:T(8,128)} async-done(((f32[1152,144]{0,1:T(8,128)}), f32[1152,2304]{0,1:T(8,128)}) %all-gather.6.cloned.1.call-update) | async-done | bytes 10616848 | tf_op jit(solution)/shard_map/all_gather | solution.py:142
  351.4 8.4 %fusion.60 = f32[2304,144]{0,1:T(8,128)S(1)} fusion(f32[1152,2304]{0,1:T(8,128)} %all-gather.6.cloned.1.call-done, f32[1152,144]{0,1:T(8,128)S(1)} %copy-done.2), kind=kOutput, calls=%fused_computation.76 | convolution fusion | flops 2293235712 | bytes 12607488 | tf_op jit(solution)/shard_map/dot_general | solution.py:28
  360.6 2.3 collective-permute-done.10
  363.0 8.3 %fusion.35 = f32[1152,144]{0,1:T(8,128)} fusion(f32[1152,2304]{0,1:T(8,128)} %all-gather.6.cloned.1.call-done, f32[2304,144]{0,1:T(8,128)S(1)} %fusion.60, f32[2304,144]{0,1:T(8,128)S(1)} %collective-permute-done.10, f32[1152,144]{0,1:T(8,128)S(1)} %copy-done.2, f32[]{:T(128)S(6)} %mul.107, f32[]{:T(128)S(6)} %mul.102), kind=kOutput, calls=%fused_computation.29 | convolution fusion | flops 2294065152 | bytes 14598152 | tf_op jit(solution)/shard_map/dot_general | solution.py:24
  371.3 131.8 %all-gather.8.cloned.1.call-done = f32[1152,2304]{0,1:T(8,128)} async-done(((f32[1152,144]{0,1:T(8,128)}), f32[1152,2304]{0,1:T(8,128)}) %all-gather.8.cloned.1.call-update) | async-done | bytes 10616848 | tf_op jit(solution)/shard_map/all_gather | solution.py:105
  503.1 8.6 %fusion.61 = f32[2304,144]{0,1:T(8,128)S(1)} fusion(f32[1152,2304]{0,1:T(8,128)} %all-gather.8.cloned.1.call-done, f32[1152,144]{0,1:T(8,128)} %fusion.35), kind=kOutput, calls=%fused_computation.77 | convolution fusion | flops 2293235712 | bytes 12607488 | tf_op jit(solution)/shard_map/dot_general | solution.py:28
  511.8 3.0 collective-permute-done.11
  514.8 4.3 multiply_subtract_fusion
  (69 shorter events, 19.0 us)
Async XLA Ops:
  7.2 191.5 %all-gather.4.cloned.1.call-start = ((), (), s32[]{:S(2)}) async-start(), calls=%async_computation | async-start | bytes 16920576 | tf_op jit(solution)/shard_map/all_gather | solution.py:124
  8.2 1.8 collective-permute-start
  12.2 339.2 %all-gather.6.cloned.1.call-start = ((), (), s32[]{:S(2)}) async-start(), calls=%async_computation.1 | async-start | bytes 11280384 | tf_op jit(solution)/shard_map/all_gather | solution.py:142
  202.2 2.2 collective-permute-start.1
  208.1 2.2 collective-permute-start.2
  219.5 283.6 %all-gather.8.cloned.1.call-start = ((), (), s32[]{:S(2)}) async-start(), calls=%async_computation.2 | async-start | bytes 11280384 | tf_op jit(solution)/shard_map/all_gather | solution.py:105
  219.7 1.7 collective-permute-start.3
  221.4 3.8 copy-start.6
  221.5 13.8 %slice-start = ((s8[15925248]{0:T(1024)(128)(4,1)}), s8[4194304]{0:T(1024)(128)(4,1)S(1)}, s32[]{:S(2)}) async-start(s8[15925248]{0:T(1024)(128)(4,1)} %bitcast.66), calls=%async_computation.3 | async-start | bytes 8388608
  221.5 13.8 %slice-start.1 = ((s8[15925248]{0:T(1024)(128)(4,1)}), s8[4194304]{0:T(1024)(128)(4,1)S(1)}, s32[]{:S(2)}) async-start(s8[15925248]{0:T(1024)(128)(4,1)} %bitcast.66), calls=%async_computation.4 | async-start | bytes 8388608
  225.2 10.1 %slice-start.2 = ((s8[15925248]{0:T(1024)(128)(4,1)}), s8[4194304]{0:T(1024)(128)(4,1)S(1)}, s32[]{:S(2)}) async-start(s8[15925248]{0:T(1024)(128)(4,1)} %bitcast.66), calls=%async_computation.5 | async-start | bytes 8388608
  230.2 7.1 %copy-start.7 = (f32[1152,144]{0,1:T(8,128)}, f32[1152,144]{0,1:T(8,128)S(1)}, u32[]{:S(2)}) copy-start(f32[1152,144]{0,1:T(8,128)S(1)} %get-tuple-element.21) | copy-start | bytes 1990660
  230.3 7.1 %copy-start.8 = (f32[1152,144]{0,1:T(8,128)}, f32[1152,144]{0,1:T(8,128)S(1)}, u32[]{:S(2)}) copy-start(f32[1152,144]{0,1:T(8,128)S(1)} %get-tuple-element.22) | copy-start | bytes 1990660
  230.3 5.1 slice-start.3
  239.4 20.3 %collective-permute-start.4 = (f32[1152,144]{0,1:T(8,128)S(1)}, f32[1152,144]{0,1:T(8,128)S(1)}, u32[]{:S(2)}, u32[]{:S(2)}) collective-permute-start(f32[1152,144]{0,1:T(8,128)S(1)} %constant_dynamic-slice_fusion), channel_id=1, source_target_pairs={{0,16},{16,0},{1,17},{17,1},{2,18},{18,2},{3,19},{19,3},{4,20},{20... | collective-permute-start | bytes 1990664 | tf_op jit(solution)/shard_map/ppermute | solution.py:58
  241.0 3.7 collective-permute-start.5
  245.4 4.6 collective-permute-start.6
  250.6 3.7 collective-permute-start.7
  254.4 3.7 collective-permute-start.8
  258.0 1.2 collective-permute-start.9
  359.8 3.1 collective-permute-start.10
  371.3 143.6 %copy-start.1 = (f32[1152,144]{0,1:T(8,128)S(1)}, f32[1152,144]{0,1:T(8,128)}, u32[]{:S(2)}) copy-start(f32[1152,144]{0,1:T(8,128)} %fusion.35) | copy-start | bytes 1990660
  503.1 11.8 %copy-start = (f32[1152,2304]{0,1:T(8,128)S(1)}, f32[1152,2304]{0,1:T(8,128)}, u32[]{:S(2)}) copy-start(f32[1152,2304]{0,1:T(8,128)} %all-gather.8.cloned.1.call-done) | copy-start | bytes 31850500
  511.7 3.1 collective-permute-start.11
  (5 other events, 14.4 us)
Sparse Core Ops, SparseCore 0:
  12.3 186.2 all-gather.3
  219.6 131.8 all-gather.5
  371.4 131.6 all-gather.7

commit v9 on v7

--- a/solution.py
+++ b/solution.py
@@ -105,10 +105,16 @@
         hi, lo = split_bf16(block)
         return lax.all_gather(jnp.stack([hi, lo]), TS, axis=2, tiled=True)
 
+    def pair_dot(left_hi, left_lo, right, dims):
+        right_hi, right_lo = split_bf16(right)
+        width = right.shape[1]
+        both = bf16_dot(left_hi, jnp.concatenate([right_hi, right_lo], axis=1), dims)
+        return both[:, :width] + both[:, width:] + bf16_dot(left_lo, right_hi, dims)
+
     def newton_products(split_rows, block):
         rows_hi, rows_lo = split_rows[0], split_rows[1]
-        z_cols = shard_sum(split_dot(rows_hi, rows_lo, block, ((0,), (0,))))
-        return split_dot(rows_hi, rows_lo, z_cols, ((1,), (0,)))
+        z_cols = shard_sum(pair_dot(rows_hi, rows_lo, block, ((0,), (0,))))
+        return pair_dot(rows_hi, rows_lo, z_cols, ((1,), (0,)))
 
     def newton_step(iterate):
         return 1.5 * iterate - 0.5 * newton_products(gather_split_rows(iterate), iterate)
@@ -136,11 +142,9 @@
         )
         stat_next = stat_decay * stat_left + (1.0 - stat_decay) / D * gram
         by_rows = ((1,), (0,))
-        stat_hi, stat_lo = split_bf16(stat_next)
-        stat_hi, stat_lo = shard_concat(stat_hi, c), shard_concat(stat_lo, c)
-        power = (
-            bf16_dot(hi_rows, stat_hi, by_rows) + bf16_dot(hi_rows, stat_lo, by_rows) + bf16_dot(lo_rows, stat_hi, by_rows)
-        )
+        stat_hi, stat_lo = split_bf16(shard_concat(stat_next, c))
+        both = bf16_dot(hi_rows, jnp.concatenate([stat_hi, stat_lo], axis=1), by_rows)
+        power = both[:, :cols] + both[:, cols:] + bf16_dot(lo_rows, stat_hi, by_rows)
         power, stacked_later = lax.optimization_barrier((power, stacked))
         hi_later, lo_later = stacked_later[1], stacked_later[2]
         rotated = bf16_dot(hi_later, grad_cols, by_rows) + bf16_dot(lo_later, grad_cols, by_rows)

time: 533 us -> 525 us (0.985)
  matrix products: 60.6 us -> 54 us
    dot_general x20 -> x15, matrix products: 56.1 us -> 50.3 us  [bf16_dot(): lax.dot_general(left, right, (dims, ((), ())), preferred_element_type=jnp...]
    ppermute x9 -> x8, waiting for transfers between devices: 11.7 us -> 12.3 us  [partner(): return lax.ppermute(x, 'shard', [(0, 1), (1, 0)])]
  transfers between devices with their start and end apart: 16 -> 15, of which waited for: 15 -> 14; matrix products, arithmetic and copies ran while one was open for 4% -> 4% of each run, Pallas kernels for 0% -> 0%
where the time goes in v9:
time: 525 us
  waiting for transfers between devices  433 us (82%)
  matrix products  54 us (10%)
  between operations  14.8 us (3%)
  other arithmetic  8.97 us (2%)
  local copies, waits for them, and re-layouts  7.85 us (1%)
  starting transfers between devices  5.97 us (1%)
    all_gather x2, waiting for transfers between devices, gather_split_rows(): return lax.all_gather(jnp.stack([hi, lo]), TS, axis=2, tiled=True)  223 us
    all_gather x1, waiting for transfers between devices, shards(): lax.all_gather(jnp.stack([grad, basis_hi, basis_lo]), TS, axis=2, tiled=T...  186 us
    dot_general x15, matrix products, bf16_dot(): lax.dot_general(left, right, (dims, ((), ())), preferred_element_type=jnp...  50.3 us
    ppermute x8, waiting for transfers between devices, partner(): return lax.ppermute(x, 'shard', [(0, 1), (1, 0)])  12.3 us
    ppermute x4, waiting for transfers between devices, all_sum(): x = x + lax.ppermute(x, TS, [(i, i ^ step) for i in range(n_ts)])  11.3 us
  transfers between devices with their start and end apart: 15, of which 14 were waited for; matrix products, arithmetic and copies ran while one was open for 4% of the time, Pallas kernels for 0%

profile of v9, /device:TPU:0, one launch (start us, length us, event | category | flops | bytes accessed | tf_op | source)
XLA Modules:
  0.0 524.9 jit_solution(10894759715559607697)
XLA Ops:
  12.3 186.3 %all-gather.4.cloned.1.call-done = bf16[3,1152,2304]{1,2,0:T(8,128)(2,1)} async-done(((bf16[3,1152,144]{1,2,0:T(8,128)(2,1)}), bf16[3,1152,2304]{1,2,0:T(8,128)(2,1)}) %all-gather.4.cloned.1.call-update) | async-done | bytes 15925264 | tf_op jit(solution)/shard_map/all_gather | solution.py:137
  198.6 2.5 slice-done.4
  202.3 2.1 collective-permute-done.1
  204.4 3.6 fusion.64
  208.3 2.0 collective-permute-done.2
  210.6 4.4 fusion.1
  215.0 3.6 fusion.63
  222.4 3.7 fusion.12
  226.1 5.0 multiply_add_fusion
  231.2 5.0 fusion.14
  238.2 2.0 fusion.39
  241.2 3.6 collective-permute-done.5
  246.9 3.2 collective-permute-done.6
  252.2 2.2 collective-permute-done.7
  255.9 2.2 collective-permute-done.8
  260.7 91.6 %all-gather.6.cloned.1.call-done = bf16[2,1152,2304]{1,2,0:T(8,128)(2,1)} async-done(((bf16[2,1152,144]{1,2,0:T(8,128)(2,1)}), bf16[2,1152,2304]{1,2,0:T(8,128)(2,1)}) %all-gather.6.cloned.1.call-update) | async-done | bytes 10616848 | tf_op jit(solution)/shard_map/all_gather | solution.py:106
  352.3 4.6 fusion.8
  360.1 2.4 collective-permute-done.10
  362.8 4.4 fusion.6
  367.2 3.9 fusion.82
  372.1 131.9 %all-gather.8.cloned.1.call-done = bf16[2,1152,2304]{1,2,0:T(8,128)(2,1)} async-done(((bf16[2,1152,144]{1,2,0:T(8,128)(2,1)}), bf16[2,1152,2304]{1,2,0:T(8,128)(2,1)}) %all-gather.8.cloned.1.call-update) | async-done | bytes 10616848 | tf_op jit(solution)/shard_map/all_gather | solution.py:106
  503.9 4.6 fusion.23
  511.2 3.0 collective-permute-done.11
  516.4 2.0 fusion.50
  (75 shorter events, 30.1 us)
Async XLA Ops:
  7.2 191.5 %all-gather.4.cloned.1.call-start = ((), (), s32[]{:S(2)}) async-start(), calls=%async_computation | async-start | bytes 16920576 | tf_op jit(solution)/shard_map/all_gather | solution.py:137
  8.2 1.8 collective-permute-start
  12.2 340.1 %all-gather.6.cloned.1.call-start = ((), (), s32[]{:S(2)}) async-start(), calls=%async_computation.1 | async-start | bytes 11280384 | tf_op jit(solution)/shard_map/all_gather | solution.py:106
  202.2 2.2 collective-permute-start.1
  208.1 2.2 collective-permute-start.2
  220.3 283.6 %all-gather.8.cloned.1.call-start = ((), (), s32[]{:S(2)}) async-start(), calls=%async_computation.2 | async-start | bytes 11280384 | tf_op jit(solution)/shard_map/all_gather | solution.py:106
  220.6 1.7 collective-permute-start.3
  222.3 3.9 copy-start.5
  222.4 13.8 %slice-start = ((s8[15925248]{0:T(1024)(128)(4,1)}), s8[4194304]{0:T(1024)(128)(4,1)S(1)}, s32[]{:S(2)}) async-start(s8[15925248]{0:T(1024)(128)(4,1)} %bitcast.104), calls=%async_computation.3 | async-start | bytes 8388608
  222.4 13.8 %slice-start.1 = ((s8[15925248]{0:T(1024)(128)(4,1)}), s8[4194304]{0:T(1024)(128)(4,1)S(1)}, s32[]{:S(2)}) async-start(s8[15925248]{0:T(1024)(128)(4,1)} %bitcast.104), calls=%async_computation.4 | async-start | bytes 8388608
  226.1 10.1 %slice-start.2 = ((s8[15925248]{0:T(1024)(128)(4,1)}), s8[4194304]{0:T(1024)(128)(4,1)S(1)}, s32[]{:S(2)}) async-start(s8[15925248]{0:T(1024)(128)(4,1)} %bitcast.104), calls=%async_computation.5 | async-start | bytes 8388608
  231.1 7.1 %copy-start.6 = (f32[1152,144]{0,1:T(8,128)}, f32[1152,144]{0,1:T(8,128)S(1)}, u32[]{:S(2)}) copy-start(f32[1152,144]{0,1:T(8,128)S(1)} %get-tuple-element.30) | copy-start | bytes 1990660
  231.1 7.1 %copy-start.7 = (f32[1152,144]{0,1:T(8,128)}, f32[1152,144]{0,1:T(8,128)S(1)}, u32[]{:S(2)}) copy-start(f32[1152,144]{0,1:T(8,128)S(1)} %get-tuple-element.31) | copy-start | bytes 1990660
  231.2 5.1 slice-start.3
  240.3 19.5 %collective-permute-start.4 = (f32[1152,144]{0,1:T(8,128)S(1)}, f32[1152,144]{0,1:T(8,128)S(1)}, u32[]{:S(2)}, u32[]{:S(2)}) collective-permute-start(f32[1152,144]{0,1:T(8,128)S(1)} %constant_dynamic-slice_fusion), channel_id=1, source_target_pairs={{0,16},{16,0},{1,17},{17,1},{2,18},{18,2},{3,19},{19,3},{4,20},{20... | collective-permute-start | bytes 1990664 | tf_op jit(solution)/shard_map/ppermute | solution.py:58
  241.2 3.7 collective-permute-start.5
  245.5 4.6 collective-permute-start.6
  250.8 3.7 collective-permute-start.7
  254.5 3.7 collective-permute-start.8
  258.1 1.2 collective-permute-start.9
  352.3 5.6 %copy-start.1 = (bf16[2,1152,2304]{1,2,0:T(8,128)(2,1)S(1)}, bf16[2,1152,2304]{1,2,0:T(8,128)(2,1)}, u32[]{:S(2)}) copy-start(bf16[2,1152,2304]{1,2,0:T(8,128)(2,1)} %all-gather.6.cloned.1.call-done) | copy-start | bytes 31850500
  359.4 3.1 collective-permute-start.10
  503.9 5.6 %copy-start.2 = (bf16[2,1152,2304]{1,2,0:T(8,128)(2,1)S(1)}, bf16[2,1152,2304]{1,2,0:T(8,128)(2,1)}, u32[]{:S(2)}) copy-start(bf16[2,1152,2304]{1,2,0:T(8,128)(2,1)} %all-gather.8.cloned.1.call-done) | copy-start | bytes 31850500
  511.1 3.1 collective-permute-start.11
  (4 other events, 12.1 us)
Sparse Core Ops, SparseCore 0:
  12.3 186.2 all-gather.3
  220.4 131.7 all-gather.5
  372.2 131.6 all-gather.7

commit v10 on v8

--- a/solution.py
+++ b/solution.py
@@ -130,8 +130,8 @@
         stat_next = stat_decay * stat_left + (1.0 - stat_decay) / D * gram
         by_rows = ((1,), (0,))
         stat_hi, stat_lo = split_bf16(shard_concat(stat_next, c))
-        both = bf16_dot(hi_rows, jnp.concatenate([stat_hi, stat_lo], axis=1), by_rows)
-        power = both[:, :cols] + both[:, cols:] + bf16_dot(lo_rows, stat_hi, by_rows)
+        quads = bf16_dot(stacked[1:], jnp.concatenate([stat_hi, stat_lo], axis=1), ((2,), (0,)))
+        power = quads[0, :, :cols] + quads[0, :, cols:] + quads[1, :, :cols]
         power, stacked_later = lax.optimization_barrier((power, stacked))
         hi_later, lo_later = stacked_later[1], stacked_later[2]
         rotated = bf16_dot(hi_later, grad_cols, by_rows) + bf16_dot(lo_later, grad_cols, by_rows)

time: 526 us -> 525 us (level)
    dot_general x7 -> x6, matrix products: 26.5 us -> 24.1 us  [bf16_dot(): lax.dot_general(left, right, (dims, ((), ())), preferred_element_type=jnp...]
where the time goes in v10:
time: 525 us; the launch traced here: 524 us
  waiting for transfers between devices  432 us (82%)
  matrix products  57.4 us (11%)
  between operations  14.8 us (3%)
  other arithmetic  7.63 us (1%)
  starting transfers between devices  6.03 us (1%)
  local copies, waits for them, and re-layouts  5.94 us (1%)
    all_gather x1, waiting for transfers between devices, shards(): lax.all_gather(jnp.stack([grad, basis_hi, basis_lo]), TS, axis=2, tiled=T...  186 us
    all_gather x1, waiting for transfers between devices, newton_step(): iterate_rows = lax.all_gather(iterate, TS, axis=1, tiled=True)  132 us
    all_gather x1, waiting for transfers between devices, shards(): power_rows = lax.all_gather(power, TS, axis=1, tiled=True)  90.8 us
    dot_general x6, matrix products, bf16_dot(): lax.dot_general(left, right, (dims, ((), ())), preferred_element_type=jnp...  24.1 us
    dot_general x2, matrix products, contract_rows(): lax.dot_general(left, right, (((0,), (0,)), ((), ())), precision=lax.Prec...  17.1 us
    dot_general x2, matrix products, exact_dot(): jnp.dot(left, right, precision=lax.Precision.HIGH, preferred_element_type...  12.6 us
    ppermute x8, waiting for transfers between devices, partner(): return lax.ppermute(x, 'shard', [(0, 1), (1, 0)])  12.2 us
    ppermute x4, waiting for transfers between devices, all_sum(): x = x + lax.ppermute(x, TS, [(i, i ^ step) for i in range(n_ts)])  11.3 us
  transfers between devices with their start and end apart: 15, of which 14 were waited for; matrix products, arithmetic and copies ran while one was open for 4% of the time, Pallas kernels for 0%

profile of v10, /device:TPU:0, one launch (start us, length us, event | category | flops | bytes accessed | tf_op | source)
XLA Modules:
  0.0 524.2 jit_solution(3347959291051157756)
XLA Ops:
  12.3 186.3 %all-gather.4.cloned.1.call-done = bf16[3,1152,2304]{1,2,0:T(8,128)(2,1)} async-done(((bf16[3,1152,144]{1,2,0:T(8,128)(2,1)}), bf16[3,1152,2304]{1,2,0:T(8,128)(2,1)}) %all-gather.4.cloned.1.call-update) | async-done | bytes 15925264 | tf_op jit(solution)/shard_map/all_gather | solution.py:124
  198.6 2.5 slice-done.4
  202.3 2.1 collective-permute-done.1
  204.4 3.6 fusion.31
  208.3 2.0 collective-permute-done.2
  210.6 6.4 %fusion = f32[2,1152,288]{1,2,0:T(8,128)S(1)} fusion(bf16[3,1152,2304]{1,2,0:T(8,128)(2,1)} %all-gather.4.cloned.1.call-done, bf16[2304,144]{0,1:T(8,128)(2,1)S(1)} %get-tuple-element.16, bf16[2304,144]{0,1:T(8,128)(2,1)S(1)} %get-tuple-element.15), kind=kOutput, calls=%fused_computation | convolution fusion | flops 3060301824 | bytes 14598144 | tf_op jit(solution)/shard_map/dot_general | solution.py:43
  218.3 1.5 collective-permute-done.3
  219.9 3.7 fusion.4
  223.7 5.0 multiply_add_fusion
  228.7 5.0 fusion.6
  233.8 2.0 fusion.19
  235.8 2.0 fusion.22
  239.6 3.6 collective-permute-done.5
  245.2 3.2 collective-permute-done.6
  250.5 2.3 collective-permute-done.7
  254.3 2.2 collective-permute-done.8
  259.1 90.8 %all-gather.6.cloned.1.call-done = f32[1152,2304]{0,1:T(8,128)} async-done(((f32[1152,144]{0,1:T(8,128)}), f32[1152,2304]{0,1:T(8,128)}) %all-gather.6.cloned.1.call-update) | async-done | bytes 10616848 | tf_op jit(solution)/shard_map/all_gather | solution.py:142
  349.9 8.4 %fusion.59 = f32[2304,144]{0,1:T(8,128)S(1)} fusion(f32[1152,2304]{0,1:T(8,128)} %all-gather.6.cloned.1.call-done, f32[1152,144]{0,1:T(8,128)S(1)} %copy-done.1), kind=kOutput, calls=%fused_computation.75 | convolution fusion | flops 2293235712 | bytes 12607488 | tf_op jit(solution)/shard_map/dot_general | solution.py:28
  359.1 2.3 collective-permute-done.10
  361.4 8.3 %fusion.34 = f32[1152,144]{0,1:T(8,128)} fusion(f32[1152,2304]{0,1:T(8,128)} %all-gather.6.cloned.1.call-done, f32[2304,144]{0,1:T(8,128)S(1)} %fusion.59, f32[2304,144]{0,1:T(8,128)S(1)} %collective-permute-done.10, f32[1152,144]{0,1:T(8,128)S(1)} %copy-done.1, f32[]{:T(128)S(6)} %mul.107, f32[]{:T(128)S(6)} %mul.102), kind=kOutput, calls=%fused_computation.26 | convolution fusion | flops 2294065152 | bytes 14598152 | tf_op jit(solution)/shard_map/dot_general | solution.py:24
  369.7 131.8 %all-gather.8.cloned.1.call-done = f32[1152,2304]{0,1:T(8,128)} async-done(((f32[1152,144]{0,1:T(8,128)}), f32[1152,2304]{0,1:T(8,128)}) %all-gather.8.cloned.1.call-update) | async-done | bytes 10616848 | tf_op jit(solution)/shard_map/all_gather | solution.py:105
  501.5 8.6 %fusion.60 = f32[2304,144]{0,1:T(8,128)S(1)} fusion(f32[1152,2304]{0,1:T(8,128)} %all-gather.8.cloned.1.call-done, f32[1152,144]{0,1:T(8,128)} %fusion.34), kind=kOutput, calls=%fused_computation.76 | convolution fusion | flops 2293235712 | bytes 12607488 | tf_op jit(solution)/shard_map/dot_general | solution.py:28
  510.2 3.0 collective-permute-done.11
  513.3 4.3 multiply_subtract_fusion
  (69 shorter events, 18.4 us)
Async XLA Ops:
  7.2 191.5 %all-gather.4.cloned.1.call-start = ((), (), s32[]{:S(2)}) async-start(), calls=%async_computation | async-start | bytes 16920576 | tf_op jit(solution)/shard_map/all_gather | solution.py:124
  8.2 1.8 collective-permute-start
  12.2 337.7 %all-gather.6.cloned.1.call-start = ((), (), s32[]{:S(2)}) async-start(), calls=%async_computation.1 | async-start | bytes 11280384 | tf_op jit(solution)/shard_map/all_gather | solution.py:142
  202.2 2.2 collective-permute-start.1
  208.1 2.2 collective-permute-start.2
  217.9 283.6 %all-gather.8.cloned.1.call-start = ((), (), s32[]{:S(2)}) async-start(), calls=%async_computation.2 | async-start | bytes 11280384 | tf_op jit(solution)/shard_map/all_gather | solution.py:105
  218.1 1.7 collective-permute-start.3
  219.8 3.8 copy-start.6
  219.9 13.8 %slice-start = ((s8[15925248]{0:T(1024)(128)(4,1)}), s8[4194304]{0:T(1024)(128)(4,1)S(1)}, s32[]{:S(2)}) async-start(s8[15925248]{0:T(1024)(128)(4,1)} %bitcast.62), calls=%async_computation.3 | async-start | bytes 8388608
  219.9 13.8 %slice-start.1 = ((s8[15925248]{0:T(1024)(128)(4,1)}), s8[4194304]{0:T(1024)(128)(4,1)S(1)}, s32[]{:S(2)}) async-start(s8[15925248]{0:T(1024)(128)(4,1)} %bitcast.62), calls=%async_computation.4 | async-start | bytes 8388608
  223.7 10.1 %slice-start.2 = ((s8[15925248]{0:T(1024)(128)(4,1)}), s8[4194304]{0:T(1024)(128)(4,1)S(1)}, s32[]{:S(2)}) async-start(s8[15925248]{0:T(1024)(128)(4,1)} %bitcast.62), calls=%async_computation.5 | async-start | bytes 8388608
  228.7 7.1 %copy-start.7 = (f32[1152,144]{0,1:T(8,128)}, f32[1152,144]{0,1:T(8,128)S(1)}, u32[]{:S(2)}) copy-start(f32[1152,144]{0,1:T(8,128)S(1)} %get-tuple-element.21) | copy-start | bytes 1990660
  228.7 7.1 %copy-start.8 = (f32[1152,144]{0,1:T(8,128)}, f32[1152,144]{0,1:T(8,128)S(1)}, u32[]{:S(2)}) copy-start(f32[1152,144]{0,1:T(8,128)S(1)} %get-tuple-element.22) | copy-start | bytes 1990660
  228.7 5.1 slice-start.3
  237.9 20.3 %collective-permute-start.4 = (f32[1152,144]{0,1:T(8,128)S(1)}, f32[1152,144]{0,1:T(8,128)S(1)}, u32[]{:S(2)}, u32[]{:S(2)}) collective-permute-start(f32[1152,144]{0,1:T(8,128)S(1)} %constant_dynamic-slice_fusion), channel_id=1, source_target_pairs={{0,16},{16,0},{1,17},{17,1},{2,18},{18,2},{3,19},{19,3},{4,20},{20... | collective-permute-start | bytes 1990664 | tf_op jit(solution)/shard_map/ppermute | solution.py:58
  239.5 3.7 collective-permute-start.5
  243.8 4.6 collective-permute-start.6
  249.1 3.7 collective-permute-start.7
  252.8 3.7 collective-permute-start.8
  256.5 1.2 collective-permute-start.9
  358.3 3.1 collective-permute-start.10
  369.7 143.6 %copy-start.2 = (f32[1152,144]{0,1:T(8,128)S(1)}, f32[1152,144]{0,1:T(8,128)}, u32[]{:S(2)}) copy-start(f32[1152,144]{0,1:T(8,128)} %fusion.34) | copy-start | bytes 1990660
  501.5 11.8 %copy-start = (f32[1152,2304]{0,1:T(8,128)S(1)}, f32[1152,2304]{0,1:T(8,128)}, u32[]{:S(2)}) copy-start(f32[1152,2304]{0,1:T(8,128)} %all-gather.8.cloned.1.call-done) | copy-start | bytes 31850500
  510.2 3.1 collective-permute-start.11
  (5 other events, 14.4 us)
Sparse Core Ops, SparseCore 0:
  12.3 186.2 all-gather.3
  218.0 131.8 all-gather.5
  369.8 131.6 all-gather.7

commit v11 on v9

--- a/solution.py
+++ b/solution.py
@@ -105,16 +105,15 @@
         hi, lo = split_bf16(block)
         return lax.all_gather(jnp.stack([hi, lo]), TS, axis=2, tiled=True)
 
-    def pair_dot(left_hi, left_lo, right, dims):
+    def quad_dot(split_left, right, axis):
         right_hi, right_lo = split_bf16(right)
         width = right.shape[1]
-        both = bf16_dot(left_hi, jnp.concatenate([right_hi, right_lo], axis=1), dims)
-        return both[:, :width] + both[:, width:] + bf16_dot(left_lo, right_hi, dims)
+        quads = bf16_dot(split_left, jnp.concatenate([right_hi, right_lo], axis=1), ((axis,), (0,)))
+        return quads[0, :, :width] + quads[0, :, width:] + quads[1, :, :width]
 
     def newton_products(split_rows, block):
-        rows_hi, rows_lo = split_rows[0], split_rows[1]
-        z_cols = shard_sum(pair_dot(rows_hi, rows_lo, block, ((0,), (0,))))
-        return pair_dot(rows_hi, rows_lo, z_cols, ((1,), (0,)))
+        z_cols = shard_sum(quad_dot(split_rows, block, 1))
+        return quad_dot(split_rows, z_cols, 2)
 
     def newton_step(iterate):
         return 1.5 * iterate - 0.5 * newton_products(gather_split_rows(iterate), iterate)
@@ -143,8 +142,8 @@
         stat_next = stat_decay * stat_left + (1.0 - stat_decay) / D * gram
         by_rows = ((1,), (0,))
         stat_hi, stat_lo = split_bf16(shard_concat(stat_next, c))
-        both = bf16_dot(hi_rows, jnp.concatenate([stat_hi, stat_lo], axis=1), by_rows)
-        power = both[:, :cols] + both[:, cols:] + bf16_dot(lo_rows, stat_hi, by_rows)
+        quads = bf16_dot(stacked[1:], jnp.concatenate([stat_hi, stat_lo], axis=1), ((2,), (0,)))
+        power = quads[0, :, :cols] + quads[0, :, cols:] + quads[1, :, :cols]
         power, stacked_later = lax.optimization_barrier((power, stacked))
         hi_later, lo_later = stacked_later[1], stacked_later[2]
         rotated = bf16_dot(hi_later, grad_cols, by_rows) + bf16_dot(lo_later, grad_cols, by_rows)

time: 525 us -> 526 us (level)
    dot_general x15 -> x10, matrix products: 50.3 us -> 46.5 us  [bf16_dot(): lax.dot_general(left, right, (dims, ((), ())), preferred_element_type=jnp...]
where the time goes in v11:
time: 526 us; the launch traced here: 525 us
  waiting for transfers between devices  434 us (83%)
  matrix products  50.3 us (10%)
  between operations  14.9 us (3%)
  other arithmetic  13.5 us (3%)
  local copies, waits for them, and re-layouts  7.54 us (1%)
  starting transfers between devices  5.44 us (1%)
    all_gather x2, waiting for transfers between devices, gather_split_rows(): return lax.all_gather(jnp.stack([hi, lo]), TS, axis=2, tiled=True)  223 us
    all_gather x1, waiting for transfers between devices, shards(): lax.all_gather(jnp.stack([grad, basis_hi, basis_lo]), TS, axis=2, tiled=T...  186 us
    dot_general x10, matrix products, bf16_dot(): lax.dot_general(left, right, (dims, ((), ())), preferred_element_type=jnp...  46.5 us
    ppermute x8, waiting for transfers between devices, partner(): return lax.ppermute(x, 'shard', [(0, 1), (1, 0)])  12.4 us
    ppermute x4, waiting for transfers between devices, all_sum(): x = x + lax.ppermute(x, TS, [(i, i ^ step) for i in range(n_ts)])  11.6 us
  transfers between devices with their start and end apart: 15, of which 14 were waited for; matrix products, arithmetic and copies ran while one was open for 4% of the time, Pallas kernels for 0%

profile of v11, /device:TPU:0, one launch (start us, length us, event | category | flops | bytes accessed | tf_op | source)
XLA Modules:
  0.0 525.4 jit_solution(4280981099713585914)
XLA Ops:
  11.4 186.3 %all-gather.4.cloned.1.call-done = bf16[3,1152,2304]{1,2,0:T(8,128)(2,1)} async-done(((bf16[3,1152,144]{1,2,0:T(8,128)(2,1)}), bf16[3,1152,2304]{1,2,0:T(8,128)(2,1)}) %all-gather.4.cloned.1.call-update) | async-done | bytes 15925264 | tf_op jit(solution)/shard_map/all_gather | solution.py:136
  197.7 2.5 slice-done.4
  201.4 2.1 collective-permute-done.1
  203.5 3.8 fusion.31
  207.5 2.0 collective-permute-done.2
  209.8 6.4 %fusion = f32[2,1152,288]{1,2,0:T(8,128)S(1)} fusion(bf16[3,1152,2304]{1,2,0:T(8,128)(2,1)} %all-gather.4.cloned.1.call-done, bf16[2304,144]{0,1:T(8,128)(2,1)S(1)} %get-tuple-element.22, bf16[2304,144]{0,1:T(8,128)(2,1)S(1)} %get-tuple-element.21), kind=kOutput, calls=%fused_computation | convolution fusion | flops 3060301824 | bytes 14598144 | tf_op jit(solution)/shard_map/dot_general | solution.py:43
  219.8 3.7 fusion.4
  223.6 5.0 multiply_add_fusion
  228.6 5.0 fusion.6
  233.7 2.0 fusion.19
  235.7 2.0 fusion.22
  238.7 3.7 collective-permute-done.5
  244.3 3.3 collective-permute-done.6
  249.6 2.3 collective-permute-done.7
  253.3 2.3 collective-permute-done.8
  258.3 91.6 %all-gather.6.cloned.1.call-done = bf16[2,1152,2304]{1,2,0:T(8,128)(2,1)} async-done(((bf16[2,1152,144]{1,2,0:T(8,128)(2,1)}), bf16[2,1152,2304]{1,2,0:T(8,128)(2,1)}) %all-gather.6.cloned.1.call-update) | async-done | bytes 10616848 | tf_op jit(solution)/shard_map/all_gather | solution.py:106
  349.9 6.4 %fusion.59 = f32[2,2304,288]{1,2,0:T(8,128)S(1)} fusion(bf16[2,1152,2304]{1,2,0:T(8,128)(2,1)} %all-gather.6.cloned.1.call-done, bf16[1152,144]{0,1:T(8,128)(2,1)S(1)} %get-tuple-element.28, bf16[1152,144]{0,1:T(8,128)(2,1)S(1)} %get-tuple-element.29), kind=kOutput, calls=%fused_computation.82 | convolution fusion | flops 3058974720 | bytes 16588800 | tf_op jit(solution)/shard_map/dot_general | solution.py:43
  359.8 2.5 collective-permute-done.10
  362.4 2.4 reduce-precision_convert_fusion.1
  364.8 6.3 %fusion.41 = f32[2,1152,288]{1,2,0:T(8,128)S(1)} fusion(bf16[2,1152,2304]{1,2,0:T(8,128)(2,1)} %all-gather.6.cloned.1.call-done, bf16[2304,144]{0,1:T(8,128)(2,1)S(1)} %get-tuple-element.20, bf16[2304,144]{0,1:T(8,128)(2,1)S(1)} %get-tuple-element.19), kind=kOutput, calls=%fused_computation.44 | convolution fusion | flops 3060301824 | bytes 14598144 | tf_op jit(solution)/shard_map/dot_general | solution.py:43
  372.4 131.8 %all-gather.8.cloned.1.call-done = bf16[2,1152,2304]{1,2,0:T(8,128)(2,1)} async-done(((bf16[2,1152,144]{1,2,0:T(8,128)(2,1)}), bf16[2,1152,2304]{1,2,0:T(8,128)(2,1)}) %all-gather.8.cloned.1.call-update) | async-done | bytes 10616848 | tf_op jit(solution)/shard_map/all_gather | solution.py:106
  504.2 6.4 %fusion.62 = f32[2,2304,288]{1,2,0:T(8,128)S(1)} fusion(bf16[2,1152,2304]{1,2,0:T(8,128)(2,1)} %all-gather.8.cloned.1.call-done, bf16[1152,144]{0,1:T(8,128)(2,1)S(1)} %fusion.50, bf16[1152,144]{0,1:T(8,128)(2,1)S(1)} %get-tuple-element.15), kind=kOutput, calls=%fused_computation.87 | convolution fusion | flops 3058974720 | bytes 16588800 | tf_op jit(solution)/shard_map/dot_general | solution.py:43
  510.9 3.0 collective-permute-done.11
  514.6 3.3 fusion.44
  (77 shorter events, 24.3 us)
Async XLA Ops:
  7.2 190.5 %all-gather.4.cloned.1.call-start = ((), (), s32[]{:S(2)}) async-start(), calls=%async_computation | async-start | bytes 16920576 | tf_op jit(solution)/shard_map/all_gather | solution.py:136
  8.3 1.8 collective-permute-start
  11.3 338.6 %all-gather.6.cloned.1.call-start = ((), (), s32[]{:S(2)}) async-start(), calls=%async_computation.1 | async-start | bytes 11280384 | tf_op jit(solution)/shard_map/all_gather | solution.py:106
  201.3 2.2 collective-permute-start.1
  207.3 2.2 collective-permute-start.2
  218.0 286.2 %all-gather.8.cloned.1.call-start = ((), (), s32[]{:S(2)}) async-start(), calls=%async_computation.2 | async-start | bytes 11280384 | tf_op jit(solution)/shard_map/all_gather | solution.py:106
  218.0 1.7 collective-permute-start.3
  219.7 3.8 copy-start.4
  219.7 3.8 copy-start.5
  219.8 13.8 %slice-start = ((s8[15925248]{0:T(1024)(128)(4,1)}), s8[4194304]{0:T(1024)(128)(4,1)S(1)}, s32[]{:S(2)}) async-start(s8[15925248]{0:T(1024)(128)(4,1)} %bitcast.94), calls=%async_computation.3 | async-start | bytes 8388608
  219.8 13.8 %slice-start.1 = ((s8[15925248]{0:T(1024)(128)(4,1)}), s8[4194304]{0:T(1024)(128)(4,1)S(1)}, s32[]{:S(2)}) async-start(s8[15925248]{0:T(1024)(128)(4,1)} %bitcast.94), calls=%async_computation.4 | async-start | bytes 8388608
  223.6 10.1 %slice-start.2 = ((s8[15925248]{0:T(1024)(128)(4,1)}), s8[4194304]{0:T(1024)(128)(4,1)S(1)}, s32[]{:S(2)}) async-start(s8[15925248]{0:T(1024)(128)(4,1)} %bitcast.94), calls=%async_computation.5 | async-start | bytes 8388608
  228.6 7.1 %copy-start.6 = (f32[1152,144]{0,1:T(8,128)}, f32[1152,144]{0,1:T(8,128)S(1)}, u32[]{:S(2)}) copy-start(f32[1152,144]{0,1:T(8,128)S(1)} %get-tuple-element.30) | copy-start | bytes 1990660
  228.6 7.1 %copy-start.7 = (f32[1152,144]{0,1:T(8,128)}, f32[1152,144]{0,1:T(8,128)S(1)}, u32[]{:S(2)}) copy-start(f32[1152,144]{0,1:T(8,128)S(1)} %get-tuple-element.31) | copy-start | bytes 1990660
  228.6 5.1 slice-start.3
  237.8 19.6 %collective-permute-start.4 = (f32[1152,144]{0,1:T(8,128)S(1)}, f32[1152,144]{0,1:T(8,128)S(1)}, u32[]{:S(2)}, u32[]{:S(2)}) collective-permute-start(f32[1152,144]{0,1:T(8,128)S(1)} %constant_dynamic-slice_fusion), channel_id=1, source_target_pairs={{0,16},{16,0},{1,17},{17,1},{2,18},{18,2},{3,19},{19,3},{4,20},{20... | collective-permute-start | bytes 1990664 | tf_op jit(solution)/shard_map/ppermute | solution.py:58
  238.6 3.8 collective-permute-start.5
  243.0 4.6 collective-permute-start.6
  248.3 3.7 collective-permute-start.7
  251.9 3.7 collective-permute-start.8
  255.6 1.2 collective-permute-start.9
  359.1 3.3 collective-permute-start.10
  510.6 4.0 copy-start.3
  510.8 3.1 collective-permute-start.11
  (4 other events, 10.5 us)
Sparse Core Ops, SparseCore 0:
  11.4 186.2 all-gather.3
  218.1 131.7 all-gather.5
  372.5 131.6 all-gather.7

commit v12 on v10

--- a/solution.py
+++ b/solution.py
@@ -123,7 +123,11 @@
         basis_hi, basis_lo = split_bf16(basis_left)
         stacked = lax.all_gather(jnp.stack([grad, basis_hi, basis_lo]), TS, axis=2, tiled=True)
         grad_rows, hi_rows, lo_rows = stacked[0], stacked[1], stacked[2]
-        grad_krows = block_rows(grad_rows, k, c)
+        if cols <= rows and pair:
+            piece = lax.dynamic_slice(stacked, (0, (k * cols) % rows, 0), (1, cols, D))[0]
+            grad_krows = jnp.where((k * cols) // rows == c, piece, partner(piece))
+        else:
+            grad_krows = block_rows(grad_rows, k, c)
         gram = lax.dot_general(
             grad_rows, grad_krows, (((1,), (1,)), ((), ())), preferred_element_type=jnp.float32
         )

time: 525 us -> 524 us (level)
  no operation moved by 1% of the time
where the time goes in v12:
time: 524 us; the launch traced here: 523 us
  waiting for transfers between devices  432 us (82%)
  matrix products  57.4 us (11%)
  between operations  14.8 us (3%)
  other arithmetic  7.58 us (1%)
  starting transfers between devices  6.04 us (1%)
    all_gather x1, waiting for transfers between devices, shards(): lax.all_gather(jnp.stack([grad, basis_hi, basis_lo]), TS, axis=2, tiled=T...  186 us
    all_gather x1, waiting for transfers between devices, newton_step(): iterate_rows = lax.all_gather(iterate, TS, axis=1, tiled=True)  132 us
    all_gather x1, waiting for transfers between devices, shards(): power_rows = lax.all_gather(power, TS, axis=1, tiled=True)  90.8 us
    dot_general x6, matrix products, bf16_dot(): lax.dot_general(left, right, (dims, ((), ())), preferred_element_type=jnp...  24.1 us
    dot_general x2, matrix products, contract_rows(): lax.dot_general(left, right, (((0,), (0,)), ((), ())), precision=lax.Prec...  17.1 us
    dot_general x2, matrix products, exact_dot(): jnp.dot(left, right, precision=lax.Precision.HIGH, preferred_element_type...  12.6 us
    ppermute x8, waiting for transfers between devices, partner(): return lax.ppermute(x, 'shard', [(0, 1), (1, 0)])  12.2 us
    ppermute x4, waiting for transfers between devices, all_sum(): x = x + lax.ppermute(x, TS, [(i, i ^ step) for i in range(n_ts)])  11.2 us
  transfers between devices with their start and end apart: 15, of which 14 were waited for; matrix products, arithmetic and copies ran while one was open for 4% of the time, Pallas kernels for 0%

profile of v12, /device:TPU:0, one launch (start us, length us, event | category | flops | bytes accessed | tf_op | source)
XLA Modules:
  0.0 523.1 jit_solution(11538976663344151876)
XLA Ops:
  12.3 186.3 %all-gather.4.cloned.1.call-done = bf16[3,1152,2304]{1,2,0:T(8,128)(2,1)} async-done(((bf16[3,1152,144]{1,2,0:T(8,128)(2,1)}), bf16[3,1152,2304]{1,2,0:T(8,128)(2,1)}) %all-gather.4.cloned.1.call-update) | async-done | bytes 15925264 | tf_op jit(solution)/shard_map/all_gather | solution.py:124
  198.6 2.0 constant_dynamic-slice_fusion.1
  201.3 2.1 collective-permute-done.1
  203.4 3.6 fusion.28
  207.3 2.0 collective-permute-done.2
  209.5 6.4 %fusion = f32[2,1152,288]{1,2,0:T(8,128)S(1)} fusion(bf16[3,1152,2304]{1,2,0:T(8,128)(2,1)} %all-gather.4.cloned.1.call-done, bf16[2304,144]{0,1:T(8,128)(2,1)S(1)} %get-tuple-element.16, bf16[2304,144]{0,1:T(8,128)(2,1)S(1)} %get-tuple-element.15), kind=kOutput, calls=%fused_computation | convolution fusion | flops 3060301824 | bytes 14598144 | tf_op jit(solution)/shard_map/dot_general | solution.py:43
  217.3 1.5 collective-permute-done.3
  218.9 3.7 fusion.5
  222.6 5.0 multiply_add_fusion
  227.7 5.0 fusion.7
  232.7 2.0 fusion.18
  234.7 2.0 fusion.21
  238.5 3.6 collective-permute-done.5
  244.2 3.2 collective-permute-done.6
  249.5 2.3 collective-permute-done.7
  253.2 2.2 collective-permute-done.8
  258.1 90.8 %all-gather.6.cloned.1.call-done = f32[1152,2304]{0,1:T(8,128)} async-done(((f32[1152,144]{0,1:T(8,128)}), f32[1152,2304]{0,1:T(8,128)}) %all-gather.6.cloned.1.call-update) | async-done | bytes 10616848 | tf_op jit(solution)/shard_map/all_gather | solution.py:146
  348.8 8.4 %fusion.53 = f32[2304,144]{0,1:T(8,128)S(1)} fusion(f32[1152,2304]{0,1:T(8,128)} %all-gather.6.cloned.1.call-done, f32[1152,144]{0,1:T(8,128)S(1)} %copy-done.1), kind=kOutput, calls=%fused_computation.74 | convolution fusion | flops 2293235712 | bytes 12607488 | tf_op jit(solution)/shard_map/dot_general | solution.py:28
  358.0 2.3 collective-permute-done.10
  360.4 8.3 %fusion.29 = f32[1152,144]{0,1:T(8,128)} fusion(f32[1152,2304]{0,1:T(8,128)} %all-gather.6.cloned.1.call-done, f32[2304,144]{0,1:T(8,128)S(1)} %fusion.53, f32[2304,144]{0,1:T(8,128)S(1)} %collective-permute-done.10, f32[1152,144]{0,1:T(8,128)S(1)} %copy-done.1, f32[]{:T(128)S(6)} %mul.108, f32[]{:T(128)S(6)} %mul.103), kind=kOutput, calls=%fused_computation.26 | convolution fusion | flops 2294065152 | bytes 14598152 | tf_op jit(solution)/shard_map/dot_general | solution.py:24
  368.6 131.8 %all-gather.8.cloned.1.call-done = f32[1152,2304]{0,1:T(8,128)} async-done(((f32[1152,144]{0,1:T(8,128)}), f32[1152,2304]{0,1:T(8,128)}) %all-gather.8.cloned.1.call-update) | async-done | bytes 10616848 | tf_op jit(solution)/shard_map/all_gather | solution.py:105
  500.4 8.6 %fusion.54 = f32[2304,144]{0,1:T(8,128)S(1)} fusion(f32[1152,2304]{0,1:T(8,128)} %all-gather.8.cloned.1.call-done, f32[1152,144]{0,1:T(8,128)} %fusion.29), kind=kOutput, calls=%fused_computation.75 | convolution fusion | flops 2293235712 | bytes 12607488 | tf_op jit(solution)/shard_map/dot_general | solution.py:28
  509.2 3.0 collective-permute-done.11
  512.2 4.3 multiply_subtract_fusion
  (67 shorter events, 17.8 us)
Async XLA Ops:
  7.2 191.5 %all-gather.4.cloned.1.call-start = ((), (), s32[]{:S(2)}) async-start(), calls=%async_computation | async-start | bytes 16920576 | tf_op jit(solution)/shard_map/all_gather | solution.py:124
  8.2 1.8 collective-permute-start
  12.2 191.2 %copy-start.4 = (f32[1152,144]{0,1:T(8,128)S(1)}, f32[1152,144]{0,1:T(8,128)}, u32[]{:S(2)}) copy-start(f32[1152,144]{0,1:T(8,128)} %param.8) | copy-start | bytes 1990660
  12.2 336.6 %all-gather.6.cloned.1.call-start = ((), (), s32[]{:S(2)}) async-start(), calls=%async_computation.1 | async-start | bytes 11280384 | tf_op jit(solution)/shard_map/all_gather | solution.py:146
  201.2 2.2 collective-permute-start.1
  207.1 2.2 collective-permute-start.2
  216.8 283.6 %all-gather.8.cloned.1.call-start = ((), (), s32[]{:S(2)}) async-start(), calls=%async_computation.2 | async-start | bytes 11280384 | tf_op jit(solution)/shard_map/all_gather | solution.py:105
  217.1 1.7 collective-permute-start.3
  218.8 13.8 %slice-start = ((s8[15925248]{0:T(1024)(128)(4,1)}), s8[4194304]{0:T(1024)(128)(4,1)S(1)}, s32[]{:S(2)}) async-start(s8[15925248]{0:T(1024)(128)(4,1)} %bitcast.63), calls=%async_computation.3 | async-start | bytes 8388608
  218.9 13.8 %slice-start.1 = ((s8[15925248]{0:T(1024)(128)(4,1)}), s8[4194304]{0:T(1024)(128)(4,1)S(1)}, s32[]{:S(2)}) async-start(s8[15925248]{0:T(1024)(128)(4,1)} %bitcast.63), calls=%async_computation.4 | async-start | bytes 8388608
  222.6 10.1 %slice-start.2 = ((s8[15925248]{0:T(1024)(128)(4,1)}), s8[4194304]{0:T(1024)(128)(4,1)S(1)}, s32[]{:S(2)}) async-start(s8[15925248]{0:T(1024)(128)(4,1)} %bitcast.63), calls=%async_computation.5 | async-start | bytes 8388608
  227.6 7.1 %copy-start.7 = (f32[1152,144]{0,1:T(8,128)}, f32[1152,144]{0,1:T(8,128)S(1)}, u32[]{:S(2)}) copy-start(f32[1152,144]{0,1:T(8,128)S(1)} %get-tuple-element.21) | copy-start | bytes 1990660
  227.6 7.1 %copy-start.8 = (f32[1152,144]{0,1:T(8,128)}, f32[1152,144]{0,1:T(8,128)S(1)}, u32[]{:S(2)}) copy-start(f32[1152,144]{0,1:T(8,128)S(1)} %get-tuple-element.22) | copy-start | bytes 1990660
  227.6 5.1 slice-start.3
  236.8 20.3 %collective-permute-start.4 = (f32[1152,144]{0,1:T(8,128)S(1)}, f32[1152,144]{0,1:T(8,128)S(1)}, u32[]{:S(2)}, u32[]{:S(2)}) collective-permute-start(f32[1152,144]{0,1:T(8,128)S(1)} %constant_dynamic-slice_fusion), channel_id=1, source_target_pairs={{0,16},{16,0},{1,17},{17,1},{2,18},{18,2},{3,19},{19,3},{4,20},{20... | collective-permute-start | bytes 1990664 | tf_op jit(solution)/shard_map/ppermute | solution.py:58
  238.4 3.7 collective-permute-start.5
  242.8 4.6 collective-permute-start.6
  248.0 3.7 collective-permute-start.7
  251.7 3.7 collective-permute-start.8
  255.4 1.2 collective-permute-start.9
  357.2 3.1 collective-permute-start.10
  368.6 143.6 %copy-start.2 = (f32[1152,144]{0,1:T(8,128)S(1)}, f32[1152,144]{0,1:T(8,128)}, u32[]{:S(2)}) copy-start(f32[1152,144]{0,1:T(8,128)} %fusion.29) | copy-start | bytes 1990660
  500.4 11.8 %copy-start = (f32[1152,2304]{0,1:T(8,128)S(1)}, f32[1152,2304]{0,1:T(8,128)}, u32[]{:S(2)}) copy-start(f32[1152,2304]{0,1:T(8,128)} %all-gather.8.cloned.1.call-done) | copy-start | bytes 31850500
  509.1 3.1 collective-permute-start.11
  (4 other events, 12.3 us)
Sparse Core Ops, SparseCore 0:
  12.3 186.2 all-gather.3
  217.0 131.8 all-gather.5
  368.8 131.6 all-gather.7

commit v13 on v12

--- a/solution.py
+++ b/solution.py
@@ -133,7 +133,8 @@
         )
         stat_next = stat_decay * stat_left + (1.0 - stat_decay) / D * gram
         by_rows = ((1,), (0,))
-        stat_hi, stat_lo = split_bf16(shard_concat(stat_next, c))
+        stat_hi, stat_lo = split_bf16(stat_next)
+        stat_hi, stat_lo = shard_concat(stat_hi, c), shard_concat(stat_lo, c)
         quads = bf16_dot(stacked[1:], jnp.concatenate([stat_hi, stat_lo], axis=1), ((2,), (0,)))
         power = quads[0, :, :cols] + quads[0, :, cols:] + quads[1, :, :cols]
         power, stacked_later = lax.optimization_barrier((power, stacked))

time: 524 us -> 524 us (level)
    ppermute x8 -> x9, waiting for transfers between devices: 12.2 us -> 11.8 us  [partner(): return lax.ppermute(x, 'shard', [(0, 1), (1, 0)])]
  transfers between devices with their start and end apart: 15 -> 16, of which waited for: 14 -> 15; matrix products, arithmetic and copies ran while one was open for 4% -> 4% of each run, Pallas kernels for 0% -> 0%
where the time goes in v13:
time: 524 us
  waiting for transfers between devices  432 us (82%)
  matrix products  58.2 us (11%)
  between operations  14.8 us (3%)
  other arithmetic  7.51 us (1%)
  starting transfers between devices  6.4 us (1%)
    all_gather x1, waiting for transfers between devices, shards(): lax.all_gather(jnp.stack([grad, basis_hi, basis_lo]), TS, axis=2, tiled=T...  186 us
    all_gather x1, waiting for transfers between devices, newton_step(): iterate_rows = lax.all_gather(iterate, TS, axis=1, tiled=True)  132 us
    all_gather x1, waiting for transfers between devices, shards(): power_rows = lax.all_gather(power, TS, axis=1, tiled=True)  90.8 us
    dot_general x6, matrix products, bf16_dot(): lax.dot_general(left, right, (dims, ((), ())), preferred_element_type=jnp...  24 us
    dot_general x2, matrix products, contract_rows(): lax.dot_general(left, right, (((0,), (0,)), ((), ())), precision=lax.Prec...  17.1 us
    dot_general x2, matrix products, exact_dot(): jnp.dot(left, right, precision=lax.Precision.HIGH, preferred_element_type...  12.6 us
    ppermute x9, waiting for transfers between devices, partner(): return lax.ppermute(x, 'shard', [(0, 1), (1, 0)])  11.8 us
    ppermute x4, waiting for transfers between devices, all_sum(): x = x + lax.ppermute(x, TS, [(i, i ^ step) for i in range(n_ts)])  11.2 us
  transfers between devices with their start and end apart: 16, of which 15 were waited for; matrix products, arithmetic and copies ran while one was open for 4% of the time, Pallas kernels for 0%

profile of v13, /device:TPU:0, one launch (start us, length us, event | category | flops | bytes accessed | tf_op | source)
XLA Modules:
  0.0 523.7 jit_solution(11189854266160847681)
XLA Ops:
  12.3 186.3 %all-gather.4.cloned.1.call-done = bf16[3,1152,2304]{1,2,0:T(8,128)(2,1)} async-done(((bf16[3,1152,144]{1,2,0:T(8,128)(2,1)}), bf16[3,1152,2304]{1,2,0:T(8,128)(2,1)}) %all-gather.4.cloned.1.call-update) | async-done | bytes 15925264 | tf_op jit(solution)/shard_map/all_gather | solution.py:124
  198.6 2.0 constant_dynamic-slice_fusion.1
  201.3 2.1 collective-permute-done.1
  203.4 4.5 reduce-precision_convert_fusion.1
  210.1 6.4 %fusion = f32[2,1152,288]{1,2,0:T(8,128)S(1)} fusion(bf16[3,1152,2304]{1,2,0:T(8,128)(2,1)} %all-gather.4.cloned.1.call-done, bf16[1152,144]{0,1:T(8,128)(2,1)S(1)} %get-tuple-element.26, bf16[1152,144]{0,1:T(8,128)(2,1)S(1)} %get-tuple-element.25, bf16[1152,144]{0,1:T(8,128)(2,1)S(1)} %get-tuple-element.22, bf16[1152,144]{0,1:T(8,128)(2,1)S(1)} %get-tuple-element.21), kind=kOutput, calls=%fused_computation | convolution fusion | flops 3062956032 | bytes 14598144 | tf_op jit(solution)/shard_map/dot_general | solution.py:43
  217.8 1.5 collective-permute-done.4
  219.4 3.7 fusion.5
  223.2 5.0 multiply_add_fusion
  228.2 5.0 fusion.7
  233.3 2.0 fusion.18
  235.3 2.0 fusion.21
  239.1 3.6 collective-permute-done.6
  244.7 3.2 collective-permute-done.7
  248.6 1.5 collective-permute-start.8
  250.1 2.2 collective-permute-done.8
  253.8 2.2 collective-permute-done.9
  258.6 90.8 %all-gather.6.cloned.1.call-done = f32[1152,2304]{0,1:T(8,128)} async-done(((f32[1152,144]{0,1:T(8,128)}), f32[1152,2304]{0,1:T(8,128)}) %all-gather.6.cloned.1.call-update) | async-done | bytes 10616848 | tf_op jit(solution)/shard_map/all_gather | solution.py:147
  349.4 8.4 %fusion.57 = f32[2304,144]{0,1:T(8,128)S(1)} fusion(f32[1152,2304]{0,1:T(8,128)} %all-gather.6.cloned.1.call-done, f32[1152,144]{0,1:T(8,128)S(1)} %copy-done.1), kind=kOutput, calls=%fused_computation.79 | convolution fusion | flops 2293235712 | bytes 12607488 | tf_op jit(solution)/shard_map/dot_general | solution.py:28
  358.5 2.4 collective-permute-done.11
  360.9 8.3 %fusion.29 = f32[1152,144]{0,1:T(8,128)} fusion(f32[1152,2304]{0,1:T(8,128)} %all-gather.6.cloned.1.call-done, f32[2304,144]{0,1:T(8,128)S(1)} %fusion.57, f32[2304,144]{0,1:T(8,128)S(1)} %collective-permute-done.11, f32[1152,144]{0,1:T(8,128)S(1)} %copy-done.1, f32[]{:T(128)S(6)} %mul.108, f32[]{:T(128)S(6)} %mul.103), kind=kOutput, calls=%fused_computation.26 | convolution fusion | flops 2294065152 | bytes 14598152 | tf_op jit(solution)/shard_map/dot_general | solution.py:24
  369.2 131.8 %all-gather.8.cloned.1.call-done = f32[1152,2304]{0,1:T(8,128)} async-done(((f32[1152,144]{0,1:T(8,128)}), f32[1152,2304]{0,1:T(8,128)}) %all-gather.8.cloned.1.call-update) | async-done | bytes 10616848 | tf_op jit(solution)/shard_map/all_gather | solution.py:105
  501.0 8.6 %fusion.58 = f32[2304,144]{0,1:T(8,128)S(1)} fusion(f32[1152,2304]{0,1:T(8,128)} %all-gather.8.cloned.1.call-done, f32[1152,144]{0,1:T(8,128)} %fusion.29), kind=kOutput, calls=%fused_computation.80 | convolution fusion | flops 2293235712 | bytes 12607488 | tf_op jit(solution)/shard_map/dot_general | solution.py:28
  509.8 3.0 collective-permute-done.12
  512.8 4.3 multiply_subtract_fusion
  (67 shorter events, 18.1 us)
Async XLA Ops:
  7.2 191.5 %all-gather.4.cloned.1.call-start = ((), (), s32[]{:S(2)}) async-start(), calls=%async_computation | async-start | bytes 16920576 | tf_op jit(solution)/shard_map/all_gather | solution.py:124
  8.2 1.8 collective-permute-start
  12.2 191.2 %copy-start.3 = (f32[1152,144]{0,1:T(8,128)S(1)}, f32[1152,144]{0,1:T(8,128)}, u32[]{:S(2)}) copy-start(f32[1152,144]{0,1:T(8,128)} %param.8) | copy-start | bytes 1990660
  12.2 337.2 %all-gather.6.cloned.1.call-start = ((), (), s32[]{:S(2)}) async-start(), calls=%async_computation.1 | async-start | bytes 11280384 | tf_op jit(solution)/shard_map/all_gather | solution.py:147
  201.2 2.2 collective-permute-start.1
  207.9 1.6 collective-permute-start.2
  208.0 2.0 collective-permute-start.3
  217.4 283.6 %all-gather.8.cloned.1.call-start = ((), (), s32[]{:S(2)}) async-start(), calls=%async_computation.2 | async-start | bytes 11280384 | tf_op jit(solution)/shard_map/all_gather | solution.py:105
  217.6 1.7 collective-permute-start.4
  219.4 13.8 %slice-start = ((s8[15925248]{0:T(1024)(128)(4,1)}), s8[4194304]{0:T(1024)(128)(4,1)S(1)}, s32[]{:S(2)}) async-start(s8[15925248]{0:T(1024)(128)(4,1)} %bitcast.67), calls=%async_computation.3 | async-start | bytes 8388608
  219.4 13.8 %slice-start.1 = ((s8[15925248]{0:T(1024)(128)(4,1)}), s8[4194304]{0:T(1024)(128)(4,1)S(1)}, s32[]{:S(2)}) async-start(s8[15925248]{0:T(1024)(128)(4,1)} %bitcast.67), calls=%async_computation.4 | async-start | bytes 8388608
  223.2 10.1 %slice-start.2 = ((s8[15925248]{0:T(1024)(128)(4,1)}), s8[4194304]{0:T(1024)(128)(4,1)S(1)}, s32[]{:S(2)}) async-start(s8[15925248]{0:T(1024)(128)(4,1)} %bitcast.67), calls=%async_computation.5 | async-start | bytes 8388608
  228.2 7.1 %copy-start.6 = (f32[1152,144]{0,1:T(8,128)}, f32[1152,144]{0,1:T(8,128)S(1)}, u32[]{:S(2)}) copy-start(f32[1152,144]{0,1:T(8,128)S(1)} %get-tuple-element.17) | copy-start | bytes 1990660
  228.2 7.1 %copy-start.7 = (f32[1152,144]{0,1:T(8,128)}, f32[1152,144]{0,1:T(8,128)S(1)}, u32[]{:S(2)}) copy-start(f32[1152,144]{0,1:T(8,128)S(1)} %get-tuple-element.18) | copy-start | bytes 1990660
  237.4 20.3 %collective-permute-start.5 = (f32[1152,144]{0,1:T(8,128)S(1)}, f32[1152,144]{0,1:T(8,128)S(1)}, u32[]{:S(2)}, u32[]{:S(2)}) collective-permute-start(f32[1152,144]{0,1:T(8,128)S(1)} %constant_dynamic-slice_fusion), channel_id=1, source_target_pairs={{0,16},{16,0},{1,17},{17,1},{2,18},{18,2},{3,19},{19,3},{4,20},{20... | collective-permute-start | bytes 1990664 | tf_op jit(solution)/shard_map/ppermute | solution.py:58
  239.0 3.7 collective-permute-start.6
  243.3 4.6 collective-permute-start.7
  248.6 3.7 collective-permute-start.8
  252.3 3.7 collective-permute-start.9
  256.0 1.2 collective-permute-start.10
  357.8 3.1 collective-permute-start.11
  369.2 143.6 %copy-start.2 = (f32[1152,144]{0,1:T(8,128)S(1)}, f32[1152,144]{0,1:T(8,128)}, u32[]{:S(2)}) copy-start(f32[1152,144]{0,1:T(8,128)} %fusion.29) | copy-start | bytes 1990660
  501.0 11.8 %copy-start = (f32[1152,2304]{0,1:T(8,128)S(1)}, f32[1152,2304]{0,1:T(8,128)}, u32[]{:S(2)}) copy-start(f32[1152,2304]{0,1:T(8,128)} %all-gather.8.cloned.1.call-done) | copy-start | bytes 31850500
  509.7 3.1 collective-permute-start.12
  (4 other events, 15.0 us)
Sparse Core Ops, SparseCore 0:
  12.3 186.2 all-gather.3
  217.5 131.8 all-gather.5
  369.3 131.6 all-gather.7

commit v14 on v12

--- a/solution.py
+++ b/solution.py
@@ -101,10 +101,17 @@
             x = lax.psum(x, TS)
         return shard_sum(x)[0, 0]
 
+    def newton_products(rows_all, block):
+        half = cols // 2
+        parts = []
+        for lo_col in (0, half):
+            z_half = shard_sum(contract_rows(rows_all, block[:, lo_col:lo_col + half]))
+            parts.append(exact_dot(rows_all, z_half))
+        return jnp.concatenate(parts, axis=1)
+
     def newton_step(iterate):
         iterate_rows = lax.all_gather(iterate, TS, axis=1, tiled=True)
-        z_cols = shard_sum(contract_rows(iterate_rows, iterate))
-        return 1.5 * iterate - 0.5 * exact_dot(iterate_rows, z_cols)
+        return 1.5 * iterate - 0.5 * newton_products(iterate_rows, iterate)
 
     def shards(grad_parts, moment, second, stat_left, basis_left):
         c = lax.axis_index("shard")
@@ -146,9 +153,8 @@
         power_rows = lax.all_gather(power, TS, axis=1, tiled=True)
         total_sq = all_sum(jnp.sum(power * power))
         power_rows, update, total_sq = lax.optimization_barrier((power_rows, update, total_sq))
-        z_cols = shard_sum(contract_rows(power_rows, power))
         scale = shrink * jnp.sqrt(D / (total_sq + norm_eps))
-        iterate = (1.5 * scale) * power - (0.5 * scale * scale * scale) * exact_dot(power_rows, z_cols)
+        iterate = (1.5 * scale) * power - (0.5 * scale * scale * scale) * newton_products(power_rows, power)
         for turn in range(NS_ITERS - 1):
             iterate = newton_step(iterate)
         return (update, moment_next, second_next, stat_next, iterate)

time: 524 us -> 540 us (1.031)
  matrix products: 57.4 us -> 72.1 us
    dot_general x2 -> x4, matrix products: 17.1 us -> 27.4 us  [contract_rows(): lax.dot_general(left, right, (((0,), (0,)), ((), ())), precision=lax.Prec...]
    ppermute x8 -> x10, waiting for transfers between devices: 12.2 us -> 6.81 us  [partner(): return lax.ppermute(x, 'shard', [(0, 1), (1, 0)])]
    dot_general x2 -> x4, matrix products: 12.6 us -> 17.3 us  [exact_dot(): jnp.dot(left, right, precision=lax.Precision.HIGH, preferred_element_type...]
  transfers between devices with their start and end apart: 15 -> 17, of which waited for: 14 -> 12; matrix products, arithmetic and copies ran while one was open for 4% -> 8% of each run, Pallas kernels for 0% -> 0%
where the time goes in v14:
time: 540 us; the launch traced here: 536 us
  waiting for transfers between devices  427 us (79%)
  matrix products  72.1 us (13%)
  between operations  15.4 us (3%)
  other arithmetic  9.52 us (2%)
  starting transfers between devices  7.09 us (1%)
    all_gather x1, waiting for transfers between devices, shards(): lax.all_gather(jnp.stack([grad, basis_hi, basis_lo]), TS, axis=2, tiled=T...  186 us
    all_gather x1, waiting for transfers between devices, newton_step(): iterate_rows = lax.all_gather(iterate, TS, axis=1, tiled=True)  132 us
    all_gather x1, waiting for transfers between devices, shards(): power_rows = lax.all_gather(power, TS, axis=1, tiled=True)  91.1 us
    dot_general x4, matrix products, contract_rows(): lax.dot_general(left, right, (((0,), (0,)), ((), ())), precision=lax.Prec...  27.4 us
    dot_general x6, matrix products, bf16_dot(): lax.dot_general(left, right, (dims, ((), ())), preferred_element_type=jnp...  23.8 us
    dot_general x4, matrix products, exact_dot(): jnp.dot(left, right, precision=lax.Precision.HIGH, preferred_element_type...  17.3 us
    ppermute x4, waiting for transfers between devices, all_sum(): x = x + lax.ppermute(x, TS, [(i, i ^ step) for i in range(n_ts)])  11.2 us
  transfers between devices with their start and end apart: 17, of which 12 were waited for; matrix products, arithmetic and copies ran while one was open for 8% of the time, Pallas kernels for 0%

profile of v14, /device:TPU:0, one launch (start us, length us, event | category | flops | bytes accessed | tf_op | source)
XLA Modules:
  0.0 536.5 jit_solution(17792067071312335014)
XLA Ops:
  12.3 186.3 %all-gather.4.cloned.1.call-done = bf16[3,1152,2304]{1,2,0:T(8,128)(2,1)} async-done(((bf16[3,1152,144]{1,2,0:T(8,128)(2,1)}), bf16[3,1152,2304]{1,2,0:T(8,128)(2,1)}) %all-gather.4.cloned.1.call-update) | async-done | bytes 15925264 | tf_op jit(solution)/shard_map/all_gather | solution.py:131
  198.7 2.0 constant_dynamic-slice_fusion.1
  201.4 2.1 collective-permute-done.1
  203.5 3.6 fusion.28
  209.6 6.4 %fusion = f32[2,1152,288]{1,2,0:T(8,128)S(1)} fusion(bf16[3,1152,2304]{1,2,0:T(8,128)(2,1)} %all-gather.4.cloned.1.call-done, bf16[2304,144]{0,1:T(8,128)(2,1)S(1)} %get-tuple-element.16, bf16[2304,144]{0,1:T(8,128)(2,1)S(1)} %get-tuple-element.15), kind=kOutput, calls=%fused_computation | convolution fusion | flops 3060301824 | bytes 14598144 | tf_op jit(solution)/shard_map/dot_general | solution.py:43
  219.0 3.7 fusion.5
  222.7 4.7 multiply_add_fusion
  227.5 5.0 fusion.7
  232.5 2.0 fusion.18
  234.6 2.0 fusion.21
  238.3 3.6 collective-permute-done.5
  244.0 3.1 collective-permute-done.6
  249.3 2.2 collective-permute-done.7
  252.9 2.2 collective-permute-done.8
  257.8 91.1 %all-gather.6.cloned.1.call-done = f32[1152,2304]{0,1:T(8,128)} async-done(((f32[1152,144]{0,1:T(8,128)}), f32[1152,2304]{0,1:T(8,128)}) %all-gather.6.cloned.1.call-update) | async-done | bytes 10616848 | tf_op jit(solution)/shard_map/all_gather | solution.py:153
  348.9 9.4 %fusion.58 = f32[2304,72]{0,1:T(8,128)} fusion(f32[1152,2304]{0,1:T(8,128)} %all-gather.6.cloned.1.call-done, f32[1152,144]{0,1:T(8,128)S(1)} %copy-done.2), kind=kOutput, calls=%fused_computation.72 | convolution fusion | flops 1146617856 | bytes 11612160 | tf_op jit(solution)/shard_map/dot_general | solution.py:28
  358.3 4.7 fusion.56
  364.3 7.3 %fusion.45 = f32[1152,72]{0,1:T(8,128)S(1)} fusion(f32[1152,2304]{0,1:T(8,128)} %all-gather.6.cloned.1.call-done, f32[2304,72]{0,1:T(8,128)} %fusion.58, f32[2304,72]{0,1:T(8,128)} %collective-permute-done.10), kind=kOutput, calls=%fused_computation.56 | convolution fusion | flops 1146783744 | bytes 12275712 | tf_op jit(solution)/shard_map/dot_general | solution.py:24
  371.8 4.1 fusion.43
  376.8 131.8 %all-gather.8.cloned.1.call-done = f32[1152,2304]{0,1:T(8,128)} async-done(((f32[1152,144]{0,1:T(8,128)}), f32[1152,2304]{0,1:T(8,128)}) %all-gather.8.cloned.1.call-update) | async-done | bytes 10616848 | tf_op jit(solution)/shard_map/all_gather | solution.py:113
  508.6 8.8 %fusion.54 = f32[2304,72]{0,1:T(8,128)S(1)} fusion(f32[1152,2304]{0,1:T(8,128)} %all-gather.8.cloned.1.call-done, f32[1152,144]{0,1:T(8,128)} %fusion.36), kind=kOutput, calls=%fused_computation.68 | convolution fusion | flops 1146617856 | bytes 11612160 | tf_op jit(solution)/shard_map/dot_general | solution.py:28
  517.5 4.5 fusion.52
  522.6 3.0 fusion.41
  525.6 3.0 fusion.39
  (86 shorter events, 24.5 us)
Async XLA Ops:
  7.2 196.3 %copy-start.5 = (f32[1152,144]{0,1:T(8,128)S(1)}, f32[1152,144]{0,1:T(8,128)}, u32[]{:S(2)}) copy-start(f32[1152,144]{0,1:T(8,128)} %param.8) | copy-start | bytes 1990660
  7.2 191.5 %all-gather.4.cloned.1.call-start = ((), (), s32[]{:S(2)}) async-start(), calls=%async_computation | async-start | bytes 16920576 | tf_op jit(solution)/shard_map/all_gather | solution.py:131
  8.3 1.8 collective-permute-start
  12.3 336.6 %all-gather.6.cloned.1.call-start = ((), (), s32[]{:S(2)}) async-start(), calls=%async_computation.1 | async-start | bytes 11280384 | tf_op jit(solution)/shard_map/all_gather | solution.py:153
  201.3 2.2 collective-permute-start.1
  207.1 2.2 collective-permute-start.2
  216.9 291.7 %all-gather.8.cloned.1.call-start = ((), (), s32[]{:S(2)}) async-start(), calls=%async_computation.2 | async-start | bytes 11280384 | tf_op jit(solution)/shard_map/all_gather | solution.py:113
  217.2 1.7 collective-permute-start.3
  218.9 13.5 %slice-start.3 = ((s8[15925248]{0:T(1024)(128)(4,1)}), s8[4194304]{0:T(1024)(128)(4,1)S(1)}, s32[]{:S(2)}) async-start(s8[15925248]{0:T(1024)(128)(4,1)} %bitcast.67), calls=%async_computation.6 | async-start | bytes 8388608
  219.0 13.5 %slice-start.4 = ((s8[15925248]{0:T(1024)(128)(4,1)}), s8[4194304]{0:T(1024)(128)(4,1)S(1)}, s32[]{:S(2)}) async-start(s8[15925248]{0:T(1024)(128)(4,1)} %bitcast.67), calls=%async_computation.7 | async-start | bytes 8388608
  222.7 9.8 %slice-start.5 = ((s8[15925248]{0:T(1024)(128)(4,1)}), s8[4194304]{0:T(1024)(128)(4,1)S(1)}, s32[]{:S(2)}) async-start(s8[15925248]{0:T(1024)(128)(4,1)} %bitcast.67), calls=%async_computation.8 | async-start | bytes 8388608
  236.6 20.2 %collective-permute-start.4 = (f32[1152,144]{0,1:T(8,128)S(1)}, f32[1152,144]{0,1:T(8,128)S(1)}, u32[]{:S(2)}, u32[]{:S(2)}) collective-permute-start(f32[1152,144]{0,1:T(8,128)S(1)} %constant_dynamic-slice_fusion), channel_id=1, source_target_pairs={{0,16},{16,0},{1,17},{17,1},{2,18},{18,2},{3,19},{19,3},{4,20},{20... | collective-permute-start | bytes 1990664 | tf_op jit(solution)/shard_map/ppermute | solution.py:58
  238.2 3.7 collective-permute-start.5
  242.5 4.6 collective-permute-start.6
  247.8 3.7 collective-permute-start.7
  251.5 3.7 collective-permute-start.8
  255.2 1.2 collective-permute-start.9
  348.9 9.4 %copy-start = (f32[1152,2304]{0,1:T(8,128)S(1)}, f32[1152,2304]{0,1:T(8,128)}, u32[]{:S(2)}) copy-start(f32[1152,2304]{0,1:T(8,128)} %all-gather.6.cloned.1.call-done) | copy-start | bytes 31850500
  358.3 6.0 %collective-permute-start.10 = (f32[2304,72]{0,1:T(8,128)}, f32[2304,72]{0,1:T(8,128)}, u32[]{:S(2)}, u32[]{:S(2)}) collective-permute-start(f32[2304,72]{0,1:T(8,128)} %fusion.58), channel_id=1, source_target_pairs={{0,16},{16,0},{1,17},{17,1},{2,18},{18,2},{3,19},{19,3},{4,20},{20... | collective-permute-start | bytes 1990664 | tf_op jit(solution)/shard_map/ppermute | solution.py:58
  363.0 8.6 %collective-permute-start.11 = (f32[2304,72]{0,1:T(8,128)S(1)}, f32[2304,72]{0,1:T(8,128)}, u32[]{:S(2)}, u32[]{:S(2)}) collective-permute-start(f32[2304,72]{0,1:T(8,128)S(1)} %fusion.56), channel_id=1, source_target_pairs={{0,16},{16,0},{1,17},{17,1},{2,18},{18,2},{3,19},{19,3},{4,20},{20... | collective-permute-start | bytes 1990664 | tf_op jit(solution)/shard_map/ppermute | solution.py:58
  376.8 140.7 %copy-start.3 = (f32[1152,144]{0,1:T(8,128)S(1)}, f32[1152,144]{0,1:T(8,128)}, u32[]{:S(2)}) copy-start(f32[1152,144]{0,1:T(8,128)} %fusion.36) | copy-start | bytes 1990660
  508.6 8.9 %copy-start.1 = (f32[1152,2304]{0,1:T(8,128)S(1)}, f32[1152,2304]{0,1:T(8,128)}, u32[]{:S(2)}) copy-start(f32[1152,2304]{0,1:T(8,128)} %all-gather.8.cloned.1.call-done) | copy-start | bytes 31850500
  517.4 5.1 collective-permute-start.12
  522.0 3.6 collective-permute-start.13
  (10 other events, 64.0 us)
Sparse Core Ops, SparseCore 0:
  12.4 186.2 all-gather.3
  217.1 131.7 all-gather.5
  376.9 131.6 all-gather.7

commit v15 on v12

--- a/solution.py
+++ b/solution.py
@@ -136,8 +136,7 @@
         stat_hi, stat_lo = split_bf16(shard_concat(stat_next, c))
         quads = bf16_dot(stacked[1:], jnp.concatenate([stat_hi, stat_lo], axis=1), ((2,), (0,)))
         power = quads[0, :, :cols] + quads[0, :, cols:] + quads[1, :, :cols]
-        power, stacked_later = lax.optimization_barrier((power, stacked))
-        hi_later, lo_later = stacked_later[1], stacked_later[2]
+        hi_later, lo_later = hi_rows, lo_rows
         rotated = bf16_dot(hi_later, grad_cols, by_rows) + bf16_dot(lo_later, grad_cols, by_rows)
         moment_next = beta_one * moment + (1.0 - beta_one) * rotated
         second_next = beta_two * second + (1.0 - beta_two) * rotated * rotated

time: 524 us -> 524 us (level)
  no operation moved by 1% of the time
where the time goes in v15:
time: 524 us
  waiting for transfers between devices  433 us (83%)
  matrix products  57.3 us (11%)
  between operations  14.8 us (3%)
  other arithmetic  7.44 us (1%)
  starting transfers between devices  6.01 us (1%)
    all_gather x1, waiting for transfers between devices, shards(): lax.all_gather(jnp.stack([grad, basis_hi, basis_lo]), TS, axis=2, tiled=T...  186 us
    all_gather x1, waiting for transfers between devices, newton_step(): iterate_rows = lax.all_gather(iterate, TS, axis=1, tiled=True)  132 us
    all_gather x1, waiting for transfers between devices, shards(): power_rows = lax.all_gather(power, TS, axis=1, tiled=True)  92.4 us
    dot_general x6, matrix products, bf16_dot(): lax.dot_general(left, right, (dims, ((), ())), preferred_element_type=jnp...  24.1 us
    dot_general x2, matrix products, contract_rows(): lax.dot_general(left, right, (((0,), (0,)), ((), ())), precision=lax.Prec...  17.1 us
    dot_general x2, matrix products, exact_dot(): jnp.dot(left, right, precision=lax.Precision.HIGH, preferred_element_type...  12.6 us
    ppermute x4, waiting for transfers between devices, all_sum(): x = x + lax.ppermute(x, TS, [(i, i ^ step) for i in range(n_ts)])  11.3 us
    ppermute x8, waiting for transfers between devices, partner(): return lax.ppermute(x, 'shard', [(0, 1), (1, 0)])  11.3 us
  transfers between devices with their start and end apart: 15, of which 14 were waited for; matrix products, arithmetic and copies ran while one was open for 4% of the time, Pallas kernels for 0%

profile of v15, /device:TPU:0, one launch (start us, length us, event | category | flops | bytes accessed | tf_op | source)
XLA Modules:
  0.0 523.6 jit_solution(17663908707530239238)
XLA Ops:
  12.3 186.3 %all-gather.5.cloned.1.call-done = bf16[3,1152,2304]{1,2,0:T(8,128)(2,1)} async-done(((bf16[3,1152,144]{1,2,0:T(8,128)(2,1)}), bf16[3,1152,2304]{1,2,0:T(8,128)(2,1)}) %all-gather.5.cloned.1.call-update) | async-done | bytes 15925264 | tf_op jit(solution)/shard_map/all_gather | solution.py:124
  198.6 2.0 constant_dynamic-slice_fusion.1
  201.3 2.1 collective-permute-done.1
  203.4 3.6 fusion.12
  207.3 2.0 collective-permute-done.2
  209.5 6.4 %fusion = f32[2,1152,288]{1,2,0:T(8,128)S(1)} fusion(bf16[3,1152,2304]{1,2,0:T(8,128)(2,1)} %all-gather.5.cloned.1.call-done, bf16[2304,144]{0,1:T(8,128)(2,1)S(1)} %get-tuple-element.14, bf16[2304,144]{0,1:T(8,128)(2,1)S(1)} %get-tuple-element.13), kind=kOutput, calls=%fused_computation | convolution fusion | flops 3060301824 | bytes 14598144 | tf_op jit(solution)/shard_map/dot_general | solution.py:43
  215.9 1.5 fusion.25
  219.5 3.7 fusion.4
  223.2 5.0 multiply_add_fusion
  228.3 5.0 fusion.5
  233.3 2.0 fusion.8
  235.3 2.0 fusion.9
  238.3 3.6 collective-permute-done.5
  244.0 3.2 collective-permute-done.6
  249.3 2.2 collective-permute-done.7
  253.0 2.2 collective-permute-done.8
  256.9 92.4 %all-gather.9.cloned.1.call-done = f32[1,1152,2304]{1,2,0:T(8,128)} async-done(((f32[1,1152,144]{1,2,0:T(8,128)}), f32[1,1152,2304]{1,2,0:T(8,128)}) %all-gather.9.cloned.1.call-update) | async-done | bytes 10616848 | tf_op jit(solution)/shard_map/all_gather | solution.py:145
  349.4 8.4 %fusion.23 = f32[2304,144]{0,1:T(8,128)S(1)} fusion(f32[1152,2304]{0,1:T(8,128)} %bitcast.66, f32[1,1152,144]{1,2,0:T(8,128)S(1)} %copy-done.2), kind=kOutput, calls=%fused_computation.44 | convolution fusion | flops 2293235712 | bytes 12607488 | tf_op jit(solution)/shard_map/dot_general | solution.py:28
  358.5 2.4 collective-permute-done.10
  360.9 8.3 %fusion.13 = f32[1152,144]{0,1:T(8,128)} fusion(f32[1152,2304]{0,1:T(8,128)} %bitcast.67, f32[2304,144]{0,1:T(8,128)S(1)} %fusion.23, f32[2304,144]{0,1:T(8,128)S(1)} %collective-permute-done.10, f32[1,1152,144]{1,2,0:T(8,128)S(1)} %copy-done.2, f32[]{:T(128)S(6)} %mul.108, f32[]{:T(128)S(6)} %mul.103), kind=kOutput, calls=%fused_computation.18 | convolution fusion | flops 2294065152 | bytes 14598152 | tf_op jit(solution)/shard_map/dot_general | solution.py:24
  369.2 131.8 %all-gather.7.cloned.1.call-done = f32[1152,2304]{0,1:T(8,128)} async-done(((f32[1152,144]{0,1:T(8,128)}), f32[1152,2304]{0,1:T(8,128)}) %all-gather.7.cloned.1.call-update) | async-done | bytes 10616848 | tf_op jit(solution)/shard_map/all_gather | solution.py:105
  501.0 8.6 %fusion.39 = f32[2304,144]{0,1:T(8,128)S(1)} fusion(f32[1152,2304]{0,1:T(8,128)} %all-gather.7.cloned.1.call-done, f32[1152,144]{0,1:T(8,128)} %fusion.13), kind=kOutput, calls=%fused_computation.69 | convolution fusion | flops 2293235712 | bytes 12607488 | tf_op jit(solution)/shard_map/dot_general | solution.py:28
  509.7 3.0 collective-permute-done.11
  512.8 4.3 multiply_subtract_fusion
  (66 shorter events, 16.6 us)
Async XLA Ops:
  7.2 191.5 %all-gather.5.cloned.1.call-start = ((), (), s32[]{:S(2)}) async-start(), calls=%async_computation | async-start | bytes 16920576 | tf_op jit(solution)/shard_map/all_gather | solution.py:124
  8.2 1.8 collective-permute-start
  12.2 191.2 %copy-start.4 = (f32[1152,144]{0,1:T(8,128)S(1)}, f32[1152,144]{0,1:T(8,128)}, u32[]{:S(2)}) copy-start(f32[1152,144]{0,1:T(8,128)} %param.8) | copy-start | bytes 1990660
  12.2 337.2 %all-gather.9.cloned.1.call-start = ((), (), s32[]{:S(2)}) async-start(), calls=%async_computation.2 | async-start | bytes 11280384 | tf_op jit(solution)/shard_map/all_gather | solution.py:145
  201.2 2.2 collective-permute-start.1
  207.1 2.2 collective-permute-start.2
  217.4 283.5 %all-gather.7.cloned.1.call-start = ((), (), s32[]{:S(2)}) async-start(), calls=%async_computation.1 | async-start | bytes 11280384 | tf_op jit(solution)/shard_map/all_gather | solution.py:105
  217.7 1.7 collective-permute-start.3
  219.4 13.8 %slice-start = ((s8[15925248]{0:T(1024)(128)(4,1)}), s8[4194304]{0:T(1024)(128)(4,1)S(1)}, s32[]{:S(2)}) async-start(s8[15925248]{0:T(1024)(128)(4,1)} %bitcast.69), calls=%async_computation.3 | async-start | bytes 8388608
  219.5 13.8 %slice-start.1 = ((s8[15925248]{0:T(1024)(128)(4,1)}), s8[4194304]{0:T(1024)(128)(4,1)S(1)}, s32[]{:S(2)}) async-start(s8[15925248]{0:T(1024)(128)(4,1)} %bitcast.69), calls=%async_computation.4 | async-start | bytes 8388608
  223.2 10.1 %slice-start.2 = ((s8[15925248]{0:T(1024)(128)(4,1)}), s8[4194304]{0:T(1024)(128)(4,1)S(1)}, s32[]{:S(2)}) async-start(s8[15925248]{0:T(1024)(128)(4,1)} %bitcast.69), calls=%async_computation.5 | async-start | bytes 8388608
  228.2 7.1 %copy-start.7 = (f32[1152,144]{0,1:T(8,128)}, f32[1152,144]{0,1:T(8,128)S(1)}, u32[]{:S(2)}) copy-start(f32[1152,144]{0,1:T(8,128)S(1)} %get-tuple-element.19) | copy-start | bytes 1990660
  228.2 7.1 %copy-start.8 = (f32[1152,144]{0,1:T(8,128)}, f32[1152,144]{0,1:T(8,128)S(1)}, u32[]{:S(2)}) copy-start(f32[1152,144]{0,1:T(8,128)S(1)} %get-tuple-element.20) | copy-start | bytes 1990660
  237.3 112.0 %copy-start.2 = (f32[1,1152,144]{1,2,0:T(8,128)S(1)}, f32[1,1152,144]{1,2,0:T(8,128)}, u32[]{:S(2)}) copy-start(f32[1,1152,144]{1,2,0:T(8,128)} %get-tuple-element.12) | copy-start | bytes 1990660
  237.4 17.8 %collective-permute-start.4 = (f32[1152,144]{0,1:T(8,128)S(1)}, f32[1152,144]{0,1:T(8,128)S(1)}, u32[]{:S(2)}, u32[]{:S(2)}) collective-permute-start(f32[1152,144]{0,1:T(8,128)S(1)} %constant_dynamic-slice_fusion), channel_id=1, source_target_pairs={{0,16},{16,0},{1,17},{17,1},{2,18},{18,2},{3,19},{19,3},{4,20},{20... | collective-permute-start | bytes 1990664 | tf_op jit(solution)/shard_map/ppermute | solution.py:58
  238.3 3.7 collective-permute-start.5
  242.6 4.6 collective-permute-start.6
  247.9 3.7 collective-permute-start.7
  251.6 3.7 collective-permute-start.8
  255.2 1.2 collective-permute-start.9
  357.8 3.1 collective-permute-start.10
  369.2 143.6 %copy-start.1 = (f32[1152,144]{0,1:T(8,128)S(1)}, f32[1152,144]{0,1:T(8,128)}, u32[]{:S(2)}) copy-start(f32[1152,144]{0,1:T(8,128)} %fusion.13) | copy-start | bytes 1990660
  501.0 11.8 %copy-start = (f32[1152,2304]{0,1:T(8,128)S(1)}, f32[1152,2304]{0,1:T(8,128)}, u32[]{:S(2)}) copy-start(f32[1152,2304]{0,1:T(8,128)} %all-gather.7.cloned.1.call-done) | copy-start | bytes 31850500
  509.6 3.1 collective-permute-start.11
  (4 other events, 15.1 us)
Sparse Core Ops, SparseCore 0:
  12.3 186.2 all-gather.4
  217.6 131.7 all-gather.8
  369.3 131.6 all-gather.6
